TPU v7x, 256 devices: a whole 4x4x8 slice. The times are simulated.
256 devices in a mesh: cache: 8 (over y, core), dev: 32 (over x, z).
Axes of the slice: x: 4, y: 4, z: 8, core: 2. Of those that a mesh axis runs over, the one named last changes fastest.
Arguments:
- queries: bfloat16 [8, 1024, 8192], P('cache', None, 'dev'), may hold values from -8 to 8
- store_kv: bfloat16 [256, 512, 2048], P('cache', 'dev'), may hold values from -4 to 4
- self_kv: bfloat16 [8, 1024, 2048], P('cache'), may hold values from -5 to 5
- rec_states: bfloat16 [8, 512, 8192], P('cache', None, 'dev'), may hold values from -400 to 400
- norm_gain: bfloat16 [8192], P('dev'), may hold values from 0.099609375 to 1.8984375
- w_kv: bfloat16 [8192, 2048], P('dev'), may hold values from -0.0625 to 0.0625
- retrieval: int32 [8, 16], replicated, may hold values from 0 to 255, as said below
- doc_home: int32 [256], replicated, may hold values from 0 to 255, as said below
- rec_index: int32 [8, 16, 32], P('cache'), may hold values from 0 to 511, as said below
Outputs:
- attended: bfloat16 [8, 1024, 8192], P('cache', None, 'dev')
Inputs may be any that keep to these rules, and one draw needn't show every extreme that they name: `retrieval`: each request names 16 distinct documents; their store rows lie in exactly 4 of the groups of 32 consecutive rows, 4 in each. `doc_home`: every store row holds exactly one document. `rec_index`: the 32 positions of one block are distinct.
All inputs are finite; a program needn't handle non-finite values.
Results may differ from a plain program's by a relative error of at most 0.0045.
Values may be sent and summed in bfloat16 or wider, within the bound.
No kernel may reach another device: no remote copies, remote signals or barrier semaphores. Data moves between devices by JAX's collectives and lax.ppermute only.
A program may use at most 128 MiB of HBM per device.

v0:
```python
import math

import jax
import jax.numpy as jnp
from jax import lax
from jax.sharding import PartitionSpec as P

D = 8192
QH = 64
KVH = 8
HD = 128
RET = 16
CAP = 4
REC = 32
DOC_GRP = 32


eps_norm = 1e-05
tile_rows = 512


def own_head(wide_rows, head_count, head_size, chosen):
    shaped = wide_rows.reshape(wide_rows.shape[:-1] + (2, head_count, head_size))
    taken = lax.dynamic_index_in_dim(shaped, chosen, shaped.ndim - 2, keepdims=False)
    return taken.reshape(wide_rows.shape[:-1] + (2 * head_size,))


def pick_heads(wide_rows, head_count, head_size, chosen):
    shaped = wide_rows.reshape(wide_rows.shape[:-1] + (2, head_count, head_size))
    taken = jnp.take(shaped, chosen, axis=shaped.ndim - 2)
    moved = jnp.moveaxis(taken, shaped.ndim - 2, 0)
    return moved.reshape(moved.shape[:-2] + (2 * head_size,))


def shards(queries, store_kv, self_kv, rec_states, norm_gain, w_kv, retrieval, doc_home, rec_index):
    groups = lax.axis_size("cache")
    members = lax.axis_size("dev")
    my_group = lax.axis_index("cache")
    my_member = lax.axis_index("dev")
    per_device = QH // members
    ratio_heads = QH // KVH
    my_head = my_member * per_device // ratio_heads
    shard_rows = store_kv.shape[1]
    kv_width = store_kv.shape[2]
    inv_root = 1.0 / math.sqrt(HD)
    stored_at = jnp.take(doc_home, retrieval, axis=0)
    source = stored_at // DOC_GRP
    local_row = stored_at % DOC_GRP
    before = jnp.arange(RET)[None, :] < jnp.arange(RET)[:, None]
    same_home = source[:, :, None] == source[:, None, :]
    rank_within = jnp.sum((same_home & before[None, :, :]).astype(jnp.int32), axis=2)
    places = jnp.arange(CAP, dtype=jnp.int32)
    matching = (source[:, None, :] == my_group) & (rank_within[:, None, :] == places[None, :, None])
    pick_row = jnp.sum(jnp.where(matching, local_row[:, None, :], 0), axis=2)
    filled = jnp.any(matching, axis=2)
    outgoing = jnp.take(store_kv, pick_row.reshape(-1), axis=0).reshape(
        groups, CAP, shard_rows, kv_width
    )
    outgoing = jnp.where(filled[:, :, None, None], outgoing, jnp.zeros((), store_kv.dtype))
    my_source = lax.dynamic_index_in_dim(source, my_group, 0, keepdims=False)
    my_rank = lax.dynamic_index_in_dim(rank_within, my_group, 0, keepdims=False)
    slot_place = my_source * CAP + my_rank
    dest_heads = jnp.arange(members, dtype=jnp.int32) * per_device // ratio_heads
    arrived = lax.all_to_all(outgoing, "cache", split_axis=0, concat_axis=0, tiled=True)
    compact = jnp.take(arrived.reshape(groups * CAP, shard_rows, kv_width), slot_place, axis=0)
    spread = pick_heads(compact, KVH, HD, dest_heads)
    fetched = lax.all_to_all(spread, "dev", split_axis=0, concat_axis=2, tiled=True)[0]
    states = rec_states[0].astype(jnp.float32)
    partial_sq = jnp.sum(states * states, axis=1)
    total_sq = lax.psum(partial_sq, "dev")
    inv_rms = lax.rsqrt(total_sq / D + eps_norm)
    normed = (states * norm_gain.astype(jnp.float32)[None, :] * inv_rms[:, None]).astype(
        jnp.bfloat16
    )
    summed = lax.psum(jnp.dot(normed, w_kv, preferred_element_type=jnp.float32), "dev")
    redone = summed.astype(jnp.bfloat16)
    own_rows = own_head(redone.reshape(RET, REC, kv_width), KVH, HD, my_head)
    full_block = fetched.shape[1]
    positions = rec_index[0]
    onehot = positions[:, :, None] == jnp.arange(full_block, dtype=jnp.int32)[None, None, :]
    placed = jnp.einsum(
        "kib,kic->kbc", onehot.astype(jnp.bfloat16), own_rows, preferred_element_type=jnp.float32
    ).astype(jnp.bfloat16)
    replaced_at = jnp.any(onehot, axis=1)
    blocks = jnp.where(replaced_at[:, :, None], placed, fetched)
    doc_keys = blocks[:, :, :HD].reshape(-1, HD)
    doc_values = blocks[:, :, HD:].reshape(-1, HD)
    own_self = own_head(self_kv[0], KVH, HD, my_head)
    self_keys = own_self[:, :HD]
    self_values = own_self[:, HD:]
    prompt = queries.shape[1]
    head_rows = jnp.transpose(queries[0].reshape(prompt, per_device, HD), (1, 0, 2))
    block_len = min(tile_rows, prompt)
    block_count = prompt // block_len
    key_spots = jnp.arange(prompt, dtype=jnp.int32)

    def attend(pair_index):
        head_at = pair_index // block_count
        first_row = pair_index % block_count * block_len
        query_block = lax.dynamic_slice_in_dim(
            lax.dynamic_index_in_dim(head_rows, head_at, 0, keepdims=False), first_row, block_len, 0
        )
        doc_scores = (
            jnp.einsum("qd,kd->qk", query_block, doc_keys, preferred_element_type=jnp.float32)
            * inv_root
        )
        self_scores = (
            jnp.einsum("qd,kd->qk", query_block, self_keys, preferred_element_type=jnp.float32)
            * inv_root
        )
        allowed = (
            key_spots[None, :] <= (first_row + jnp.arange(block_len, dtype=jnp.int32))[:, None]
        )
        self_scores = jnp.where(allowed, self_scores, -jnp.inf)
        top = jnp.maximum(jnp.max(doc_scores, axis=1), jnp.max(self_scores, axis=1))
        doc_expd = jnp.exp(doc_scores - top[:, None])
        self_expd = jnp.exp(self_scores - top[:, None])
        total = jnp.sum(doc_expd, axis=1) + jnp.sum(self_expd, axis=1)
        weighted = jnp.dot(
            doc_expd.astype(jnp.bfloat16), doc_values, preferred_element_type=jnp.float32
        )
        weighted = weighted + jnp.dot(
            self_expd.astype(jnp.bfloat16), self_values, preferred_element_type=jnp.float32
        )
        return (weighted / total[:, None]).astype(jnp.bfloat16)

    gathered_out = lax.map(attend, jnp.arange(per_device * block_count, dtype=jnp.int32))
    result = jnp.transpose(gathered_out.reshape(per_device, prompt, HD), (1, 0, 2))
    return result.reshape(1, prompt, per_device * HD)


def solution(mesh):
    placed = (
        P("cache", None, "dev"),
        P("cache", "dev", None),
        P("cache", None, None),
        P("cache", None, "dev"),
        P("dev"),
        P("dev", None),
        P(),
        P(),
        P("cache", None, None),
    )
    return jax.shard_map(
        shards, mesh=mesh, in_specs=placed, out_specs=P("cache", None, "dev"), check_vma=False
    )
```

profile of v0, /device:TPU:16, one launch (start us, length us, event | category | flops | bytes accessed | tf_op | source)
XLA Modules:
  0.0 543.7 jit_solution(9324490959831772054)
XLA Ops:
  1.0 1.3 gather_fusion
  3.4 2.0 gather_fusion.1
  5.4 3.2 select_select_fusion
  8.6 5.6 %all-to-all-start = ((bf16[8,4,16,2048]{3,2,1,0:T(8,128)(2,1)}), bf16[8,4,16,2048]{3,2,1,0:T(8,128)(2,1)S(1)}, u32[]{:S(2)}, u32[]{:S(2)}) async-start(bf16[8,4,16,2048]{3,2,1,0:T(8,128)(2,1)} %select_select_fusion), calls=%async_computation | async-start | bytes 4194304 | tf_op jit(solution)/shard_map/all_to_all | solution.py:64
  14.3 23.9 %all-to-all-done = bf16[8,4,16,2048]{3,2,1,0:T(8,128)(2,1)S(1)} async-done(((bf16[8,4,16,2048]{3,2,1,0:T(8,128)(2,1)}), bf16[8,4,16,2048]{3,2,1,0:T(8,128)(2,1)S(1)}, u32[]{:S(2)}, u32[]{:S(2)}) %all-to-all-start) | async-done | bytes 2097184 | tf_op jit(solution)/shard_map/all_to_all | solution.py:64
  39.3 3.4 gather_fusion.3
  42.7 5.6 %copy_bitcast_fusion = bf16[32,16,16,256]{3,2,1,0:T(8,128)(2,1)} fusion(bf16[32,16,16,2,128]{4,2,3,1,0:T(8,128)(2,1)} %gather_fusion.3, pred[32]{0:T(512)(128)(4,1)S(1)} %compare_and_fusion.2), kind=kLoop, calls=%fused_computation.30 | loop fusion | flops 2097152 | bytes 8388640 | tf_op jit(solution)/shard_map/reshape | solution.py:32
  48.3 10.8 %all-to-all-start.1 = ((bf16[32,16,16,256]{3,2,1,0:T(8,128)(2,1)}), bf16[32,16,16,256]{3,2,1,0:T(8,128)(2,1)}, u32[]{:S(2)}, u32[]{:S(2)}) async-start(bf16[32,16,16,256]{3,2,1,0:T(8,128)(2,1)} %copy_bitcast_fusion), calls=%async_computation.1 | async-start | bytes 8388608 | tf_op jit(solution)/shard_map/all_to_all | solution.py:67
  59.3 155.9 %psum.14 = f32[512]{0:T(512)S(1)} all-reduce(f32[512]{0:T(512)S(1)} %fusion.25), channel_id=1, replica_groups=mesh['cache'=8,'dev'=32] {'dev'}, use_global_device_ids=true, to_apply=%region_2.3 | all-reduce | flops 512 | bytes 4096 | tf_op jit(solution)/shard_map/psum | solution.py:70
  215.3 2.7 fusion.27
  218.0 172.1 %all-reduce.1 = bf16[512,2048]{1,0:T(8,128)(2,1)S(1)} all-reduce(f32[512,2048]{1,0:T(8,128)} %fusion.27), channel_id=1, replica_groups=mesh['cache'=8,'dev'=32] {'dev'}, use_global_device_ids=true, to_apply=%region_3.4 | all-reduce | flops 1048576 | bytes 6291456 | tf_op jit(solution)/shard_map/psum | solution.py:75
  390.1 2.0 copy.40
  392.1 3.5 dynamic-slice_reduce_fusion.1
  395.7 3.6 copy.42
  399.4 3.7 dynamic-slice_reduce_fusion
  404.5 2.6 copy.32
  407.1 3.0 convert_select_fusion
  410.1 2.5 fusion.43
  412.6 128.2 %while.14 = (s32[]{:T(128)}, bf16[4,512,128]{2,1,0:T(8,128)(2,1)}, s32[4]{0:T(128)S(1)}, bf16[2,1024,128]{1,2,0:T(8,128)(2,1)S(1)}, bf16[8192,128]{1,0:T(8,128)(...) while((s32[]{:T(128)}, bf16[4,512,128]{2,1,0:T(8,128)(2,1)}, ...), condition=%wide.region_12.13_spmd.clone, body=%wide.region_7.12_spmd.clone.sunk | while | flops 2453863936 | bytes 63343596 | solution.py:127
  416.1 9.9 %multiply_reduce_fusion.2 = (f32[512]{0:T(512)S(1)}, f32[512,8192]{1,0:T(8,128)}) fusion(bf16[8192,128]{1,0:T(8,128)(2,1)} %get-tuple-element.316, bf16[2,1024,128]{1,2,0:T(8,128)(2,1)S(1)} %get-tuple-element.315, s32[]{:T(128)S(6)} %select_n.272, s32[]{:T(128)S(6)} %select_n.275), kind=kOutput, calls=%fused_computation.6.clone.1 | convolution fusion | flops 1082129920 | bytes 19007496 | tf_op jit(solution)/shard_map/while/body/eval_jaxpr/qd,kd->qk/dot_general | solution.py:104
  427.3 8.6 %fusion.70 = f32[512]{0:T(512)S(1)} fusion(f32[512,8192]{1,0:T(8,128)} %get-tuple-element.280, f32[512]{0:T(512)S(1)} %max.13), kind=kLoop, calls=%fused_computation.7.clone.1 | loop fusion | flops 12582400 | bytes 16781312 | tf_op jit(solution)/shard_map/while/body/eval_jaxpr/reduce_sum | solution.py:118
  435.9 7.6 %fusion.69 = f32[512,128]{1,0:T(8,128)S(1)} fusion(bf16[8192,128]{1,0:T(8,128)(2,1)S(1)} %get-tuple-element.318, f32[512,8192]{1,0:T(8,128)} %get-tuple-element.280, f32[512]{0:T(512)S(1)} %max.13), kind=kOutput, calls=%fused_computation.9.clone.1 | convolution fusion | flops 1086324736 | bytes 19138560 | tf_op jit(solution)/shard_map/while/body/eval_jaxpr/dot_general | solution.py:119
  448.1 9.9 %multiply_reduce_fusion.2 = (f32[512]{0:T(512)S(1)}, f32[512,8192]{1,0:T(8,128)}) fusion(bf16[8192,128]{1,0:T(8,128)(2,1)} %get-tuple-element.316, bf16[2,1024,128]{1,2,0:T(8,128)(2,1)S(1)} %get-tuple-element.315, s32[]{:T(128)S(6)} %select_n.272, s32[]{:T(128)S(6)} %select_n.275), kind=kOutput, calls=%fused_computation.6.clone.1 | convolution fusion | flops 1082129920 | bytes 19007496 | tf_op jit(solution)/shard_map/while/body/eval_jaxpr/qd,kd->qk/dot_general | solution.py:104
  459.3 8.6 %fusion.70 = f32[512]{0:T(512)S(1)} fusion(f32[512,8192]{1,0:T(8,128)} %get-tuple-element.280, f32[512]{0:T(512)S(1)} %max.13), kind=kLoop, calls=%fused_computation.7.clone.1 | loop fusion | flops 12582400 | bytes 16781312 | tf_op jit(solution)/shard_map/while/body/eval_jaxpr/reduce_sum | solution.py:118
  467.9 7.6 %fusion.69 = f32[512,128]{1,0:T(8,128)S(1)} fusion(bf16[8192,128]{1,0:T(8,128)(2,1)S(1)} %get-tuple-element.318, f32[512,8192]{1,0:T(8,128)} %get-tuple-element.280, f32[512]{0:T(512)S(1)} %max.13), kind=kOutput, calls=%fused_computation.9.clone.1 | convolution fusion | flops 1086324736 | bytes 19138560 | tf_op jit(solution)/shard_map/while/body/eval_jaxpr/dot_general | solution.py:119
  480.2 9.8 %multiply_reduce_fusion.2 = (f32[512]{0:T(512)S(1)}, f32[512,8192]{1,0:T(8,128)}) fusion(bf16[8192,128]{1,0:T(8,128)(2,1)} %get-tuple-element.316, bf16[2,1024,128]{1,2,0:T(8,128)(2,1)S(1)} %get-tuple-element.315, s32[]{:T(128)S(6)} %select_n.272, s32[]{:T(128)S(6)} %select_n.275), kind=kOutput, calls=%fused_computation.6.clone.1 | convolution fusion | flops 1082129920 | bytes 19007496 | tf_op jit(solution)/shard_map/while/body/eval_jaxpr/qd,kd->qk/dot_general | solution.py:104
  491.4 8.6 %fusion.70 = f32[512]{0:T(512)S(1)} fusion(f32[512,8192]{1,0:T(8,128)} %get-tuple-element.280, f32[512]{0:T(512)S(1)} %max.13), kind=kLoop, calls=%fused_computation.7.clone.1 | loop fusion | flops 12582400 | bytes 16781312 | tf_op jit(solution)/shard_map/while/body/eval_jaxpr/reduce_sum | solution.py:118
  500.0 7.6 %fusion.69 = f32[512,128]{1,0:T(8,128)S(1)} fusion(bf16[8192,128]{1,0:T(8,128)(2,1)S(1)} %get-tuple-element.318, f32[512,8192]{1,0:T(8,128)} %get-tuple-element.280, f32[512]{0:T(512)S(1)} %max.13), kind=kOutput, calls=%fused_computation.9.clone.1 | convolution fusion | flops 1086324736 | bytes 19138560 | tf_op jit(solution)/shard_map/while/body/eval_jaxpr/dot_general | solution.py:119
  512.2 9.8 %multiply_reduce_fusion.2 = (f32[512]{0:T(512)S(1)}, f32[512,8192]{1,0:T(8,128)}) fusion(bf16[8192,128]{1,0:T(8,128)(2,1)} %get-tuple-element.316, bf16[2,1024,128]{1,2,0:T(8,128)(2,1)S(1)} %get-tuple-element.315, s32[]{:T(128)S(6)} %select_n.272, s32[]{:T(128)S(6)} %select_n.275), kind=kOutput, calls=%fused_computation.6.clone.1 | convolution fusion | flops 1082129920 | bytes 19007496 | tf_op jit(solution)/shard_map/while/body/eval_jaxpr/qd,kd->qk/dot_general | solution.py:104
  523.4 8.6 %fusion.70 = f32[512]{0:T(512)S(1)} fusion(f32[512,8192]{1,0:T(8,128)} %get-tuple-element.280, f32[512]{0:T(512)S(1)} %max.13), kind=kLoop, calls=%fused_computation.7.clone.1 | loop fusion | flops 12582400 | bytes 16781312 | tf_op jit(solution)/shard_map/while/body/eval_jaxpr/reduce_sum | solution.py:118
  532.1 7.6 %fusion.69 = f32[512,128]{1,0:T(8,128)S(1)} fusion(bf16[8192,128]{1,0:T(8,128)(2,1)S(1)} %get-tuple-element.318, f32[512,8192]{1,0:T(8,128)} %get-tuple-element.280, f32[512]{0:T(512)S(1)} %max.13), kind=kOutput, calls=%fused_computation.9.clone.1 | convolution fusion | flops 1086324736 | bytes 19138560 | tf_op jit(solution)/shard_map/while/body/eval_jaxpr/dot_general | solution.py:119
  540.8 1.7 copy.49
  (91 shorter events, 18.7 us)
Async XLA Ops:
  0.0 3.4 copy-start
  0.0 0.9 copy-start.2
  1.0 1.4 copy-start.7
  8.6 29.6 %all-to-all-start = ((bf16[8,4,16,2048]{3,2,1,0:T(8,128)(2,1)}), bf16[8,4,16,2048]{3,2,1,0:T(8,128)(2,1)S(1)}, u32[]{:S(2)}, u32[]{:S(2)}) async-start(bf16[8,4,16,2048]{3,2,1,0:T(8,128)(2,1)} %select_select_fusion), calls=%async_computation | async-start | bytes 4194304 | tf_op jit(solution)/shard_map/all_to_all | solution.py:64
  48.3 10.9 %copy-start.9 = (bf16[256]{0:T(256)(128)(2,1)S(1)}, bf16[256]{0:T(256)(128)(2,1)}, u32[]{:S(2)}) copy-start(bf16[256]{0:T(256)(128)(2,1)} %param.15) | copy-start | bytes 1540
  48.3 10.9 %copy-start.3 = (bf16[1,512,256]{2,1,0:T(8,128)(2,1)S(1)}, bf16[1,512,256]{2,1,0:T(8,128)(2,1)}, u32[]{:S(2)}) copy-start(bf16[1,512,256]{2,1,0:T(8,128)(2,1)} %param.14) | copy-start | bytes 786436
  48.3 167.0 %copy-start.4 = (bf16[256,2048]{1,0:T(8,128)(2,1)S(1)}, bf16[256,2048]{1,0:T(8,128)(2,1)}, u32[]{:S(2)}) copy-start(bf16[256,2048]{1,0:T(8,128)(2,1)} %param.16) | copy-start | bytes 3145732
  48.3 356.2 %all-to-all-start.1 = ((bf16[32,16,16,256]{3,2,1,0:T(8,128)(2,1)}), bf16[32,16,16,256]{3,2,1,0:T(8,128)(2,1)}, u32[]{:S(2)}, u32[]{:S(2)}) async-start(bf16[32,16,16,256]{3,2,1,0:T(8,128)(2,1)} %copy_bitcast_fusion), calls=%async_computation.1 | async-start | bytes 8388608 | tf_op jit(solution)/shard_map/all_to_all | solution.py:67
  399.3 3.8 copy-start.5
  399.4 4.0 copy-start.8
  416.1 9.9 %copy-start.6 = (bf16[1024,128]{1,0:T(8,128)(2,1)S(1)}, bf16[1024,128]{1,0:T(8,128)(2,1)}, u32[]{:S(2)}) copy-start(bf16[1024,128]{1,0:T(8,128)(2,1)} %get-tuple-element.317) | copy-start | bytes 786436 | tf_op jit(solution)/shard_map/while
  448.1 9.9 %copy-start.6 = (bf16[1024,128]{1,0:T(8,128)(2,1)S(1)}, bf16[1024,128]{1,0:T(8,128)(2,1)}, u32[]{:S(2)}) copy-start(bf16[1024,128]{1,0:T(8,128)(2,1)} %get-tuple-element.317) | copy-start | bytes 786436 | tf_op jit(solution)/shard_map/while
  480.2 9.9 %copy-start.6 = (bf16[1024,128]{1,0:T(8,128)(2,1)S(1)}, bf16[1024,128]{1,0:T(8,128)(2,1)}, u32[]{:S(2)}) copy-start(bf16[1024,128]{1,0:T(8,128)(2,1)} %get-tuple-element.317) | copy-start | bytes 786436 | tf_op jit(solution)/shard_map/while
  512.2 9.9 %copy-start.6 = (bf16[1024,128]{1,0:T(8,128)(2,1)S(1)}, bf16[1024,128]{1,0:T(8,128)(2,1)}, u32[]{:S(2)}) copy-start(bf16[1024,128]{1,0:T(8,128)(2,1)} %get-tuple-element.317) | copy-start | bytes 786436 | tf_op jit(solution)/shard_map/while
  540.8 2.9 copy-start.1
where the time goes:
time: 546 us; the launch traced here: 544 us
  blocking collectives  328 us (60%)
  matrix products  83.4 us (15%)
  other arithmetic  47.7 us (9%)
  local copies, waits for them, and re-layouts  32.7 us (6%)
  waiting for transfers between devices  23.9 us (4%)
  starting transfers between devices  16.4 us (3%)
  loops' own time  11.3 us (2%)
    psum x1, blocking collectives, shards(): lax.psum(jnp.dot(normed, w_kv, preferred_element_type=jnp.float32), 'dev')  172 us
    psum x1, blocking collectives, shards(): total_sq = lax.psum(partial_sq, 'dev')  156 us
    dot_general x4, matrix products, attend(): jnp.einsum('qd,kd->qk', query_block, doc_keys, preferred_element_type=jnp...  39.4 us
    reduce_sum x8, other arithmetic, attend(): total = jnp.sum(doc_expd, axis=1) + jnp.sum(self_expd, axis=1)  36.5 us
    dot_general x4, matrix products, attend(): jnp.dot(doc_expd.astype(jnp.bfloat16), doc_values, preferred_element_type...  30.3 us
    all_to_all x1, waiting for transfers between devices, shards(): lax.all_to_all(outgoing, 'cache', split_axis=0, concat_axis=0, tiled=True)  23.9 us
    another operation x1, loops' own time, shards(): lax.map(attend, jnp.arange(per_device * block_count, dtype=jnp.int32))  11.3 us
  transfers between devices with their start and end apart: 2, of which 1 were waited for; matrix products, arithmetic and copies ran while one was open for 3% of the time, Pallas kernels for 0%

commit v1 on v0

--- a/solution.py
+++ b/solution.py
@@ -3,7 +3,7 @@
 import jax
 import jax.numpy as jnp
 from jax import lax
-from jax.sharding import PartitionSpec as P
+from jax.sharding import Mesh, PartitionSpec as P
 
 D = 8192
 QH = 64
@@ -13,6 +13,7 @@
 CAP = 4
 REC = 32
 DOC_GRP = 32
+MODE = 1
 
 
 eps_norm = 1e-05
@@ -34,9 +35,9 @@
 
 def shards(queries, store_kv, self_kv, rec_states, norm_gain, w_kv, retrieval, doc_home, rec_index):
     groups = lax.axis_size("cache")
-    members = lax.axis_size("dev")
+    members = lax.axis_size("dh") * lax.axis_size("dq")
     my_group = lax.axis_index("cache")
-    my_member = lax.axis_index("dev")
+    my_member = lax.axis_index("dh") * lax.axis_size("dq") + lax.axis_index("dq")
     per_device = QH // members
     ratio_heads = QH // KVH
     my_head = my_member * per_device // ratio_heads
@@ -64,17 +65,28 @@
     arrived = lax.all_to_all(outgoing, "cache", split_axis=0, concat_axis=0, tiled=True)
     compact = jnp.take(arrived.reshape(groups * CAP, shard_rows, kv_width), slot_place, axis=0)
     spread = pick_heads(compact, KVH, HD, dest_heads)
-    fetched = lax.all_to_all(spread, "dev", split_axis=0, concat_axis=2, tiled=True)[0]
+    fetched = lax.all_to_all(spread, ("dh", "dq"), split_axis=0, concat_axis=2, tiled=True)[0]
     states = rec_states[0].astype(jnp.float32)
+    rows_rec = states.shape[0]
     partial_sq = jnp.sum(states * states, axis=1)
-    total_sq = lax.psum(partial_sq, "dev")
-    inv_rms = lax.rsqrt(total_sq / D + eps_norm)
-    normed = (states * norm_gain.astype(jnp.float32)[None, :] * inv_rms[:, None]).astype(
-        jnp.bfloat16
-    )
-    summed = lax.psum(jnp.dot(normed, w_kv, preferred_element_type=jnp.float32), "dev")
-    redone = summed.astype(jnp.bfloat16)
-    own_rows = own_head(redone.reshape(RET, REC, kv_width), KVH, HD, my_head)
+    scaled = (states * norm_gain.astype(jnp.float32)[None, :]).astype(jnp.bfloat16)
+    partial_kv = jnp.dot(scaled, w_kv, preferred_element_type=jnp.float32)
+    by_head = jnp.transpose(partial_kv.reshape(rows_rec, 2, KVH, HD), (2, 0, 1, 3)).reshape(KVH, rows_rec, 2 * HD)
+    sq_cols = jnp.broadcast_to(partial_sq[None, :, None], (KVH, rows_rec, HD))
+    packed = jnp.concatenate([by_head, sq_cols], axis=2)
+    if MODE == 0:
+        summed = lax.psum(packed, ("dh", "dq"))
+        summed = lax.dynamic_index_in_dim(summed, my_head, 0, keepdims=False)
+    elif MODE == 1:
+        head_sum = lax.psum_scatter(packed, "dh", scatter_dimension=0, tiled=True)[0]
+        summed = lax.psum(head_sum, "dq")
+    else:
+        head_sum = lax.psum_scatter(packed, "dh", scatter_dimension=0, tiled=True)[0]
+        piece = lax.psum_scatter(head_sum, "dq", scatter_dimension=0, tiled=True)
+        summed = lax.all_gather(piece, "dq", axis=0, tiled=True)
+    inv_rms = lax.rsqrt(summed[:, 2 * HD] / D + eps_norm)
+    redone = (summed[:, : 2 * HD] * inv_rms[:, None]).astype(jnp.bfloat16)
+    own_rows = redone.reshape(RET, REC, 2 * HD)
     full_block = fetched.shape[1]
     positions = rec_index[0]
     onehot = positions[:, :, None] == jnp.arange(full_block, dtype=jnp.int32)[None, None, :]
@@ -130,17 +142,21 @@
 
 
 def solution(mesh):
+    dev = ("dh", "dq")
+    groups = mesh.shape["cache"]
+    members = mesh.shape["dev"]
+    view = Mesh(mesh.devices.reshape(groups, KVH, members // KVH), ("cache", "dh", "dq"))
     placed = (
-        P("cache", None, "dev"),
-        P("cache", "dev", None),
+        P("cache", None, dev),
+        P("cache", dev, None),
         P("cache", None, None),
-        P("cache", None, "dev"),
-        P("dev"),
-        P("dev", None),
+        P("cache", None, dev),
+        P(dev),
+        P(dev, None),
         P(),
         P(),
         P("cache", None, None),
     )
     return jax.shard_map(
-        shards, mesh=mesh, in_specs=placed, out_specs=P("cache", None, "dev"), check_vma=False
+        shards, mesh=view, in_specs=placed, out_specs=P("cache", None, dev), check_vma=False
     )

time: 546 us -> 435 us (0.80)
  blocking collectives: 328 us -> 0 us
  waiting for transfers between devices: 23.9 us -> 218 us
  between operations: 0.29 us -> 13.7 us
  other arithmetic: 47.7 us -> 54 us
    psum x2 -> x0, blocking collectives: 328 us -> none  [the longest x1 172 us: shards(): lax.psum(jnp.dot(normed, w_kv, preferred_element_type=jnp.float32), 'dev')]
    reduce_scatter x0 -> x1, waiting for transfers between devices: none -> 149 us  [shards(): lax.psum_scatter(packed, 'dh', scatter_dimension=0, tiled=True)[0]]
    psum x0 -> x1, waiting for transfers between devices: none -> 44.5 us  [shards(): summed = lax.psum(head_sum, 'dq')]
  transfers between devices with their start and end apart: 2 -> 4, of which waited for: 1 -> 3; matrix products, arithmetic and copies ran while one was open for 3% -> 8% of each run, Pallas kernels for 0% -> 0%
where the time goes in v1:
time: 435 us; the launch traced here: 434 us
  waiting for transfers between devices  218 us (50%)
  matrix products  84.3 us (19%)
  other arithmetic  54 us (12%)
  local copies, waits for them, and re-layouts  36.4 us (8%)
  starting transfers between devices  16.5 us (4%)
  between operations  13.7 us (3%)
  loops' own time  11.3 us (3%)
    reduce_scatter x1, waiting for transfers between devices, shards(): lax.psum_scatter(packed, 'dh', scatter_dimension=0, tiled=True)[0]  149 us
    psum x1, waiting for transfers between devices, shards(): summed = lax.psum(head_sum, 'dq')  44.5 us
    dot_general x4, matrix products, attend(): jnp.einsum('qd,kd->qk', query_block, doc_keys, preferred_element_type=jnp...  39.4 us
    reduce_sum x8, other arithmetic, attend(): total = jnp.sum(doc_expd, axis=1) + jnp.sum(self_expd, axis=1)  36.5 us
    dot_general x4, matrix products, attend(): jnp.dot(doc_expd.astype(jnp.bfloat16), doc_values, preferred_element_type...  30.3 us
    all_to_all x1, waiting for transfers between devices, shards(): lax.all_to_all(outgoing, 'cache', split_axis=0, concat_axis=0, tiled=True)  23.9 us
    another operation x1, loops' own time, shards(): lax.map(attend, jnp.arange(per_device * block_count, dtype=jnp.int32))  11.3 us
    all_to_all x1, starting transfers between devices, shards(): lax.all_to_all(spread, ('dh', 'dq'), split_axis=0, concat_axis=2, tiled=T...  10.7 us
  transfers between devices with their start and end apart: 4, of which 3 were waited for; matrix products, arithmetic and copies ran while one was open for 8% of the time, Pallas kernels for 0%

profile of v1, /device:TPU:16, one launch (start us, length us, event | category | flops | bytes accessed | tf_op | source)
XLA Modules:
  0.0 433.8 jit_solution(604568661620236360)
XLA Ops:
  6.5 1.6 copy.44
  9.9 1.7 convolution_bitcast_fusion
  12.4 3.5 pad_maximum_fusion
  16.6 1.3 gather_fusion
  19.0 2.0 gather_fusion.1
  21.1 3.3 select_select_fusion
  24.4 5.6 %all-to-all-start = ((bf16[8,4,16,2048]{3,2,1,0:T(8,128)(2,1)}), bf16[8,4,16,2048]{3,2,1,0:T(8,128)(2,1)S(1)}, u32[]{:S(2)}, u32[]{:S(2)}) async-start(bf16[8,4,16,2048]{3,2,1,0:T(8,128)(2,1)} %select_select_fusion), calls=%async_computation.1 | async-start | bytes 4194304 | tf_op jit(solution)/shard_map/all_to_all | solution.py:65
  30.0 23.9 %all-to-all-done = bf16[8,4,16,2048]{3,2,1,0:T(8,128)(2,1)S(1)} async-done(((bf16[8,4,16,2048]{3,2,1,0:T(8,128)(2,1)}), bf16[8,4,16,2048]{3,2,1,0:T(8,128)(2,1)S(1)}, u32[]{:S(2)}, u32[]{:S(2)}) %all-to-all-start) | async-done | bytes 2097184 | tf_op jit(solution)/shard_map/all_to_all | solution.py:65
  55.1 3.4 gather_fusion.3
  58.5 5.7 %copy_bitcast_fusion = bf16[32,16,16,256]{3,2,1,0:T(8,128)(2,1)} fusion(bf16[32,16,16,2,128]{4,2,3,1,0:T(8,128)(2,1)} %gather_fusion.3, pred[32]{0:T(512)(128)(4,1)S(1)} %compare_and_fusion.2), kind=kLoop, calls=%fused_computation.31 | loop fusion | flops 2097152 | bytes 8388640 | tf_op jit(solution)/shard_map/reshape | solution.py:33
  64.3 10.7 %all-to-all-start.1 = ((bf16[32,16,16,256]{3,2,1,0:T(8,128)(2,1)}), bf16[32,16,16,256]{3,2,1,0:T(8,128)(2,1)}, u32[]{:S(2)}, u32[]{:S(2)}) async-start(bf16[32,16,16,256]{3,2,1,0:T(8,128)(2,1)} %copy_bitcast_fusion), calls=%async_computation.2 | async-start | bytes 8388608 | tf_op jit(solution)/shard_map/all_to_all | solution.py:68
  75.2 149.2 %reduce-scatter.2.cloned.1.call-done = f32[1,512,384]{1,2,0:T(8,128)} async-done(((f32[8,512,384]{1,2,0:T(8,128)}), f32[1,512,384]{1,2,0:T(8,128)}) %reduce-scatter.2.cloned.1.call-update) | async-done | bytes 786448 | tf_op jit(solution)/shard_map/reduce_scatter | solution.py:81
  224.4 5.6 %copy.49 = bf16[128,8,16,128]{3,2,1,0:T(8,128)(2,1)} copy(bf16[128,8,16,128]{3,1,2,0:T(8,128)(2,1)} %bitcast.106) | data formatting | bytes 8388608
  230.0 5.9 %dynamic-slice_reduce_fusion = bf16[1024,2,128]{2,1,0:T(2,128)(2,1)S(1)} fusion(bf16[1024,2,8,128]{3,2,1,0:T(8,128)(2,1)} %bitcast.102, s32[]{:T(128)S(6)} %select_n.206), kind=kLoop, calls=%fused_computation.37 | loop fusion | bytes 1048580 | tf_op jit(solution)/shard_map/jit(dynamic_index_in_dim)/dynamic_slice | solution.py:25
  237.4 4.6 %copy.39 = bf16[1,16,32,16,256]{4,3,2,1,0:T(8,128)(2,1)} copy(bf16[1,16,32,16,256]{4,3,1,2,0:T(8,128)(2,1)} %bitcast.21) | data formatting | bytes 8388608 | tf_op jit(solution)/shard_map/all_to_all | solution.py:68
  241.9 44.5 %all-reduce.2.cloned.1.call-done = f32[512,384]{0,1:T(8,128)} async-done(((f32[512,384]{0,1:T(8,128)}), f32[512,384]{0,1:T(8,128)}) %all-reduce.2.cloned.1.call-update) | async-done | bytes 786448 | tf_op jit(solution)/shard_map/psum | solution.py:82
  288.4 4.9 %convert_select_fusion = bf16[16,512,256]{2,1,0:T(8,128)(2,1)S(1)} fusion(bf16[16,512,256]{2,1,0:T(8,128)(2,1)} %bitcast.99, pred[16,512]{1,0:T(8,128)(4,1)S(1)} %fusion.22, bf16[16,32,256]{2,1,0:T(8,128)(2,1)S(1)} %bitcast.111, s32[16,32]{1,0:T(8,128)S(1)} %bitcast.115), kind=kOutput, calls=%fused_computation.33 | convolution fusion | flops 138674176 | bytes 8660992 | tf_op jit(solution)/shard_map/kib,kic->kbc/dot_general | solution.py:93
  293.4 2.5 fusion.43
  295.9 128.2 %while.14 = (s32[]{:T(128)}, bf16[4,512,128]{2,1,0:T(8,128)(2,1)}, s32[4]{0:T(128)S(1)}, bf16[2,1024,128]{1,2,0:T(8,128)(2,1)S(1)}, bf16[8192,128]{1,0:T(8,128)(...) while((s32[]{:T(128)}, bf16[4,512,128]{2,1,0:T(8,128)(2,1)}, ...), condition=%wide.region_12.13_spmd.clone, body=%wide.region_7.12_spmd.clone.sunk | while | flops 2453863936 | bytes 63343596 | solution.py:139
  299.3 9.9 %multiply_reduce_fusion.2 = (f32[512]{0:T(512)S(1)}, f32[512,8192]{1,0:T(8,128)}) fusion(bf16[8192,128]{1,0:T(8,128)(2,1)} %get-tuple-element.316, bf16[2,1024,128]{1,2,0:T(8,128)(2,1)S(1)} %get-tuple-element.315, s32[]{:T(128)S(6)} %select_n.270, s32[]{:T(128)S(6)} %select_n.273), kind=kOutput, calls=%fused_computation.6.clone.1 | convolution fusion | flops 1082129920 | bytes 19007496 | tf_op jit(solution)/shard_map/while/body/eval_jaxpr/qd,kd->qk/dot_general | solution.py:116
  310.5 8.6 %fusion.70 = f32[512]{0:T(512)S(1)} fusion(f32[512,8192]{1,0:T(8,128)} %get-tuple-element.280, f32[512]{0:T(512)S(1)} %max.13), kind=kLoop, calls=%fused_computation.7.clone.1 | loop fusion | flops 12582400 | bytes 16781312 | tf_op jit(solution)/shard_map/while/body/eval_jaxpr/reduce_sum | solution.py:130
  319.2 7.6 %fusion.69 = f32[512,128]{1,0:T(8,128)S(1)} fusion(bf16[8192,128]{1,0:T(8,128)(2,1)S(1)} %get-tuple-element.318, f32[512,8192]{1,0:T(8,128)} %get-tuple-element.280, f32[512]{0:T(512)S(1)} %max.13), kind=kOutput, calls=%fused_computation.9.clone.1 | convolution fusion | flops 1086324736 | bytes 19138560 | tf_op jit(solution)/shard_map/while/body/eval_jaxpr/dot_general | solution.py:131
  331.4 9.9 %multiply_reduce_fusion.2 = (f32[512]{0:T(512)S(1)}, f32[512,8192]{1,0:T(8,128)}) fusion(bf16[8192,128]{1,0:T(8,128)(2,1)} %get-tuple-element.316, bf16[2,1024,128]{1,2,0:T(8,128)(2,1)S(1)} %get-tuple-element.315, s32[]{:T(128)S(6)} %select_n.270, s32[]{:T(128)S(6)} %select_n.273), kind=kOutput, calls=%fused_computation.6.clone.1 | convolution fusion | flops 1082129920 | bytes 19007496 | tf_op jit(solution)/shard_map/while/body/eval_jaxpr/qd,kd->qk/dot_general | solution.py:116
  342.6 8.6 %fusion.70 = f32[512]{0:T(512)S(1)} fusion(f32[512,8192]{1,0:T(8,128)} %get-tuple-element.280, f32[512]{0:T(512)S(1)} %max.13), kind=kLoop, calls=%fused_computation.7.clone.1 | loop fusion | flops 12582400 | bytes 16781312 | tf_op jit(solution)/shard_map/while/body/eval_jaxpr/reduce_sum | solution.py:130
  351.2 7.6 %fusion.69 = f32[512,128]{1,0:T(8,128)S(1)} fusion(bf16[8192,128]{1,0:T(8,128)(2,1)S(1)} %get-tuple-element.318, f32[512,8192]{1,0:T(8,128)} %get-tuple-element.280, f32[512]{0:T(512)S(1)} %max.13), kind=kOutput, calls=%fused_computation.9.clone.1 | convolution fusion | flops 1086324736 | bytes 19138560 | tf_op jit(solution)/shard_map/while/body/eval_jaxpr/dot_general | solution.py:131
  363.5 9.8 %multiply_reduce_fusion.2 = (f32[512]{0:T(512)S(1)}, f32[512,8192]{1,0:T(8,128)}) fusion(bf16[8192,128]{1,0:T(8,128)(2,1)} %get-tuple-element.316, bf16[2,1024,128]{1,2,0:T(8,128)(2,1)S(1)} %get-tuple-element.315, s32[]{:T(128)S(6)} %select_n.270, s32[]{:T(128)S(6)} %select_n.273), kind=kOutput, calls=%fused_computation.6.clone.1 | convolution fusion | flops 1082129920 | bytes 19007496 | tf_op jit(solution)/shard_map/while/body/eval_jaxpr/qd,kd->qk/dot_general | solution.py:116
  374.6 8.6 %fusion.70 = f32[512]{0:T(512)S(1)} fusion(f32[512,8192]{1,0:T(8,128)} %get-tuple-element.280, f32[512]{0:T(512)S(1)} %max.13), kind=kLoop, calls=%fused_computation.7.clone.1 | loop fusion | flops 12582400 | bytes 16781312 | tf_op jit(solution)/shard_map/while/body/eval_jaxpr/reduce_sum | solution.py:130
  383.3 7.6 %fusion.69 = f32[512,128]{1,0:T(8,128)S(1)} fusion(bf16[8192,128]{1,0:T(8,128)(2,1)S(1)} %get-tuple-element.318, f32[512,8192]{1,0:T(8,128)} %get-tuple-element.280, f32[512]{0:T(512)S(1)} %max.13), kind=kOutput, calls=%fused_computation.9.clone.1 | convolution fusion | flops 1086324736 | bytes 19138560 | tf_op jit(solution)/shard_map/while/body/eval_jaxpr/dot_general | solution.py:131
  395.5 9.8 %multiply_reduce_fusion.2 = (f32[512]{0:T(512)S(1)}, f32[512,8192]{1,0:T(8,128)}) fusion(bf16[8192,128]{1,0:T(8,128)(2,1)} %get-tuple-element.316, bf16[2,1024,128]{1,2,0:T(8,128)(2,1)S(1)} %get-tuple-element.315, s32[]{:T(128)S(6)} %select_n.270, s32[]{:T(128)S(6)} %select_n.273), kind=kOutput, calls=%fused_computation.6.clone.1 | convolution fusion | flops 1082129920 | bytes 19007496 | tf_op jit(solution)/shard_map/while/body/eval_jaxpr/qd,kd->qk/dot_general | solution.py:116
  406.7 8.6 %fusion.70 = f32[512]{0:T(512)S(1)} fusion(f32[512,8192]{1,0:T(8,128)} %get-tuple-element.280, f32[512]{0:T(512)S(1)} %max.13), kind=kLoop, calls=%fused_computation.7.clone.1 | loop fusion | flops 12582400 | bytes 16781312 | tf_op jit(solution)/shard_map/while/body/eval_jaxpr/reduce_sum | solution.py:130
  415.3 7.6 %fusion.69 = f32[512,128]{1,0:T(8,128)S(1)} fusion(bf16[8192,128]{1,0:T(8,128)(2,1)S(1)} %get-tuple-element.318, f32[512,8192]{1,0:T(8,128)} %get-tuple-element.280, f32[512]{0:T(512)S(1)} %max.13), kind=kOutput, calls=%fused_computation.9.clone.1 | convolution fusion | flops 1086324736 | bytes 19138560 | tf_op jit(solution)/shard_map/while/body/eval_jaxpr/dot_general | solution.py:131
  424.1 1.7 copy.56
  (92 shorter events, 22.9 us)
Async XLA Ops:
  6.5 12.5 %copy-start = (bf16[32,16,2048]{2,1,0:T(8,128)(2,1)S(1)}, bf16[32,16,2048]{2,1,0:T(8,128)(2,1)}, u32[]{:S(2)}) copy-start(bf16[32,16,2048]{2,1,0:T(8,128)(2,1)} %param.12) | copy-start | bytes 6291460
  6.5 217.8 %reduce-scatter.2.cloned.1.call-start = ((), (), s32[]{:S(2)}) async-start(), calls=%async_computation.3 | async-start | bytes 7077888 | tf_op jit(solution)/shard_map/reduce_scatter | solution.py:81
  15.8 0.7 copy-start.5
  15.8 0.8 copy-start.2
  24.4 29.6 %all-to-all-start = ((bf16[8,4,16,2048]{3,2,1,0:T(8,128)(2,1)}), bf16[8,4,16,2048]{3,2,1,0:T(8,128)(2,1)S(1)}, u32[]{:S(2)}, u32[]{:S(2)}) async-start(bf16[8,4,16,2048]{3,2,1,0:T(8,128)(2,1)} %select_select_fusion), calls=%async_computation.1 | async-start | bytes 4194304 | tf_op jit(solution)/shard_map/all_to_all | solution.py:65
  64.3 173.1 %all-to-all-start.1 = ((bf16[32,16,16,256]{3,2,1,0:T(8,128)(2,1)}), bf16[32,16,16,256]{3,2,1,0:T(8,128)(2,1)}, u32[]{:S(2)}, u32[]{:S(2)}) async-start(bf16[32,16,16,256]{3,2,1,0:T(8,128)(2,1)} %copy_bitcast_fusion), calls=%async_computation.2 | async-start | bytes 8388608 | tf_op jit(solution)/shard_map/all_to_all | solution.py:68
  75.0 211.5 %all-reduce.2.cloned.1.call-start = ((), (), s32[]{:S(2)}) async-start(), calls=%async_computation.4 | async-start | bytes 1572864 | tf_op jit(solution)/shard_map/psum | solution.py:82
  224.4 11.6 %copy-start.3 = (bf16[1,1024,256]{2,1,0:T(8,128)(2,1)S(1)}, bf16[1,1024,256]{2,1,0:T(8,128)(2,1)}, u32[]{:S(2)}) copy-start(bf16[1,1024,256]{2,1,0:T(8,128)(2,1)} %param.11) | copy-start | bytes 1572868
  224.4 11.8 %copy-start.6 = (s32[1,16,32]{2,1,0:T(8,128)S(1)}, s32[1,16,32]{2,1,0:T(8,128)}, u32[]{:S(2)}) copy-start(s32[1,16,32]{2,1,0:T(8,128)} %param.19) | copy-start | bytes 6148
  299.3 9.9 %copy-start.4 = (bf16[1024,128]{1,0:T(8,128)(2,1)S(1)}, bf16[1024,128]{1,0:T(8,128)(2,1)}, u32[]{:S(2)}) copy-start(bf16[1024,128]{1,0:T(8,128)(2,1)} %get-tuple-element.317) | copy-start | bytes 786436 | tf_op jit(solution)/shard_map/while
  331.4 9.9 %copy-start.4 = (bf16[1024,128]{1,0:T(8,128)(2,1)S(1)}, bf16[1024,128]{1,0:T(8,128)(2,1)}, u32[]{:S(2)}) copy-start(bf16[1024,128]{1,0:T(8,128)(2,1)} %get-tuple-element.317) | copy-start | bytes 786436 | tf_op jit(solution)/shard_map/while
  363.4 9.9 %copy-start.4 = (bf16[1024,128]{1,0:T(8,128)(2,1)S(1)}, bf16[1024,128]{1,0:T(8,128)(2,1)}, u32[]{:S(2)}) copy-start(bf16[1024,128]{1,0:T(8,128)(2,1)} %get-tuple-element.317) | copy-start | bytes 786436 | tf_op jit(solution)/shard_map/while
  395.5 9.9 %copy-start.4 = (bf16[1024,128]{1,0:T(8,128)(2,1)S(1)}, bf16[1024,128]{1,0:T(8,128)(2,1)}, u32[]{:S(2)}) copy-start(bf16[1024,128]{1,0:T(8,128)(2,1)} %get-tuple-element.317) | copy-start | bytes 786436 | tf_op jit(solution)/shard_map/while
  424.1 2.9 copy-start.1
Sparse Core Ops, SparseCore 0:
  16.0 208.3 reduce-scatter.1
  227.2 59.2 all-reduce.1

commit v2 on v1

v2 whole, which is shorter than its diff:
```python
import functools
import math

import jax
import jax.numpy as jnp
from jax import lax
from jax.experimental import pallas as pl
from jax.experimental.pallas import tpu as pltpu
from jax.sharding import Mesh, PartitionSpec as P

D = 8192
QH = 64
KVH = 8
HD = 128
RET = 16
CAP = 4
REC = 32
DOC_GRP = 32
MODE = 2
SQ_ROWS = 128


eps_norm = 1e-05
tile_rows = 512


def own_head(wide_rows, head_count, head_size, chosen):
    shaped = wide_rows.reshape(wide_rows.shape[:-1] + (2, head_count, head_size))
    taken = lax.dynamic_index_in_dim(shaped, chosen, shaped.ndim - 2, keepdims=False)
    return taken.reshape(wide_rows.shape[:-1] + (2 * head_size,))


def pick_heads(wide_rows, head_count, head_size, chosen):
    shaped = wide_rows.reshape(wide_rows.shape[:-1] + (2, head_count, head_size))
    taken = jnp.take(shaped, chosen, axis=shaped.ndim - 2)
    moved = jnp.moveaxis(taken, shaped.ndim - 2, 0)
    return moved.reshape(moved.shape[:-2] + (2 * head_size,))


def attn_kernel(q_ref, kd_ref, vd_ref, ks_ref, vs_ref, o_ref, m_sc, l_sc, acc_sc, *, n_doc, n_self, blk, inv_root):
    phase = pl.program_id(1)
    j = pl.program_id(2)
    rows = q_ref.shape[0]

    @pl.when((phase == 0) & (j == 0))
    def _():
        m_sc[...] = jnp.full(m_sc.shape, -jnp.inf, jnp.float32)
        l_sc[...] = jnp.zeros(l_sc.shape, jnp.float32)
        acc_sc[...] = jnp.zeros(acc_sc.shape, jnp.float32)

    def scores(k_ref, first_key):
        s = lax.dot_general(q_ref[...], k_ref[...], (((1,), (1,)), ((), ())),
                            preferred_element_type=jnp.float32) * inv_root
        if first_key is None:
            return s
        t = lax.broadcasted_iota(jnp.int32, s.shape, 0)
        u = lax.broadcasted_iota(jnp.int32, s.shape, 1) + first_key
        return jnp.where(u <= t, s, -jnp.inf)

    def step(k_ref, v_ref, first_key):
        @pl.when(phase == 0)
        def _():
            s = scores(k_ref, first_key)
            m_sc[...] = jnp.maximum(m_sc[...], jnp.max(s, axis=1, keepdims=True))

        @pl.when(phase == 1)
        def _():
            s = scores(k_ref, first_key)
            e = jnp.exp(s - m_sc[:, :1])
            l_sc[...] = l_sc[...] + jnp.sum(e, axis=1, keepdims=True)
            acc_sc[...] = acc_sc[...] + jnp.dot(e.astype(jnp.bfloat16), v_ref[...],
                                                preferred_element_type=jnp.float32)

    @pl.when(j < n_doc)
    def _():
        step(kd_ref, vd_ref, None)

    for b in range(n_self):
        @pl.when(j == n_doc + b)
        def _(b=b):
            step(ks_ref, vs_ref, b * blk)

    @pl.when((phase == 1) & (j == pl.num_programs(2) - 1))
    def _():
        o_ref[...] = (acc_sc[...] / l_sc[:, :1]).astype(o_ref.dtype)


def attention(q2d, blocks, own_self):
    T, width = q2d.shape
    heads = width // HD
    n_doc, blk, _ = blocks.shape
    n_self = T // blk
    last_doc = n_doc - 1
    kern = functools.partial(attn_kernel, n_doc=n_doc, n_self=n_self, blk=blk, inv_root=1.0 / math.sqrt(HD))
    doc_at = lambda j: jnp.minimum(j, last_doc)
    self_at = lambda j: jnp.maximum(j - n_doc, 0)
    return pl.pallas_call(
        kern,
        grid=(heads, 2, n_doc + n_self),
        in_specs=[
            pl.BlockSpec((T, HD), lambda h, p, j: (0, h)),
            pl.BlockSpec((None, blk, HD), lambda h, p, j: (doc_at(j), 0, 0)),
            pl.BlockSpec((None, blk, HD), lambda h, p, j: (doc_at(j), 0, 1)),
            pl.BlockSpec((blk, HD), lambda h, p, j: (self_at(j), 0)),
            pl.BlockSpec((blk, HD), lambda h, p, j: (self_at(j), 1)),
        ],
        out_specs=pl.BlockSpec((T, HD), lambda h, p, j: (0, h)),
        out_shape=jax.ShapeDtypeStruct((T, width), q2d.dtype),
        scratch_shapes=[pltpu.VMEM((T, HD), jnp.float32)] * 3,
    )(q2d, blocks, blocks, own_self, own_self)


def shards(queries, store_kv, self_kv, rec_states, norm_gain, w_kv, retrieval, doc_home, rec_index):
    groups = lax.axis_size("cache")
    members = lax.axis_size("dh") * lax.axis_size("dq")
    my_group = lax.axis_index("cache")
    my_member = lax.axis_index("dh") * lax.axis_size("dq") + lax.axis_index("dq")
    per_device = QH // members
    ratio_heads = QH // KVH
    my_head = my_member * per_device // ratio_heads
    shard_rows = store_kv.shape[1]
    kv_width = store_kv.shape[2]
    inv_root = 1.0 / math.sqrt(HD)
    stored_at = jnp.take(doc_home, retrieval, axis=0)
    source = stored_at // DOC_GRP
    local_row = stored_at % DOC_GRP
    before = jnp.arange(RET)[None, :] < jnp.arange(RET)[:, None]
    same_home = source[:, :, None] == source[:, None, :]
    rank_within = jnp.sum((same_home & before[None, :, :]).astype(jnp.int32), axis=2)
    places = jnp.arange(CAP, dtype=jnp.int32)
    matching = (source[:, None, :] == my_group) & (rank_within[:, None, :] == places[None, :, None])
    pick_row = jnp.sum(jnp.where(matching, local_row[:, None, :], 0), axis=2)
    filled = jnp.any(matching, axis=2)
    outgoing = jnp.take(store_kv, pick_row.reshape(-1), axis=0).reshape(
        groups, CAP, shard_rows, kv_width
    )
    outgoing = jnp.where(filled[:, :, None, None], outgoing, jnp.zeros((), store_kv.dtype))
    my_source = lax.dynamic_index_in_dim(source, my_group, 0, keepdims=False)
    my_rank = lax.dynamic_index_in_dim(rank_within, my_group, 0, keepdims=False)
    slot_place = my_source * CAP + my_rank
    dest_heads = jnp.arange(members, dtype=jnp.int32) * per_device // ratio_heads
    arrived = lax.all_to_all(outgoing, "cache", split_axis=0, concat_axis=0, tiled=True)
    compact = jnp.take(arrived.reshape(groups * CAP, shard_rows, kv_width), slot_place, axis=0)
    spread = pick_heads(compact, KVH, HD, dest_heads)
    fetched = lax.all_to_all(spread, ("dh", "dq"), split_axis=0, concat_axis=2, tiled=True)[0]
    states = rec_states[0].astype(jnp.float32)
    rows_rec = states.shape[0]
    partial_sq = jnp.sum(states * states, axis=1)
    if MODE == 0:
        total_sq = lax.psum(partial_sq, ("dh", "dq"))
    elif MODE == 1:
        total_sq = lax.psum(lax.psum(partial_sq, "dq"), "dh")
    else:
        total_sq = lax.psum(jnp.broadcast_to(partial_sq[None, :], (SQ_ROWS, rows_rec)), ("dh", "dq"))[0]
    inv_rms = lax.rsqrt(total_sq / D + eps_norm)
    normed = (states * norm_gain.astype(jnp.float32)[None, :] * inv_rms[:, None]).astype(jnp.bfloat16)
    partial_kv = jnp.dot(normed, w_kv, preferred_element_type=jnp.float32)
    by_head = jnp.transpose(partial_kv.reshape(rows_rec, 2, KVH, HD), (2, 0, 1, 3)).reshape(KVH, rows_rec, 2 * HD)
    head_sum = lax.psum_scatter(by_head, "dh", scatter_dimension=0, tiled=True)[0]
    redone = lax.psum(head_sum, "dq")
    own_rows = redone.reshape(RET, REC, 2 * HD)
    full_block = fetched.shape[1]
    positions = rec_index[0]
    onehot = positions[:, :, None] == jnp.arange(full_block, dtype=jnp.int32)[None, None, :]
    placed = jnp.einsum(
        "kib,kic->kbc", onehot.astype(jnp.float32), own_rows, precision=lax.Precision.HIGHEST
    ).astype(jnp.bfloat16)
    replaced_at = jnp.any(onehot, axis=1)
    blocks = jnp.where(replaced_at[:, :, None], placed, fetched)
    own_self = own_head(self_kv[0], KVH, HD, my_head)
    return attention(queries[0], blocks, own_self)[None]


def solution(mesh):
    dev = ("dh", "dq")
    groups = mesh.shape["cache"]
    members = mesh.shape["dev"]
    view = Mesh(mesh.devices.reshape(groups, KVH, members // KVH), ("cache", "dh", "dq"))
    placed = (
        P("cache", None, dev),
        P("cache", dev, None),
        P("cache", None, None),
        P("cache", None, dev),
        P(dev),
        P(dev, None),
        P(),
        P(),
        P("cache", None, None),
    )
    return jax.shard_map(
        shards, mesh=view, in_specs=placed, out_specs=P("cache", None, dev), check_vma=False
    )
```

time: 435 us -> 479 us (1.10)
  waiting for transfers between devices: 218 us -> 332 us
  matrix products: 84.3 us -> 8.64 us
  Pallas kernels: 0 us -> 64.7 us
  other arithmetic: 54 us -> 12 us
  loops' own time: 11.3 us -> 0 us
    psum x1 -> x2, waiting for transfers between devices: 44.5 us -> 180 us  [the longest x1 147 us: shards(): lax.psum(jnp.broadcast_to(partial_sq[None, :], (SQ_ROWS, rows_rec)), ('dh...]
    dot_general x18 -> x2, matrix products: 84.3 us -> 8.64 us  [the longest x1 7.83 us: shards(): jnp.einsum('kib,kic->kbc', onehot.astype(jnp.float32), own_rows, precisio...]
    pallas_call x0 -> x1, Pallas kernels: none -> 64.7 us  [attention(): pl.pallas_call(kern, grid=(heads, 2, n_doc + n_self), in_specs=[pl.BlockS...]
    reduce_sum x8 -> x0, other arithmetic: 36.5 us -> none  [attend(): total = jnp.sum(doc_expd, axis=1) + jnp.sum(self_expd, axis=1)]
    all_to_all x1, waiting for transfers between devices: 23.9 us -> 0.01 us  [shards(): lax.all_to_all(outgoing, 'cache', split_axis=0, concat_axis=0, tiled=True)]
    another operation x1 -> x0, loops' own time: 11.3 us -> none  [shards(): lax.map(attend, jnp.arange(per_device * block_count, dtype=jnp.int32))]
    all_to_all x1, starting transfers between devices: 10.7 us -> 5.67 us  [shards(): lax.all_to_all(spread, ('dh', 'dq'), split_axis=0, concat_axis=2, tiled=T...]
  transfers between devices with their start and end apart: 4 -> 5, of which waited for: 3 -> 3; matrix products, arithmetic and copies ran while one was open for 8% -> 8% of each run, Pallas kernels for 0% -> 0%
where the time goes in v2:
time: 479 us; the launch traced here: 477 us
  waiting for transfers between devices  332 us (69%)
  Pallas kernels  64.7 us (14%)
  local copies, waits for them, and re-layouts  33.9 us (7%)
  between operations  13.3 us (3%)
  starting transfers between devices  12.3 us (3%)
  other arithmetic  12 us (3%)
  matrix products  8.64 us (2%)
    reduce_scatter x1, waiting for transfers between devices, shards(): lax.psum_scatter(by_head, 'dh', scatter_dimension=0, tiled=True)[0]  153 us
    psum x1, waiting for transfers between devices, shards(): lax.psum(jnp.broadcast_to(partial_sq[None, :], (SQ_ROWS, rows_rec)), ('dh...  147 us
    pallas_call x1, Pallas kernels, attention(): pl.pallas_call(kern, grid=(heads, 2, n_doc + n_self), in_specs=[pl.BlockS...  64.7 us
    psum x1, waiting for transfers between devices, shards(): redone = lax.psum(head_sum, 'dq')  32.5 us
  transfers between devices with their start and end apart: 5, of which 3 were waited for; matrix products, arithmetic and copies ran while one was open for 8% of the time, Pallas kernels for 0%

profile of v2, /device:TPU:16, one launch (start us, length us, event | category | flops | bytes accessed | tf_op | source)
XLA Modules:
  0.0 477.2 jit_solution(10538020313079921616)
XLA Ops:
  6.6 0.8 compare_select_fusion
  7.5 1.6 gather_fusion
  9.2 0.3 convert_reduce_fusion
  9.5 0.2 fusion.10
  9.7 0.2 select_reduce_fusion
  10.2 2.0 gather_fusion.1
  12.2 3.3 select_select_fusion
  15.6 6.3 %all-to-all-start = ((bf16[8,4,16,2048]{3,2,1,0:T(8,128)(2,1)}), bf16[8,4,16,2048]{3,2,1,0:T(8,128)(2,1)}, u32[]{:S(2)}, u32[]{:S(2)}) async-start(bf16[8,4,16,2048]{3,2,1,0:T(8,128)(2,1)} %select_select_fusion), calls=%async_computation.1 | async-start | bytes 4194304 | tf_op jit(solution)/shard_map/all_to_all | solution.py:142
  21.9 0.1 fusion.3
  22.1 0.7 broadcast_in_dim.94
  22.9 1.5 copy.34
  24.4 147.0 %all-reduce.3.cloned.1.call-done = f32[128,512]{1,0:T(8,128)} async-done(((f32[128,512]{1,0:T(8,128)}), f32[128,512]{1,0:T(8,128)}) %all-reduce.3.cloned.1.call-update) | async-done | bytes 262160 | tf_op jit(solution)/shard_map/psum | solution.py:154
  171.4 0.7 fusion.14
  172.1 0.8 convolution_bitcast_fusion
  172.9 2.7 copy.24
  175.7 2.2 gather_fusion.2
  177.9 0.2 copy.37
  178.1 0.2 copy_select_fusion
  178.4 3.3 gather_fusion.3
  181.7 5.6 %copy_bitcast_fusion = bf16[32,16,16,256]{3,2,1,0:T(8,128)(2,1)} fusion(bf16[32,16,16,2,128]{4,2,3,1,0:T(8,128)(2,1)} %gather_fusion.3, pred[32]{0:T(512)(128)(4,1)S(1)} %compare_and_fusion.2), kind=kLoop, calls=%fused_computation.4 | loop fusion | flops 2097152 | bytes 8388640 | tf_op jit(solution)/shard_map/reshape | solution.py:37
  187.3 5.7 %all-to-all-start.1 = ((bf16[32,16,16,256]{3,2,1,0:T(8,128)(2,1)}), bf16[32,16,16,256]{3,2,1,0:T(8,128)(2,1)}, u32[]{:S(2)}, u32[]{:S(2)}) async-start(bf16[32,16,16,256]{3,2,1,0:T(8,128)(2,1)} %copy_bitcast_fusion), calls=%async_computation.2 | async-start | bytes 8388608 | tf_op jit(solution)/shard_map/all_to_all | solution.py:145
  193.0 0.2 all-reduce.5.cloned.1.call-start
  193.2 152.9 %reduce-scatter.2.cloned.1.call-done = f32[1,512,256]{1,2,0:T(8,128)} async-done(((f32[8,512,256]{1,2,0:T(8,128)}), f32[1,512,256]{1,2,0:T(8,128)}) %reduce-scatter.2.cloned.1.call-update) | async-done | bytes 524304 | tf_op jit(solution)/shard_map/reduce_scatter | solution.py:159
  346.2 2.0 copy.25
  348.2 5.6 %copy.38 = bf16[128,8,16,128]{3,2,1,0:T(8,128)(2,1)} copy(bf16[128,8,16,128]{3,1,2,0:T(8,128)(2,1)} %bitcast.60) | data formatting | bytes 8388608
  353.8 5.9 %dynamic-slice_reduce_fusion = bf16[1024,2,128]{2,1,0:T(2,128)(2,1)S(1)} fusion(bf16[1024,2,8,128]{3,2,1,0:T(8,128)(2,1)} %bitcast.55, s32[]{:T(128)S(6)} %select_n.160), kind=kLoop, calls=%fused_computation.10 | loop fusion | bytes 1048580 | tf_op jit(solution)/shard_map/jit(dynamic_index_in_dim)/dynamic_slice | solution.py:29
  359.8 0.9 copy.43
  360.7 0.3 fusion
  361.0 4.6 copy.31
  365.7 32.5 %all-reduce.5.cloned.1.call-done = f32[16,32,256]{2,1,0:T(8,128)} async-done(((f32[16,32,256]{2,1,0:T(8,128)}), f32[16,32,256]{2,1,0:T(8,128)}) %all-reduce.5.cloned.1.call-update) | async-done | bytes 524304 | tf_op jit(solution)/shard_map/psum | solution.py:160
  398.2 7.8 %convert_select_fusion.kd_ref.vd_ref = bf16[16,512,256]{2,1,0:T(8,128)(2,1)} fusion(bf16[16,512,256]{2,1,0:T(8,128)(2,1)} %bitcast.53, pred[16,512]{1,0:T(8,128)(4,1)S(1)} %fusion, f32[16,32,256]{2,1,0:T(8,128)} %all-reduce.5.cloned.1.call-done, s32[16,32]{1,0:T(8,128)S(1)} %bitcast.67), kind=kOutput, calls=%fused_computation.6 | convolution fusion | flops 809762816 | bytes 8923136 | tf_op jit(solution)/shard_map/kib,kic->kbc/dot_general | solution.py:165
  406.0 64.7 %shard_map.91 = bf16[1024,256]{1,0:T(8,128)(2,1)} custom-call(bf16[1024,256]{1,0:T(8,128)(2,1)} %bitcast.65, bf16[16,512,256]{2,1,0:T(8,128)(2,1)} %convert_select_fusion.kd_ref.vd_ref, bf16[16,512,256]{2,1,0:T(8,128)(2,1)} %convert_select_fusion.kd_ref.vd_ref, bf16[1024,256]{1,0:T(8,128)(2,1)} %bitcast.56, bf16[1024,256]{1,0:T(8,128)(2,1)} %bitcast.57), custom_call_target="tpu_custom_call" | custom-call | tf_op jit(solution)/shard_map/pallas_call | solution.py:97
  (36 shorter events, 0.8 us)
Async XLA Ops:
  6.5 3.7 copy-start
  6.5 2.7 copy-start.2
  12.2 9.7 %copy-start.1 = (bf16[1,512,256]{2,1,0:T(8,128)(2,1)S(1)}, bf16[1,512,256]{2,1,0:T(8,128)(2,1)}, u32[]{:S(2)}) copy-start(bf16[1,512,256]{2,1,0:T(8,128)(2,1)} %param.12) | copy-start | bytes 786436
  12.2 10.7 %copy-start.4 = (bf16[256]{0:T(256)(128)(2,1)S(1)}, bf16[256]{0:T(256)(128)(2,1)}, u32[]{:S(2)}) copy-start(bf16[256]{0:T(256)(128)(2,1)} %param.13) | copy-start | bytes 1540
  15.6 160.1 %all-to-all-start = ((bf16[8,4,16,2048]{3,2,1,0:T(8,128)(2,1)}), bf16[8,4,16,2048]{3,2,1,0:T(8,128)(2,1)}, u32[]{:S(2)}, u32[]{:S(2)}) async-start(bf16[8,4,16,2048]{3,2,1,0:T(8,128)(2,1)} %select_select_fusion), calls=%async_computation.1 | async-start | bytes 4194304 | tf_op jit(solution)/shard_map/all_to_all | solution.py:142
  21.9 149.5 %all-reduce.3.cloned.1.call-start = ((), (), s32[]{:S(2)}) async-start(), calls=%async_computation.3 | async-start | bytes 524288 | tf_op jit(solution)/shard_map/psum | solution.py:154
  22.8 323.3 %reduce-scatter.2.cloned.1.call-start = ((), (), s32[]{:S(2)}) async-start(), calls=%async_computation.4 | async-start | bytes 4718592 | tf_op jit(solution)/shard_map/reduce_scatter | solution.py:159
  187.3 173.7 %all-to-all-start.1 = ((bf16[32,16,16,256]{3,2,1,0:T(8,128)(2,1)}), bf16[32,16,16,256]{3,2,1,0:T(8,128)(2,1)}, u32[]{:S(2)}, u32[]{:S(2)}) async-start(bf16[32,16,16,256]{3,2,1,0:T(8,128)(2,1)} %copy_bitcast_fusion), calls=%async_computation.2 | async-start | bytes 8388608 | tf_op jit(solution)/shard_map/all_to_all | solution.py:145
  193.0 205.2 %all-reduce.5.cloned.1.call-start = ((), (), s32[]{:S(2)}) async-start(), calls=%async_computation.5 | async-start | bytes 1048576 | tf_op jit(solution)/shard_map/psum | solution.py:160
  348.2 12.5 %copy-start.3 = (s32[1,16,32]{2,1,0:T(8,128)S(1)}, s32[1,16,32]{2,1,0:T(8,128)}, u32[]{:S(2)}) copy-start(s32[1,16,32]{2,1,0:T(8,128)} %param.17) | copy-start | bytes 6148
Sparse Core Ops, SparseCore 0:
  26.2 145.2 all-reduce.2
  175.8 170.3 reduce-scatter.1
  348.8 49.3 all-reduce.4

commit v3 on v2

--- a/solution.py
+++ b/solution.py
@@ -16,8 +16,6 @@
 CAP = 4
 REC = 32
 DOC_GRP = 32
-MODE = 2
-SQ_ROWS = 128
 
 
 eps_norm = 1e-05
@@ -110,6 +108,15 @@
     )(q2d, blocks, blocks, own_self, own_self)
 
 
+def pair_sum(value, axis):
+    size = lax.axis_size(axis)
+    step = 1
+    while step < size:
+        value = value + lax.ppermute(value, axis, [(i, i ^ step) for i in range(size)])
+        step *= 2
+    return value
+
+
 def shards(queries, store_kv, self_kv, rec_states, norm_gain, w_kv, retrieval, doc_home, rec_index):
     groups = lax.axis_size("cache")
     members = lax.axis_size("dh") * lax.axis_size("dq")
@@ -146,18 +153,13 @@
     states = rec_states[0].astype(jnp.float32)
     rows_rec = states.shape[0]
     partial_sq = jnp.sum(states * states, axis=1)
-    if MODE == 0:
-        total_sq = lax.psum(partial_sq, ("dh", "dq"))
-    elif MODE == 1:
-        total_sq = lax.psum(lax.psum(partial_sq, "dq"), "dh")
-    else:
-        total_sq = lax.psum(jnp.broadcast_to(partial_sq[None, :], (SQ_ROWS, rows_rec)), ("dh", "dq"))[0]
+    total_sq = pair_sum(pair_sum(partial_sq, "dq"), "dh")
     inv_rms = lax.rsqrt(total_sq / D + eps_norm)
     normed = (states * norm_gain.astype(jnp.float32)[None, :] * inv_rms[:, None]).astype(jnp.bfloat16)
     partial_kv = jnp.dot(normed, w_kv, preferred_element_type=jnp.float32)
     by_head = jnp.transpose(partial_kv.reshape(rows_rec, 2, KVH, HD), (2, 0, 1, 3)).reshape(KVH, rows_rec, 2 * HD)
-    head_sum = lax.psum_scatter(by_head, "dh", scatter_dimension=0, tiled=True)[0]
-    redone = lax.psum(head_sum, "dq")
+    head_parts = lax.all_to_all(by_head, "dh", split_axis=0, concat_axis=0, tiled=True)
+    redone = pair_sum(jnp.sum(head_parts, axis=0), "dq")
     own_rows = redone.reshape(RET, REC, 2 * HD)
     full_block = fetched.shape[1]
     positions = rec_index[0]

time: 479 us -> 362 us (0.76)
  waiting for transfers between devices: 332 us -> 205 us
  starting transfers between devices: 12.3 us -> 36.6 us
  between operations: 13.3 us -> 0.19 us
    psum x2 -> x0, waiting for transfers between devices: 180 us -> none  [the longest x1 147 us: shards(): lax.psum(jnp.broadcast_to(partial_sq[None, :], (SQ_ROWS, rows_rec)), ('dh...]
    reduce_scatter x1 -> x0, waiting for transfers between devices: 153 us -> none  [shards(): lax.psum_scatter(by_head, 'dh', scatter_dimension=0, tiled=True)[0]]
    ppermute x0 -> x7, waiting for transfers between devices: none -> 122 us  [pair_sum(): lax.ppermute(value, axis, [(i, i ^ step) for i in range(size)])]
    all_to_all x0 -> x1, waiting for transfers between devices: none -> 82.5 us  [shards(): lax.all_to_all(by_head, 'dh', split_axis=0, concat_axis=0, tiled=True)]
    ppermute x0 -> x7, starting transfers between devices: none -> 15.4 us  [pair_sum(): lax.ppermute(value, axis, [(i, i ^ step) for i in range(size)])]
    all_to_all x0 -> x1, starting transfers between devices: none -> 9.42 us  [shards(): lax.all_to_all(by_head, 'dh', split_axis=0, concat_axis=0, tiled=True)]
  transfers between devices with their start and end apart: 5 -> 10, of which waited for: 3 -> 8; matrix products, arithmetic and copies ran while one was open for 8% -> 9% of each run, Pallas kernels for 0% -> 0%
where the time goes in v3:
time: 362 us; the launch traced here: 358 us
  waiting for transfers between devices  205 us (57%)
  Pallas kernels  64.7 us (18%)
  starting transfers between devices  36.6 us (10%)
  local copies, waits for them, and re-layouts  29.4 us (8%)
  other arithmetic  15.1 us (4%)
  matrix products  7.26 us (2%)
    ppermute x7, waiting for transfers between devices, pair_sum(): lax.ppermute(value, axis, [(i, i ^ step) for i in range(size)])  122 us
    all_to_all x1, waiting for transfers between devices, shards(): lax.all_to_all(by_head, 'dh', split_axis=0, concat_axis=0, tiled=True)  82.5 us
    pallas_call x1, Pallas kernels, attention(): pl.pallas_call(kern, grid=(heads, 2, n_doc + n_self), in_specs=[pl.BlockS...  64.7 us
    ppermute x7, starting transfers between devices, pair_sum(): lax.ppermute(value, axis, [(i, i ^ step) for i in range(size)])  15.4 us
    all_to_all x1, starting transfers between devices, shards(): lax.all_to_all(by_head, 'dh', split_axis=0, concat_axis=0, tiled=True)  9.42 us
  transfers between devices with their start and end apart: 10, of which 8 were waited for; matrix products, arithmetic and copies ran while one was open for 9% of the time, Pallas kernels for 0%

profile of v3, /device:TPU:16, one launch (start us, length us, event | category | flops | bytes accessed | tf_op | source)
XLA Modules:
  0.0 358.0 jit_solution(6590131331850932964)
XLA Ops:
  0.9 1.6 gather_fusion
  3.7 2.0 gather_fusion.1
  5.7 3.3 select_select_fusion
  9.0 6.4 %all-to-all-start.1 = ((bf16[8,4,16,2048]{3,2,1,0:T(8,128)(2,1)}), bf16[8,4,16,2048]{3,2,1,0:T(8,128)(2,1)}, u32[]{:S(2)}, u32[]{:S(2)}) async-start(bf16[8,4,16,2048]{3,2,1,0:T(8,128)(2,1)} %select_select_fusion), calls=%async_computation.1 | async-start | bytes 4194304 | tf_op jit(solution)/shard_map/all_to_all | solution.py:149
  16.1 3.2 collective-permute-done
  19.3 1.8 collective-permute-start.1
  21.1 2.7 collective-permute-done.1
  23.8 5.7 %collective-permute-start.2 = (f32[512]{0:T(512)S(1)}, f32[512]{0:T(512)S(1)}, u32[]{:S(2)}, u32[]{:S(2)}) collective-permute-start(f32[512]{0:T(512)S(1)} %add.145), channel_id=1, source_target_pairs={{0,4},{4,0},{8,12},{12,8},{16,20},{20,16},{24,28},{28,24},{1,5},{5... | collective-permute-start | bytes 6152 | tf_op jit(solution)/shard_map/ppermute | solution.py:115
  29.5 1.8 collective-permute-done.2
  31.3 1.2 collective-permute-start.3
  32.5 2.3 collective-permute-done.3
  34.9 2.8 collective-permute-start.4
  37.6 1.5 copy.46
  40.8 2.7 copy.36
  43.5 9.4 %all-to-all-start = ((f32[8,512,256]{1,2,0:T(8,128)}), f32[8,512,256]{1,2,0:T(8,128)}, u32[]{:S(2)}, u32[]{:S(2)}) async-start(f32[8,512,256]{1,2,0:T(8,128)} %bitcast.51), calls=%async_computation | async-start | bytes 8388608 | tf_op jit(solution)/shard_map/all_to_all | solution.py:161
  53.0 2.2 gather_fusion.2
  55.7 3.4 gather_fusion.3
  59.0 5.6 %copy_bitcast_fusion = bf16[32,16,16,256]{3,2,1,0:T(8,128)(2,1)} fusion(bf16[32,16,16,2,128]{4,2,3,1,0:T(8,128)(2,1)} %gather_fusion.3, pred[32]{0:T(512)(128)(4,1)S(1)} %compare_and_fusion.2), kind=kLoop, calls=%fused_computation.4 | loop fusion | flops 2097152 | bytes 8388640 | tf_op jit(solution)/shard_map/reshape | solution.py:35
  64.6 82.5 %all-to-all-done = f32[8,512,256]{1,2,0:T(8,128)} async-done(((f32[8,512,256]{1,2,0:T(8,128)}), f32[8,512,256]{1,2,0:T(8,128)}, u32[]{:S(2)}, u32[]{:S(2)}) %all-to-all-start) | async-done | bytes 4194336 | tf_op jit(solution)/shard_map/all_to_all | solution.py:161
  147.1 5.3 %all-to-all-start.2 = ((bf16[32,16,16,256]{3,2,1,0:T(8,128)(2,1)}), bf16[32,16,16,256]{3,2,1,0:T(8,128)(2,1)}, u32[]{:S(2)}, u32[]{:S(2)}) async-start(bf16[32,16,16,256]{3,2,1,0:T(8,128)(2,1)} %copy_bitcast_fusion), calls=%async_computation.2 | async-start | bytes 8388608 | tf_op jit(solution)/shard_map/all_to_all | solution.py:152
  152.5 2.7 reduce_sum.37
  155.2 2.5 collective-permute-start.5
  157.7 98.9 %collective-permute-done.5 = f32[512,256]{0,1:T(8,128)S(1)} collective-permute-done((f32[512,256]{0,1:T(8,128)S(1)}, f32[512,256]{0,1:T(8,128)S(1)}, u32[]{:S(2)}, u32[]{:S(2)}) %collective-permute-start.5) | collective-permute-done | bytes 524320 | tf_op jit(solution)/shard_map/ppermute | solution.py:115
  256.7 0.9 collective-permute-start.6
  257.6 5.6 %copy.50 = bf16[128,8,16,128]{3,2,1,0:T(8,128)(2,1)} copy(bf16[128,8,16,128]{3,1,2,0:T(8,128)(2,1)} %bitcast.59) | data formatting | bytes 8388608
  263.2 5.9 %dynamic-slice_reduce_fusion = bf16[1024,2,128]{2,1,0:T(2,128)(2,1)S(1)} fusion(bf16[1024,2,8,128]{3,2,1,0:T(8,128)(2,1)} %bitcast.54, s32[]{:T(128)S(6)} %select_n.160), kind=kLoop, calls=%fused_computation.10 | loop fusion | bytes 1048580 | tf_op jit(solution)/shard_map/jit(dynamic_index_in_dim)/dynamic_slice | solution.py:27
  269.1 0.9 copy.55
  270.4 12.5 %collective-permute-done.6 = f32[512,256]{0,1:T(8,128)} collective-permute-done((f32[512,256]{0,1:T(8,128)S(1)}, f32[512,256]{0,1:T(8,128)}, u32[]{:S(2)}, u32[]{:S(2)}) %collective-permute-start.6) | collective-permute-done | bytes 524320 | tf_op jit(solution)/shard_map/ppermute | solution.py:115
  282.9 1.1 add.152
  284.3 2.6 copy.43
  286.9 6.4 %convert_select_fusion.kd_ref.vd_ref = bf16[16,512,256]{2,1,0:T(8,128)(2,1)} fusion(bf16[16,512,256]{2,1,0:T(8,128)(2,1)S(1)} %bitcast.52, pred[16,512]{1,0:T(8,128)(4,1)S(1)} %fusion, f32[16,32,256]{2,1,0:T(8,128)S(1)} %bitcast.61, s32[16,32]{1,0:T(8,128)S(1)} %bitcast.66), kind=kOutput, calls=%fused_computation.6 | convolution fusion | flops 809762816 | bytes 8923136 | tf_op jit(solution)/shard_map/kib,kic->kbc/dot_general | solution.py:167
  293.3 64.7 %shard_map.91 = bf16[1024,256]{1,0:T(8,128)(2,1)} custom-call(bf16[1024,256]{1,0:T(8,128)(2,1)} %bitcast.64, bf16[16,512,256]{2,1,0:T(8,128)(2,1)} %convert_select_fusion.kd_ref.vd_ref, bf16[16,512,256]{2,1,0:T(8,128)(2,1)} %convert_select_fusion.kd_ref.vd_ref, bf16[1024,256]{1,0:T(8,128)(2,1)} %bitcast.55, bf16[1024,256]{1,0:T(8,128)(2,1)} %bitcast.56), custom_call_target="tpu_custom_call" | custom-call | tf_op jit(solution)/shard_map/pallas_call | solution.py:95
  (49 shorter events, 5.5 us)
Async XLA Ops:
  0.0 3.7 %copy-start = (bf16[32,16,2048]{2,1,0:T(8,128)(2,1)S(1)}, bf16[32,16,2048]{2,1,0:T(8,128)(2,1)}, u32[]{:S(2)}) copy-start(bf16[32,16,2048]{2,1,0:T(8,128)(2,1)} %param.10) | copy-start | bytes 6291460
  0.0 2.7 copy-start.2
  5.7 9.7 %copy-start.1 = (bf16[1,512,256]{2,1,0:T(8,128)(2,1)S(1)}, bf16[1,512,256]{2,1,0:T(8,128)(2,1)}, u32[]{:S(2)}) copy-start(bf16[1,512,256]{2,1,0:T(8,128)(2,1)} %param.12) | copy-start | bytes 786436
  9.0 30.1 %copy-start.4 = (bf16[256]{0:T(256)(128)(2,1)S(1)}, bf16[256]{0:T(256)(128)(2,1)}, u32[]{:S(2)}) copy-start(bf16[256]{0:T(256)(128)(2,1)} %param.13) | copy-start | bytes 1540
  9.0 34.4 %all-to-all-start.1 = ((bf16[8,4,16,2048]{3,2,1,0:T(8,128)(2,1)}), bf16[8,4,16,2048]{3,2,1,0:T(8,128)(2,1)}, u32[]{:S(2)}, u32[]{:S(2)}) async-start(bf16[8,4,16,2048]{3,2,1,0:T(8,128)(2,1)} %select_select_fusion), calls=%async_computation.1 | async-start | bytes 4194304 | tf_op jit(solution)/shard_map/all_to_all | solution.py:149
  15.6 3.7 %collective-permute-start = (f32[512]{0:T(512)S(1)}, f32[512]{0:T(512)S(1)}, u32[]{:S(2)}, u32[]{:S(2)}) collective-permute-start(f32[512]{0:T(512)S(1)} %fusion.3), channel_id=1, source_target_pairs={{0,1},{1,0},{2,3},{3,2},{4,5},{5,4},{6,7},{7,6},{8,9},{9,8},{10,11... | collective-permute-start | bytes 6152 | tf_op jit(solution)/shard_map/ppermute | solution.py:115
  19.3 4.5 %collective-permute-start.1 = (f32[512]{0:T(512)S(1)}, f32[512]{0:T(512)S(1)}, u32[]{:S(2)}, u32[]{:S(2)}) collective-permute-start(f32[512]{0:T(512)S(1)} %add.144), channel_id=1, source_target_pairs={{0,2},{1,3},{2,0},{3,1},{4,6},{5,7},{6,4},{7,5},{8,10},{9,11},{10,... | collective-permute-start | bytes 6152 | tf_op jit(solution)/shard_map/ppermute | solution.py:115
  23.8 7.5 %collective-permute-start.2 = (f32[512]{0:T(512)S(1)}, f32[512]{0:T(512)S(1)}, u32[]{:S(2)}, u32[]{:S(2)}) collective-permute-start(f32[512]{0:T(512)S(1)} %add.145), channel_id=1, source_target_pairs={{0,4},{4,0},{8,12},{12,8},{16,20},{20,16},{24,28},{28,24},{1,5},{5... | collective-permute-start | bytes 6152 | tf_op jit(solution)/shard_map/ppermute | solution.py:115
  31.3 3.6 %collective-permute-start.3 = (f32[512]{0:T(512)S(1)}, f32[512]{0:T(512)S(1)}, u32[]{:S(2)}, u32[]{:S(2)}) collective-permute-start(f32[512]{0:T(512)S(1)} %add.146), channel_id=1, source_target_pairs={{0,8},{4,12},{8,0},{12,4},{16,24},{20,28},{24,16},{28,20},{1,9},{5... | collective-permute-start | bytes 6152 | tf_op jit(solution)/shard_map/ppermute | solution.py:115
  34.9 5.1 %collective-permute-start.4 = (f32[512]{0:T(512)S(1)}, f32[512]{0:T(512)S(1)}, u32[]{:S(2)}, u32[]{:S(2)}) collective-permute-start(f32[512]{0:T(512)S(1)} %add.147), channel_id=1, source_target_pairs={{0,16},{4,20},{8,24},{12,28},{16,0},{20,4},{24,8},{28,12},{1,17},{... | collective-permute-start | bytes 6152 | tf_op jit(solution)/shard_map/ppermute | solution.py:115
  43.5 103.7 %all-to-all-start = ((f32[8,512,256]{1,2,0:T(8,128)}), f32[8,512,256]{1,2,0:T(8,128)}, u32[]{:S(2)}, u32[]{:S(2)}) async-start(f32[8,512,256]{1,2,0:T(8,128)} %bitcast.51), calls=%async_computation | async-start | bytes 8388608 | tf_op jit(solution)/shard_map/all_to_all | solution.py:161
  147.1 137.1 %all-to-all-start.2 = ((bf16[32,16,16,256]{3,2,1,0:T(8,128)(2,1)}), bf16[32,16,16,256]{3,2,1,0:T(8,128)(2,1)}, u32[]{:S(2)}, u32[]{:S(2)}) async-start(bf16[32,16,16,256]{3,2,1,0:T(8,128)(2,1)} %copy_bitcast_fusion), calls=%async_computation.2 | async-start | bytes 8388608 | tf_op jit(solution)/shard_map/all_to_all | solution.py:152
  155.2 101.4 %collective-permute-start.5 = (f32[512,256]{0,1:T(8,128)S(1)}, f32[512,256]{0,1:T(8,128)S(1)}, u32[]{:S(2)}, u32[]{:S(2)}) collective-permute-start(f32[512,256]{0,1:T(8,128)S(1)} %reduce_sum.37), channel_id=1, source_target_pairs={{0,1},{1,0},{2,3},{3,2},{4,5},{5,4},{6,7},{7,6},{8,9},{9,8},{10,11... | collective-permute-start | bytes 1572872 | tf_op jit(solution)/shard_map/ppermute | solution.py:115
  256.7 26.2 %collective-permute-start.6 = (f32[512,256]{0,1:T(8,128)S(1)}, f32[512,256]{0,1:T(8,128)}, u32[]{:S(2)}, u32[]{:S(2)}) collective-permute-start(f32[512,256]{0,1:T(8,128)S(1)} %add.151), channel_id=1, source_target_pairs={{0,2},{1,3},{2,0},{3,1},{4,6},{5,7},{6,4},{7,5},{8,10},{9,11},{10,... | collective-permute-start | bytes 1572872 | tf_op jit(solution)/shard_map/ppermute | solution.py:115
  257.6 12.4 %copy-start.3 = (s32[1,16,32]{2,1,0:T(8,128)S(1)}, s32[1,16,32]{2,1,0:T(8,128)}, u32[]{:S(2)}) copy-start(s32[1,16,32]{2,1,0:T(8,128)} %param.17) | copy-start | bytes 6148

commit v4 on v3

--- a/solution.py
+++ b/solution.py
@@ -114,6 +114,34 @@
     while step < size:
         value = value + lax.ppermute(value, axis, [(i, i ^ step) for i in range(size)])
         step *= 2
+    return value
+
+
+def halve_sum(value, axis):
+    size = lax.axis_size(axis)
+    me = lax.axis_index(axis)
+    step = 1
+    while step < size:
+        bit = (me // step) % 2
+        halves = value.reshape((2, value.shape[0] // 2) + value.shape[1:])
+        keep = lax.dynamic_index_in_dim(halves, bit, 0, keepdims=False)
+        send = lax.dynamic_index_in_dim(halves, 1 - bit, 0, keepdims=False)
+        value = keep + lax.ppermute(send, axis, [(i, i ^ step) for i in range(size)])
+        step *= 2
+    return value
+
+
+def double_gather(value, axis):
+    size = lax.axis_size(axis)
+    me = lax.axis_index(axis)
+    step = size // 2
+    while step >= 1:
+        bit = (me // step) % 2
+        other = lax.ppermute(value, axis, [(i, i ^ step) for i in range(size)])
+        value = jnp.where(
+            bit == 0, jnp.concatenate([value, other], axis=0), jnp.concatenate([other, value], axis=0)
+        )
+        step //= 2
     return value
 
 
@@ -157,15 +185,18 @@
     inv_rms = lax.rsqrt(total_sq / D + eps_norm)
     normed = (states * norm_gain.astype(jnp.float32)[None, :] * inv_rms[:, None]).astype(jnp.bfloat16)
     partial_kv = jnp.dot(normed, w_kv, preferred_element_type=jnp.float32)
-    by_head = jnp.transpose(partial_kv.reshape(rows_rec, 2, KVH, HD), (2, 0, 1, 3)).reshape(KVH, rows_rec, 2 * HD)
+    row_part = halve_sum(partial_kv, "dq")
+    part_rows = row_part.shape[0]
+    by_head = jnp.transpose(row_part.reshape(part_rows, 2, KVH, HD), (2, 0, 1, 3))
     head_parts = lax.all_to_all(by_head, "dh", split_axis=0, concat_axis=0, tiled=True)
-    redone = pair_sum(jnp.sum(head_parts, axis=0), "dq")
+    head_rows = jnp.sum(head_parts, axis=0).reshape(part_rows, 2 * HD).astype(jnp.bfloat16)
+    redone = double_gather(head_rows, "dq")
     own_rows = redone.reshape(RET, REC, 2 * HD)
     full_block = fetched.shape[1]
     positions = rec_index[0]
     onehot = positions[:, :, None] == jnp.arange(full_block, dtype=jnp.int32)[None, None, :]
     placed = jnp.einsum(
-        "kib,kic->kbc", onehot.astype(jnp.float32), own_rows, precision=lax.Precision.HIGHEST
+        "kib,kic->kbc", onehot.astype(jnp.bfloat16), own_rows, preferred_element_type=jnp.float32
     ).astype(jnp.bfloat16)
     replaced_at = jnp.any(onehot, axis=1)
     blocks = jnp.where(replaced_at[:, :, None], placed, fetched)

time: 362 us -> 344 us (0.950)
  waiting for transfers between devices: 205 us -> 177 us
  starting transfers between devices: 36.6 us -> 41.8 us
    ppermute x0 -> x4, waiting for transfers between devices: none -> 154 us  [the longest x2 83.9 us: double_gather(): other = lax.ppermute(value, axis, [(i, i ^ step) for i in range(size)])]
    ppermute x7 -> x5, waiting for transfers between devices: 122 us -> 7.53 us  [pair_sum(): lax.ppermute(value, axis, [(i, i ^ step) for i in range(size)])]
    all_to_all x1, waiting for transfers between devices: 82.5 us -> 16 us  [shards(): lax.all_to_all(by_head, 'dh', split_axis=0, concat_axis=0, tiled=True)]
    ppermute x0 -> x4, starting transfers between devices: none -> 6.11 us  [the longest x2 3.09 us: double_gather(): other = lax.ppermute(value, axis, [(i, i ^ step) for i in range(size)])]
    add x0 -> x2, other arithmetic: none -> 4.13 us  [halve_sum(): keep + lax.ppermute(send, axis, [(i, i ^ step) for i in range(size)])]
    unnamed x13 -> x16, local copies, waits for them, and re-layouts: 6.77 us -> 10 us
    ppermute x7 -> x5, starting transfers between devices: 15.4 us -> 16.6 us  [pair_sum(): lax.ppermute(value, axis, [(i, i ^ step) for i in range(size)])]
  transfers between devices with their start and end apart: 10 -> 12, of which waited for: 8 -> 9; matrix products, arithmetic and copies ran while one was open for 9% -> 13% of each run, Pallas kernels for 0% -> 0%
where the time goes in v4:
time: 344 us; the launch traced here: 342 us
  waiting for transfers between devices  177 us (51%)
  Pallas kernels  64.7 us (19%)
  starting transfers between devices  41.8 us (12%)
  local copies, waits for them, and re-layouts  33 us (10%)
  other arithmetic  18.6 us (5%)
  matrix products  6.29 us (2%)
    ppermute x2, waiting for transfers between devices, double_gather(): other = lax.ppermute(value, axis, [(i, i ^ step) for i in range(size)])  83.9 us
    ppermute x2, waiting for transfers between devices, halve_sum(): lax.ppermute(send, axis, [(i, i ^ step) for i in range(size)])  69.8 us
    pallas_call x1, Pallas kernels, attention(): pl.pallas_call(kern, grid=(heads, 2, n_doc + n_self), in_specs=[pl.BlockS...  64.7 us
    ppermute x5, starting transfers between devices, pair_sum(): lax.ppermute(value, axis, [(i, i ^ step) for i in range(size)])  16.6 us
    all_to_all x1, waiting for transfers between devices, shards(): lax.all_to_all(by_head, 'dh', split_axis=0, concat_axis=0, tiled=True)  16 us
    unnamed x16, local copies, waits for them, and re-layouts  10 us
    all_to_all x1, starting transfers between devices, shards(): lax.all_to_all(by_head, 'dh', split_axis=0, concat_axis=0, tiled=True)  8.62 us
    ppermute x5, waiting for transfers between devices, pair_sum(): lax.ppermute(value, axis, [(i, i ^ step) for i in range(size)])  7.53 us
  transfers between devices with their start and end apart: 12, of which 9 were waited for; matrix products, arithmetic and copies ran while one was open for 13% of the time, Pallas kernels for 0%

profile of v4, /device:TPU:16, one launch (start us, length us, event | category | flops | bytes accessed | tf_op | source)
XLA Modules:
  0.0 341.9 jit_solution(5817691887485270163)
XLA Ops:
  1.3 2.0 collective-permute-start
  3.3 1.7 collective-permute-done
  4.9 3.3 collective-permute-start.1
  8.2 1.6 collective-permute-done.1
  9.8 6.8 %collective-permute-start.2 = (f32[512]{0:T(512)S(1)}, f32[512]{0:T(512)S(1)}, u32[]{:S(2)}, u32[]{:S(2)}) collective-permute-start(f32[512]{0:T(512)S(1)} %add.174), channel_id=1, source_target_pairs={{0,4},{4,0},{8,12},{12,8},{16,20},{20,16},{24,28},{28,24},{1,5},{5... | collective-permute-start | bytes 6152 | tf_op jit(solution)/shard_map/ppermute | solution.py:115
  19.7 2.1 collective-permute-done.3
  21.8 3.0 collective-permute-start.4
  26.9 2.1 fusion
  29.0 1.9 copy-done.2
  35.8 2.0 gather_fusion.1
  37.8 3.3 select_select_fusion
  41.1 4.8 %all-to-all-start.1 = ((bf16[8,4,16,2048]{3,2,1,0:T(8,128)(2,1)}), bf16[8,4,16,2048]{3,2,1,0:T(8,128)(2,1)}, u32[]{:S(2)}, u32[]{:S(2)}) async-start(bf16[8,4,16,2048]{3,2,1,0:T(8,128)(2,1)} %select_select_fusion), calls=%async_computation.1 | async-start | bytes 4194304 | tf_op jit(solution)/shard_map/all_to_all | solution.py:177
  45.9 29.2 %collective-permute-done.5 = f32[256,2048]{1,0:T(8,128)} collective-permute-done((f32[256,2048]{1,0:T(8,128)}, f32[256,2048]{1,0:T(8,128)}, u32[]{:S(2)}, u32[]{:S(2)}) %collective-permute-start.5) | collective-permute-done | bytes 2097184 | tf_op jit(solution)/shard_map/ppermute | solution.py:129
  75.1 2.5 bitcast_add_fusion
  79.0 2.0 collective-permute-start.6
  81.0 40.6 %collective-permute-done.6 = f32[128,2048]{1,0:T(8,128)} collective-permute-done((f32[128,2048]{1,0:T(8,128)S(1)}, f32[128,2048]{1,0:T(8,128)}, u32[]{:S(2)}, u32[]{:S(2)}) %collective-permute-start.6) | collective-permute-done | bytes 1048608 | tf_op jit(solution)/shard_map/ppermute | solution.py:129
  121.6 1.7 bitcast_add_fusion.1
  124.6 2.3 copy.37
  126.9 8.6 %all-to-all-start = ((f32[8,128,2,128]{3,2,1,0:T(2,128)}), f32[8,128,2,128]{3,2,1,0:T(2,128)}, u32[]{:S(2)}, u32[]{:S(2)}) async-start(f32[8,128,2,128]{3,2,1,0:T(2,128)} %copy.37), calls=%async_computation | async-start | bytes 2097152 | tf_op jit(solution)/shard_map/all_to_all | solution.py:191
  135.6 2.2 gather_fusion.2
  138.3 3.4 gather_fusion.3
  141.7 5.6 %copy_bitcast_fusion = bf16[32,16,16,256]{3,2,1,0:T(8,128)(2,1)} fusion(bf16[32,16,16,2,128]{4,2,3,1,0:T(8,128)(2,1)} %gather_fusion.3, pred[32]{0:T(512)(128)(4,1)S(1)} %compare_and_fusion.2), kind=kLoop, calls=%fused_computation.4 | loop fusion | flops 2097152 | bytes 8388640 | tf_op jit(solution)/shard_map/reshape | solution.py:35
  147.3 16.0 %all-to-all-done = f32[8,128,2,128]{3,2,1,0:T(2,128)} async-done(((f32[8,128,2,128]{3,2,1,0:T(2,128)}), f32[8,128,2,128]{3,2,1,0:T(2,128)}, u32[]{:S(2)}, u32[]{:S(2)}) %all-to-all-start) | async-done | bytes 1048608 | tf_op jit(solution)/shard_map/all_to_all | solution.py:191
  163.3 5.6 %all-to-all-start.2 = ((bf16[32,16,16,256]{3,2,1,0:T(8,128)(2,1)}), bf16[32,16,16,256]{3,2,1,0:T(8,128)(2,1)}, u32[]{:S(2)}, u32[]{:S(2)}) async-start(bf16[32,16,16,256]{3,2,1,0:T(8,128)(2,1)} %copy_bitcast_fusion), calls=%async_computation.2 | async-start | bytes 8388608 | tf_op jit(solution)/shard_map/all_to_all | solution.py:180
  168.9 1.6 reduce_sum.37
  170.5 2.9 collective-permute-start.7
  173.4 5.6 %copy.49 = bf16[128,8,16,128]{3,2,1,0:T(8,128)(2,1)} copy(bf16[128,8,16,128]{3,1,2,0:T(8,128)(2,1)} %bitcast.68) | data formatting | bytes 8388608
  179.0 83.9 %collective-permute-done.7 = bf16[128,256]{1,0:T(8,128)(2,1)S(1)} collective-permute-done((bf16[128,256]{1,0:T(8,128)(2,1)S(1)}, bf16[128,256]{1,0:T(8,128)(2,1)S(1)}, u32[]{:S(2)}, u32[]{:S(2)}) %collective-permute-start.7) | collective-permute-done | bytes 65568 | tf_op jit(solution)/shard_map/ppermute | solution.py:140
  263.1 5.9 %dynamic-slice_reduce_fusion = bf16[1024,2,128]{2,1,0:T(2,128)(2,1)S(1)} fusion(bf16[1024,2,8,128]{3,2,1,0:T(8,128)(2,1)} %bitcast.63, s32[]{:T(128)S(6)} %select_n.226), kind=kLoop, calls=%fused_computation.14 | loop fusion | bytes 1048580 | tf_op jit(solution)/shard_map/jit(dynamic_index_in_dim)/dynamic_slice | solution.py:27
  270.4 2.6 copy.43
  273.1 4.2 %convert_select_fusion.kd_ref.vd_ref = bf16[16,512,256]{2,1,0:T(8,128)(2,1)} fusion(bf16[16,512,256]{2,1,0:T(8,128)(2,1)S(1)} %bitcast.59, pred[16,512]{1,0:T(8,128)(4,1)S(1)} %fusion.2, bf16[16,32,256]{2,1,0:T(8,128)(2,1)S(1)} %bitcast.71, s32[16,32]{1,0:T(8,128)S(1)} %bitcast.78), kind=kOutput, calls=%fused_computation.6 | convolution fusion | flops 138674176 | bytes 8660992 | tf_op jit(solution)/shard_map/kib,kic->kbc/dot_general | solution.py:198
  277.3 64.7 %shard_map.91 = bf16[1024,256]{1,0:T(8,128)(2,1)} custom-call(bf16[1024,256]{1,0:T(8,128)(2,1)} %bitcast.73, bf16[16,512,256]{2,1,0:T(8,128)(2,1)} %convert_select_fusion.kd_ref.vd_ref, bf16[16,512,256]{2,1,0:T(8,128)(2,1)} %convert_select_fusion.kd_ref.vd_ref, bf16[1024,256]{1,0:T(8,128)(2,1)} %bitcast.64, bf16[1024,256]{1,0:T(8,128)(2,1)} %bitcast.65), custom_call_target="tpu_custom_call" | custom-call | tf_op jit(solution)/shard_map/pallas_call | solution.py:95
  (60 shorter events, 16.1 us)
Async XLA Ops:
  0.0 35.8 %copy-start = (bf16[32,16,2048]{2,1,0:T(8,128)(2,1)S(1)}, bf16[32,16,2048]{2,1,0:T(8,128)(2,1)}, u32[]{:S(2)}) copy-start(bf16[32,16,2048]{2,1,0:T(8,128)(2,1)} %param.10) | copy-start | bytes 6291460
  1.3 3.7 %collective-permute-start = (f32[512]{0:T(512)S(1)}, f32[512]{0:T(512)S(1)}, u32[]{:S(2)}, u32[]{:S(2)}) collective-permute-start(f32[512]{0:T(512)S(1)} %multiply_reduce_fusion), channel_id=1, source_target_pairs={{0,1},{1,0},{2,3},{3,2},{4,5},{5,4},{6,7},{7,6},{8,9},{9,8},{10,11... | collective-permute-start | bytes 6152 | tf_op jit(solution)/shard_map/ppermute | solution.py:115
  4.9 4.8 %collective-permute-start.1 = (f32[512]{0:T(512)S(1)}, f32[512]{0:T(512)S(1)}, u32[]{:S(2)}, u32[]{:S(2)}) collective-permute-start(f32[512]{0:T(512)S(1)} %add.173), channel_id=1, source_target_pairs={{0,2},{1,3},{2,0},{3,1},{4,6},{5,7},{6,4},{7,5},{8,10},{9,11},{10,... | collective-permute-start | bytes 6152 | tf_op jit(solution)/shard_map/ppermute | solution.py:115
  9.8 8.4 %collective-permute-start.2 = (f32[512]{0:T(512)S(1)}, f32[512]{0:T(512)S(1)}, u32[]{:S(2)}, u32[]{:S(2)}) collective-permute-start(f32[512]{0:T(512)S(1)} %add.174), channel_id=1, source_target_pairs={{0,4},{4,0},{8,12},{12,8},{16,20},{20,16},{24,28},{28,24},{1,5},{5... | collective-permute-start | bytes 6152 | tf_op jit(solution)/shard_map/ppermute | solution.py:115
  18.2 3.6 %collective-permute-start.3 = (f32[512]{0:T(512)S(1)}, f32[512]{0:T(512)S(1)}, u32[]{:S(2)}, u32[]{:S(2)}) collective-permute-start(f32[512]{0:T(512)S(1)} %add.175), channel_id=1, source_target_pairs={{0,8},{4,12},{8,0},{12,4},{16,24},{20,28},{24,16},{28,20},{1,9},{5... | collective-permute-start | bytes 6152 | tf_op jit(solution)/shard_map/ppermute | solution.py:115
  21.8 5.1 %collective-permute-start.4 = (f32[512]{0:T(512)S(1)}, f32[512]{0:T(512)S(1)}, u32[]{:S(2)}, u32[]{:S(2)}) collective-permute-start(f32[512]{0:T(512)S(1)} %add.176), channel_id=1, source_target_pairs={{0,16},{4,20},{8,24},{12,28},{16,0},{20,4},{24,8},{28,12},{1,17},{... | collective-permute-start | bytes 6152 | tf_op jit(solution)/shard_map/ppermute | solution.py:115
  26.9 6.5 %copy-start.1 = (s32[256]{0:T(256)S(1)}, s32[256]{0:T(256)}, u32[]{:S(2)}) copy-start(s32[256]{0:T(256)} %param.16) | copy-start | bytes 3076
  29.0 1.9 copy-start.2
  30.9 3.8 %copy-start.4 = (s32[8,16]{1,0:T(8,128)S(1)}, s32[8,16]{1,0:T(8,128)}, u32[]{:S(2)}) copy-start(s32[8,16]{1,0:T(8,128)} %param.15) | copy-start | bytes 1540
  32.4 42.8 %collective-permute-start.5 = (f32[256,2048]{1,0:T(8,128)}, f32[256,2048]{1,0:T(8,128)}, u32[]{:S(2)}, u32[]{:S(2)}) collective-permute-start(f32[256,2048]{1,0:T(8,128)} %dynamic-slice_bitcast_fusion), channel_id=1, source_target_pairs={{0,1},{1,0},{2,3},{3,2},{4,5},{5,4},{6,7},{7,6},{8,9},{9,8},{10,11... | collective-permute-start | bytes 6291464 | tf_op jit(solution)/shard_map/ppermute | solution.py:129
  41.1 85.8 %all-to-all-start.1 = ((bf16[8,4,16,2048]{3,2,1,0:T(8,128)(2,1)}), bf16[8,4,16,2048]{3,2,1,0:T(8,128)(2,1)}, u32[]{:S(2)}, u32[]{:S(2)}) async-start(bf16[8,4,16,2048]{3,2,1,0:T(8,128)(2,1)} %select_select_fusion), calls=%async_computation.1 | async-start | bytes 4194304 | tf_op jit(solution)/shard_map/all_to_all | solution.py:177
  77.6 1.3 copy-start.3
  79.0 42.6 %collective-permute-start.6 = (f32[128,2048]{1,0:T(8,128)S(1)}, f32[128,2048]{1,0:T(8,128)}, u32[]{:S(2)}, u32[]{:S(2)}) collective-permute-start(f32[128,2048]{1,0:T(8,128)S(1)} %dynamic-slice_bitcast_fusion.1), channel_id=1, source_target_pairs={{0,2},{1,3},{2,0},{3,1},{4,6},{5,7},{6,4},{7,5},{8,10},{9,11},{10,... | collective-permute-start | bytes 3145736 | tf_op jit(solution)/shard_map/ppermute | solution.py:129
  126.9 36.4 %all-to-all-start = ((f32[8,128,2,128]{3,2,1,0:T(2,128)}), f32[8,128,2,128]{3,2,1,0:T(2,128)}, u32[]{:S(2)}, u32[]{:S(2)}) async-start(f32[8,128,2,128]{3,2,1,0:T(2,128)} %copy.37), calls=%async_computation | async-start | bytes 2097152 | tf_op jit(solution)/shard_map/all_to_all | solution.py:191
  163.3 107.1 %all-to-all-start.2 = ((bf16[32,16,16,256]{3,2,1,0:T(8,128)(2,1)}), bf16[32,16,16,256]{3,2,1,0:T(8,128)(2,1)}, u32[]{:S(2)}, u32[]{:S(2)}) async-start(bf16[32,16,16,256]{3,2,1,0:T(8,128)(2,1)} %copy_bitcast_fusion), calls=%async_computation.2 | async-start | bytes 8388608 | tf_op jit(solution)/shard_map/all_to_all | solution.py:180
  170.5 92.3 %collective-permute-start.7 = (bf16[128,256]{1,0:T(8,128)(2,1)S(1)}, bf16[128,256]{1,0:T(8,128)(2,1)S(1)}, u32[]{:S(2)}, u32[]{:S(2)}) collective-permute-start(bf16[128,256]{1,0:T(8,128)(2,1)S(1)} %bitcast.75), channel_id=1, source_target_pairs={{0,2},{1,3},{2,0},{3,1},{4,6},{5,7},{6,4},{7,5},{8,10},{9,11},{10,... | collective-permute-start | bytes 196616 | tf_op jit(solution)/shard_map/ppermute | solution.py:140
  173.4 96.6 %copy-start.5 = (s32[1,16,32]{2,1,0:T(8,128)S(1)}, s32[1,16,32]{2,1,0:T(8,128)}, u32[]{:S(2)}) copy-start(s32[1,16,32]{2,1,0:T(8,128)} %param.17) | copy-start | bytes 6148
  262.9 7.4 %collective-permute-start.8 = (bf16[256,256]{1,0:T(8,128)(2,1)S(1)}, bf16[256,256]{1,0:T(8,128)(2,1)S(1)}, u32[]{:S(2)}, u32[]{:S(2)}) collective-permute-start(bf16[256,256]{1,0:T(8,128)(2,1)S(1)} %maximum_select_fusion.1), channel_id=1, source_target_pairs={{0,1},{1,0},{2,3},{3,2},{4,5},{5,4},{6,7},{7,6},{8,9},{9,8},{10,11... | collective-permute-start | bytes 393224 | tf_op jit(solution)/shard_map/ppermute | solution.py:140

commit v5 on v4

--- a/solution.py
+++ b/solution.py
@@ -186,6 +186,7 @@
     normed = (states * norm_gain.astype(jnp.float32)[None, :] * inv_rms[:, None]).astype(jnp.bfloat16)
     partial_kv = jnp.dot(normed, w_kv, preferred_element_type=jnp.float32)
     row_part = halve_sum(partial_kv, "dq")
+    fetched, row_part = lax.optimization_barrier((fetched, row_part))
     part_rows = row_part.shape[0]
     by_head = jnp.transpose(row_part.reshape(part_rows, 2, KVH, HD), (2, 0, 1, 3))
     head_parts = lax.all_to_all(by_head, "dh", split_axis=0, concat_axis=0, tiled=True)

time: 344 us -> 404 us (1.17)
  blocking collectives: 0 us -> 37.4 us
  waiting for transfers between devices: 177 us -> 203 us
    ppermute x5, waiting for transfers between devices: 7.53 us -> 97.6 us  [pair_sum(): lax.ppermute(value, axis, [(i, i ^ step) for i in range(size)])]
    ppermute x2, waiting for transfers between devices: 83.9 us -> 0.01 us  [double_gather(): other = lax.ppermute(value, axis, [(i, i ^ step) for i in range(size)])]
    all_to_all x0 -> x1, blocking collectives: none -> 37.4 us  [shards(): lax.all_to_all(by_head, 'dh', split_axis=0, concat_axis=0, tiled=True)]
    all_to_all x1, waiting for transfers between devices: 0.01 us -> 24 us  [shards(): lax.all_to_all(outgoing, 'cache', split_axis=0, concat_axis=0, tiled=True)]
    all_to_all x1 -> x0, waiting for transfers between devices: 16 us -> none  [shards(): lax.all_to_all(by_head, 'dh', split_axis=0, concat_axis=0, tiled=True)]
    ppermute x2, waiting for transfers between devices: 69.8 us -> 81.8 us  [halve_sum(): lax.ppermute(send, axis, [(i, i ^ step) for i in range(size)])]
    all_to_all x1 -> x0, starting transfers between devices: 8.62 us -> none  [shards(): lax.all_to_all(by_head, 'dh', split_axis=0, concat_axis=0, tiled=True)]
    all_to_all x1, starting transfers between devices: 5.59 us -> 10.1 us  [shards(): lax.all_to_all(spread, ('dh', 'dq'), split_axis=0, concat_axis=2, tiled=T...]
  transfers between devices with their start and end apart: 12 -> 11, of which waited for: 9 -> 8; matrix products, arithmetic and copies ran while one was open for 13% -> 5% of each run, Pallas kernels for 0% -> 0%
where the time goes in v5:
time: 404 us; the launch traced here: 401 us
  waiting for transfers between devices  203 us (50%)
  Pallas kernels  64.7 us (16%)
  starting transfers between devices  37.8 us (9%)
  blocking collectives  37.4 us (9%)
  local copies, waits for them, and re-layouts  35.3 us (9%)
  other arithmetic  19.6 us (5%)
    ppermute x5, waiting for transfers between devices, pair_sum(): lax.ppermute(value, axis, [(i, i ^ step) for i in range(size)])  97.6 us
    ppermute x2, waiting for transfers between devices, halve_sum(): lax.ppermute(send, axis, [(i, i ^ step) for i in range(size)])  81.8 us
    pallas_call x1, Pallas kernels, attention(): pl.pallas_call(kern, grid=(heads, 2, n_doc + n_self), in_specs=[pl.BlockS...  64.7 us
    all_to_all x1, blocking collectives, shards(): lax.all_to_all(by_head, 'dh', split_axis=0, concat_axis=0, tiled=True)  37.4 us
    all_to_all x1, waiting for transfers between devices, shards(): lax.all_to_all(outgoing, 'cache', split_axis=0, concat_axis=0, tiled=True)  24 us
    ppermute x5, starting transfers between devices, pair_sum(): lax.ppermute(value, axis, [(i, i ^ step) for i in range(size)])  14.4 us
    all_to_all x1, starting transfers between devices, shards(): lax.all_to_all(spread, ('dh', 'dq'), split_axis=0, concat_axis=2, tiled=T...  10.1 us
    unnamed x22, local copies, waits for them, and re-layouts  10 us
  transfers between devices with their start and end apart: 11, of which 8 were waited for; matrix products, arithmetic and copies ran while one was open for 5% of the time, Pallas kernels for 0%

profile of v5, /device:TPU:16, one launch (start us, length us, event | category | flops | bytes accessed | tf_op | source)
XLA Modules:
  0.0 400.9 jit_solution(17729668949817872856)
XLA Ops:
  0.9 1.6 gather_fusion
  3.7 2.0 gather_fusion.1
  5.7 3.3 select_select_fusion
  9.0 6.3 %all-to-all-start = ((bf16[8,4,16,2048]{3,2,1,0:T(8,128)(2,1)}), bf16[8,4,16,2048]{3,2,1,0:T(8,128)(2,1)}, u32[]{:S(2)}, u32[]{:S(2)}) async-start(bf16[8,4,16,2048]{3,2,1,0:T(8,128)(2,1)} %select_select_fusion), calls=%async_computation | async-start | bytes 4194304 | tf_op jit(solution)/shard_map/all_to_all | solution.py:177
  15.3 24.0 %all-to-all-done = bf16[8,4,16,2048]{3,2,1,0:T(8,128)(2,1)} async-done(((bf16[8,4,16,2048]{3,2,1,0:T(8,128)(2,1)}), bf16[8,4,16,2048]{3,2,1,0:T(8,128)(2,1)}, u32[]{:S(2)}, u32[]{:S(2)}) %all-to-all-start) | async-done | bytes 2097184 | tf_op jit(solution)/shard_map/all_to_all | solution.py:177
  39.4 2.2 gather_fusion.2
  42.1 3.3 gather_fusion.3
  45.4 5.6 %copy_bitcast_fusion = bf16[32,16,16,256]{3,2,1,0:T(8,128)(2,1)} fusion(bf16[32,16,16,2,128]{4,2,3,1,0:T(8,128)(2,1)} %gather_fusion.3, pred[32]{0:T(512)(128)(4,1)S(1)} %compare_and_fusion.2), kind=kLoop, calls=%fused_computation.4 | loop fusion | flops 2097152 | bytes 8388640 | tf_op jit(solution)/shard_map/reshape | solution.py:35
  51.1 10.1 %all-to-all-start.1 = ((bf16[32,16,16,256]{3,2,1,0:T(8,128)(2,1)}), bf16[32,16,16,256]{3,2,1,0:T(8,128)(2,1)}, u32[]{:S(2)}, u32[]{:S(2)}) async-start(bf16[32,16,16,256]{3,2,1,0:T(8,128)(2,1)} %copy_bitcast_fusion), calls=%async_computation.1 | async-start | bytes 8388608 | tf_op jit(solution)/shard_map/all_to_all | solution.py:180
  61.3 1.8 collective-permute-start
  63.1 89.0 %collective-permute-done = f32[512]{0:T(512)S(1)} collective-permute-done((f32[512]{0:T(512)S(1)}, f32[512]{0:T(512)S(1)}, u32[]{:S(2)}, u32[]{:S(2)}) %collective-permute-start) | collective-permute-done | bytes 2080 | tf_op jit(solution)/shard_map/ppermute | solution.py:115
  152.1 3.5 collective-permute-start.1
  157.2 4.8 %collective-permute-start.2 = (f32[512]{0:T(512)S(1)}, f32[512]{0:T(512)S(1)}, u32[]{:S(2)}, u32[]{:S(2)}) collective-permute-start(f32[512]{0:T(512)S(1)} %add.189), channel_id=1, source_target_pairs={{0,4},{4,0},{8,12},{12,8},{16,20},{20,16},{24,28},{28,24},{1,5},{5... | collective-permute-start | bytes 6152 | tf_op jit(solution)/shard_map/ppermute | solution.py:115
  162.0 2.7 collective-permute-done.2
  166.0 2.2 collective-permute-done.3
  168.2 3.0 collective-permute-start.4
  171.2 2.1 collective-permute-done.4
  174.1 1.9 copy-done.1
  178.8 41.6 %collective-permute-done.5 = f32[256,2048]{1,0:T(8,128)} collective-permute-done((f32[256,2048]{1,0:T(8,128)}, f32[256,2048]{1,0:T(8,128)}, u32[]{:S(2)}, u32[]{:S(2)}) %collective-permute-start.5) | collective-permute-done | bytes 2097184 | tf_op jit(solution)/shard_map/ppermute | solution.py:129
  220.4 2.5 bitcast_add_fusion
  224.3 2.7 collective-permute-start.6
  227.1 40.2 %collective-permute-done.6 = f32[128,2048]{1,0:T(8,128)} collective-permute-done((f32[128,2048]{1,0:T(8,128)S(1)}, f32[128,2048]{1,0:T(8,128)}, u32[]{:S(2)}, u32[]{:S(2)}) %collective-permute-start.6) | collective-permute-done | bytes 1048608 | tf_op jit(solution)/shard_map/ppermute | solution.py:129
  267.2 1.7 bitcast_add_fusion.1
  268.9 4.6 %copy.41 = bf16[1,16,32,16,256]{4,3,2,1,0:T(8,128)(2,1)} copy(bf16[1,16,32,16,256]{4,3,1,2,0:T(8,128)(2,1)} %bitcast.10) | data formatting | bytes 8388608 | tf_op jit(solution)/shard_map/all_to_all | solution.py:180
  274.8 2.3 copy.43
  277.0 37.4 %all_to_all.25 = f32[8,128,2,128]{3,2,1,0:T(2,128)S(1)} all-to-all(f32[8,128,2,128]{3,2,1,0:T(2,128)} %copy.43), channel_id=1, replica_groups=mesh['cache'=8,'dh'=8,'dq'=4] {'dh'}, dimensions={0} | all-to-all | bytes 2097152 | tf_op jit(solution)/shard_map/all_to_all | solution.py:192
  315.2 5.5 %copy.49 = bf16[128,8,16,128]{3,2,1,0:T(8,128)(2,1)} copy(bf16[128,8,16,128]{3,1,2,0:T(8,128)(2,1)} %bitcast.68) | data formatting | bytes 8388608
  320.8 2.7 collective-permute-start.8
  323.5 5.9 %dynamic-slice_reduce_fusion = bf16[1024,2,128]{2,1,0:T(2,128)(2,1)S(1)} fusion(bf16[1024,2,8,128]{3,2,1,0:T(8,128)(2,1)} %bitcast.63, s32[]{:T(128)S(6)} %select_n.226), kind=kLoop, calls=%fused_computation.14 | loop fusion | bytes 1048580 | tf_op jit(solution)/shard_map/jit(dynamic_index_in_dim)/dynamic_slice | solution.py:27
  330.9 1.6 fusion.2
  332.5 3.7 convert_select_fusion.kd_ref.vd_ref
  336.2 64.7 %shard_map.91 = bf16[1024,256]{1,0:T(8,128)(2,1)} custom-call(bf16[1024,256]{1,0:T(8,128)(2,1)} %bitcast.73, bf16[16,512,256]{2,1,0:T(8,128)(2,1)} %convert_select_fusion.kd_ref.vd_ref, bf16[16,512,256]{2,1,0:T(8,128)(2,1)} %convert_select_fusion.kd_ref.vd_ref, bf16[1024,256]{1,0:T(8,128)(2,1)} %bitcast.64, bf16[1024,256]{1,0:T(8,128)(2,1)} %bitcast.65), custom_call_target="tpu_custom_call" | custom-call | tf_op jit(solution)/shard_map/pallas_call | solution.py:95
  (66 shorter events, 14.0 us)
Async XLA Ops:
  0.0 3.7 copy-start
  0.0 2.7 copy-start.6
  9.0 30.4 %all-to-all-start = ((bf16[8,4,16,2048]{3,2,1,0:T(8,128)(2,1)}), bf16[8,4,16,2048]{3,2,1,0:T(8,128)(2,1)}, u32[]{:S(2)}, u32[]{:S(2)}) async-start(bf16[8,4,16,2048]{3,2,1,0:T(8,128)(2,1)} %select_select_fusion), calls=%async_computation | async-start | bytes 4194304 | tf_op jit(solution)/shard_map/all_to_all | solution.py:177
  51.1 10.1 %copy-start.4 = (bf16[1,512,256]{2,1,0:T(8,128)(2,1)S(1)}, bf16[1,512,256]{2,1,0:T(8,128)(2,1)}, u32[]{:S(2)}) copy-start(bf16[1,512,256]{2,1,0:T(8,128)(2,1)} %param.12) | copy-start | bytes 786436
  51.1 120.2 %copy-start.8 = (bf16[256]{0:T(256)(128)(2,1)S(1)}, bf16[256]{0:T(256)(128)(2,1)}, u32[]{:S(2)}) copy-start(bf16[256]{0:T(256)(128)(2,1)} %param.13) | copy-start | bytes 1540
  51.1 122.3 %copy-start.5 = (bf16[256,2048]{1,0:T(8,128)(2,1)S(1)}, bf16[256,2048]{1,0:T(8,128)(2,1)}, u32[]{:S(2)}) copy-start(bf16[256,2048]{1,0:T(8,128)(2,1)} %param.14) | copy-start | bytes 3145732
  51.1 217.8 %all-to-all-start.1 = ((bf16[32,16,16,256]{3,2,1,0:T(8,128)(2,1)}), bf16[32,16,16,256]{3,2,1,0:T(8,128)(2,1)}, u32[]{:S(2)}, u32[]{:S(2)}) async-start(bf16[32,16,16,256]{3,2,1,0:T(8,128)(2,1)} %copy_bitcast_fusion), calls=%async_computation.1 | async-start | bytes 8388608 | tf_op jit(solution)/shard_map/all_to_all | solution.py:180
  61.3 90.8 %collective-permute-start = (f32[512]{0:T(512)S(1)}, f32[512]{0:T(512)S(1)}, u32[]{:S(2)}, u32[]{:S(2)}) collective-permute-start(f32[512]{0:T(512)S(1)} %multiply_reduce_fusion), channel_id=1, source_target_pairs={{0,1},{1,0},{2,3},{3,2},{4,5},{5,4},{6,7},{7,6},{8,9},{9,8},{10,11... | collective-permute-start | bytes 6152 | tf_op jit(solution)/shard_map/ppermute | solution.py:115
  152.1 5.0 %collective-permute-start.1 = (f32[512]{0:T(512)S(1)}, f32[512]{0:T(512)S(1)}, u32[]{:S(2)}, u32[]{:S(2)}) collective-permute-start(f32[512]{0:T(512)S(1)} %add.188), channel_id=1, source_target_pairs={{0,2},{1,3},{2,0},{3,1},{4,6},{5,7},{6,4},{7,5},{8,10},{9,11},{10,... | collective-permute-start | bytes 6152 | tf_op jit(solution)/shard_map/ppermute | solution.py:115
  157.2 7.5 %collective-permute-start.2 = (f32[512]{0:T(512)S(1)}, f32[512]{0:T(512)S(1)}, u32[]{:S(2)}, u32[]{:S(2)}) collective-permute-start(f32[512]{0:T(512)S(1)} %add.189), channel_id=1, source_target_pairs={{0,4},{4,0},{8,12},{12,8},{16,20},{20,16},{24,28},{28,24},{1,5},{5... | collective-permute-start | bytes 6152 | tf_op jit(solution)/shard_map/ppermute | solution.py:115
  164.7 3.6 collective-permute-start.3
  168.2 5.1 %collective-permute-start.4 = (f32[512]{0:T(512)S(1)}, f32[512]{0:T(512)S(1)}, u32[]{:S(2)}, u32[]{:S(2)}) collective-permute-start(f32[512]{0:T(512)S(1)} %add.191), channel_id=1, source_target_pairs={{0,16},{4,20},{8,24},{12,28},{16,0},{20,4},{24,8},{28,12},{1,17},{... | collective-permute-start | bytes 6152 | tf_op jit(solution)/shard_map/ppermute | solution.py:115
  174.1 1.9 copy-start.1
  177.5 42.9 %collective-permute-start.5 = (f32[256,2048]{1,0:T(8,128)}, f32[256,2048]{1,0:T(8,128)}, u32[]{:S(2)}, u32[]{:S(2)}) collective-permute-start(f32[256,2048]{1,0:T(8,128)} %dynamic-slice_bitcast_fusion), channel_id=1, source_target_pairs={{0,1},{1,0},{2,3},{3,2},{4,5},{5,4},{6,7},{7,6},{8,9},{9,8},{10,11... | collective-permute-start | bytes 6291464 | tf_op jit(solution)/shard_map/ppermute | solution.py:129
  222.9 1.4 copy-start.3
  224.3 42.9 %collective-permute-start.6 = (f32[128,2048]{1,0:T(8,128)S(1)}, f32[128,2048]{1,0:T(8,128)}, u32[]{:S(2)}, u32[]{:S(2)}) collective-permute-start(f32[128,2048]{1,0:T(8,128)S(1)} %dynamic-slice_bitcast_fusion.1), channel_id=1, source_target_pairs={{0,2},{1,3},{2,0},{3,1},{4,6},{5,7},{6,4},{7,5},{8,10},{9,11},{10,... | collective-permute-start | bytes 3145736 | tf_op jit(solution)/shard_map/ppermute | solution.py:129
  314.9 5.9 %collective-permute-start.7 = (bf16[128,256]{1,0:T(8,128)(2,1)S(1)}, bf16[128,256]{1,0:T(8,128)(2,1)S(1)}, u32[]{:S(2)}, u32[]{:S(2)}) collective-permute-start(bf16[128,256]{1,0:T(8,128)(2,1)S(1)} %bitcast.75), channel_id=1, source_target_pairs={{0,2},{1,3},{2,0},{3,1},{4,6},{5,7},{6,4},{7,5},{8,10},{9,11},{10,... | collective-permute-start | bytes 196616 | tf_op jit(solution)/shard_map/ppermute | solution.py:140
  315.2 15.2 %copy-start.7 = (s32[1,16,32]{2,1,0:T(8,128)S(1)}, s32[1,16,32]{2,1,0:T(8,128)}, u32[]{:S(2)}) copy-start(s32[1,16,32]{2,1,0:T(8,128)} %param.17) | copy-start | bytes 6148
  320.8 9.9 %collective-permute-start.8 = (bf16[256,256]{1,0:T(8,128)(2,1)S(1)}, bf16[256,256]{1,0:T(8,128)(2,1)S(1)}, u32[]{:S(2)}, u32[]{:S(2)}) collective-permute-start(bf16[256,256]{1,0:T(8,128)(2,1)S(1)} %maximum_select_fusion.1), channel_id=1, source_target_pairs={{0,1},{1,0},{2,3},{3,2},{4,5},{5,4},{6,7},{7,6},{8,9},{9,8},{10,11... | collective-permute-start | bytes 393224 | tf_op jit(solution)/shard_map/ppermute | solution.py:140
  329.5 3.0 copy-start.2

commit v6 on v4

--- a/solution.py
+++ b/solution.py
@@ -35,10 +35,9 @@
     return moved.reshape(moved.shape[:-2] + (2 * head_size,))
 
 
-def attn_kernel(q_ref, kd_ref, vd_ref, ks_ref, vs_ref, o_ref, m_sc, l_sc, acc_sc, *, n_doc, n_self, blk, inv_root):
+def attn_kernel(q_ref, kd_ref, vd_ref, ks_ref, vs_ref, o_ref, m_sc, l_sc, acc_sc, *, n_doc, n_self, blk_self, inv_root):
     phase = pl.program_id(1)
     j = pl.program_id(2)
-    rows = q_ref.shape[0]
 
     @pl.when((phase == 0) & (j == 0))
     def _():
@@ -46,9 +45,10 @@
         l_sc[...] = jnp.zeros(l_sc.shape, jnp.float32)
         acc_sc[...] = jnp.zeros(acc_sc.shape, jnp.float32)
 
-    def scores(k_ref, first_key):
-        s = lax.dot_general(q_ref[...], k_ref[...], (((1,), (1,)), ((), ())),
-                            preferred_element_type=jnp.float32) * inv_root
+    def raw(k_ref):
+        return lax.dot_general(q_ref[...], k_ref[...], (((1,), (1,)), ((), ())), preferred_element_type=jnp.float32)
+
+    def mask(s, first_key):
         if first_key is None:
             return s
         t = lax.broadcasted_iota(jnp.int32, s.shape, 0)
@@ -58,16 +58,16 @@
     def step(k_ref, v_ref, first_key):
         @pl.when(phase == 0)
         def _():
-            s = scores(k_ref, first_key)
+            s = mask(raw(k_ref) * inv_root, first_key)
             m_sc[...] = jnp.maximum(m_sc[...], jnp.max(s, axis=1, keepdims=True))
 
         @pl.when(phase == 1)
         def _():
-            s = scores(k_ref, first_key)
+            s = mask(raw(k_ref) * inv_root, first_key)
             e = jnp.exp(s - m_sc[:, :1])
+            eb = e.astype(jnp.bfloat16)
             l_sc[...] = l_sc[...] + jnp.sum(e, axis=1, keepdims=True)
-            acc_sc[...] = acc_sc[...] + jnp.dot(e.astype(jnp.bfloat16), v_ref[...],
-                                                preferred_element_type=jnp.float32)
+            acc_sc[...] = acc_sc[...] + jnp.dot(eb, v_ref[...], preferred_element_type=jnp.float32)
 
     @pl.when(j < n_doc)
     def _():
@@ -76,36 +76,39 @@
     for b in range(n_self):
         @pl.when(j == n_doc + b)
         def _(b=b):
-            step(ks_ref, vs_ref, b * blk)
+            step(ks_ref, vs_ref, b * blk_self)
 
     @pl.when((phase == 1) & (j == pl.num_programs(2) - 1))
     def _():
-        o_ref[...] = (acc_sc[...] / l_sc[:, :1]).astype(o_ref.dtype)
-
-
-def attention(q2d, blocks, own_self):
+        o_ref[...] = (acc_sc[...] / l_sc[...][:, :1]).astype(o_ref.dtype)
+
+
+def attention(q2d, blocks, own_self, bk=2048):
     T, width = q2d.shape
     heads = width // HD
-    n_doc, blk, _ = blocks.shape
-    n_self = T // blk
-    last_doc = n_doc - 1
-    kern = functools.partial(attn_kernel, n_doc=n_doc, n_self=n_self, blk=blk, inv_root=1.0 / math.sqrt(HD))
-    doc_at = lambda j: jnp.minimum(j, last_doc)
+    flat = blocks.reshape(-1, blocks.shape[-1])
+    n_doc = flat.shape[0] // bk
+    bs = min(bk, T)
+    n_self = T // bs
+    kern = functools.partial(attn_kernel, n_doc=n_doc, n_self=n_self, blk_self=bs, inv_root=1.0 / math.sqrt(HD))
+    doc_at = lambda j: jnp.minimum(j, n_doc - 1)
     self_at = lambda j: jnp.maximum(j - n_doc, 0)
+    kd_spec = pl.BlockSpec((bk, HD), lambda h, p, j: (doc_at(j), 0))
+    ks_spec = pl.BlockSpec((bs, HD), lambda h, p, j: (self_at(j), 0))
     return pl.pallas_call(
         kern,
         grid=(heads, 2, n_doc + n_self),
         in_specs=[
             pl.BlockSpec((T, HD), lambda h, p, j: (0, h)),
-            pl.BlockSpec((None, blk, HD), lambda h, p, j: (doc_at(j), 0, 0)),
-            pl.BlockSpec((None, blk, HD), lambda h, p, j: (doc_at(j), 0, 1)),
-            pl.BlockSpec((blk, HD), lambda h, p, j: (self_at(j), 0)),
-            pl.BlockSpec((blk, HD), lambda h, p, j: (self_at(j), 1)),
+            kd_spec,
+            pl.BlockSpec((bk, HD), lambda h, p, j: (doc_at(j), 1)),
+            ks_spec,
+            pl.BlockSpec((bs, HD), lambda h, p, j: (self_at(j), 1)),
         ],
         out_specs=pl.BlockSpec((T, HD), lambda h, p, j: (0, h)),
         out_shape=jax.ShapeDtypeStruct((T, width), q2d.dtype),
         scratch_shapes=[pltpu.VMEM((T, HD), jnp.float32)] * 3,
-    )(q2d, blocks, blocks, own_self, own_self)
+    )(q2d, flat, flat, own_self, own_self)
 
 
 def pair_sum(value, axis):

time: 344 us -> 322 us (0.936)
  Pallas kernels: 64.7 us -> 43.5 us
    pallas_call x1, Pallas kernels: 64.7 us -> 43.5 us  [attention(): pl.pallas_call(kern, grid=(heads, 2, n_doc + n_self), in_specs=[pl.BlockS...]
where the time goes in v6:
time: 322 us; the launch traced here: 321 us
  waiting for transfers between devices  177 us (55%)
  Pallas kernels  43.5 us (14%)
  starting transfers between devices  41.8 us (13%)
  local copies, waits for them, and re-layouts  33 us (10%)
  other arithmetic  18.6 us (6%)
  matrix products  6.29 us (2%)
    ppermute x2, waiting for transfers between devices, double_gather(): other = lax.ppermute(value, axis, [(i, i ^ step) for i in range(size)])  84.1 us
    ppermute x2, waiting for transfers between devices, halve_sum(): lax.ppermute(send, axis, [(i, i ^ step) for i in range(size)])  69.8 us
    pallas_call x1, Pallas kernels, attention(): pl.pallas_call(kern, grid=(heads, 2, n_doc + n_self), in_specs=[pl.BlockS...  43.5 us
    ppermute x5, starting transfers between devices, pair_sum(): lax.ppermute(value, axis, [(i, i ^ step) for i in range(size)])  16.6 us
    all_to_all x1, waiting for transfers between devices, shards(): lax.all_to_all(by_head, 'dh', split_axis=0, concat_axis=0, tiled=True)  16 us
    unnamed x16, local copies, waits for them, and re-layouts  10 us
    all_to_all x1, starting transfers between devices, shards(): lax.all_to_all(by_head, 'dh', split_axis=0, concat_axis=0, tiled=True)  8.62 us
    ppermute x5, waiting for transfers between devices, pair_sum(): lax.ppermute(value, axis, [(i, i ^ step) for i in range(size)])  7.53 us
  transfers between devices with their start and end apart: 12, of which 9 were waited for; matrix products, arithmetic and copies ran while one was open for 13% of the time, Pallas kernels for 0%

profile of v6, /device:TPU:16, one launch (start us, length us, event | category | flops | bytes accessed | tf_op | source)
XLA Modules:
  0.0 321.0 jit_solution(3974380430126911688)
XLA Ops:
  1.3 2.0 collective-permute-start
  3.3 1.7 collective-permute-done
  4.9 3.3 %collective-permute-start.1 = (f32[512]{0:T(512)S(1)}, f32[512]{0:T(512)S(1)}, u32[]{:S(2)}, u32[]{:S(2)}) collective-permute-start(f32[512]{0:T(512)S(1)} %add.173), channel_id=1, source_target_pairs={{0,2},{1,3},{2,0},{3,1},{4,6},{5,7},{6,4},{7,5},{8,10},{9,11},{10,... | collective-permute-start | bytes 6152 | tf_op jit(solution)/shard_map/ppermute | solution.py:118
  8.2 1.6 collective-permute-done.1
  9.8 6.8 %collective-permute-start.2 = (f32[512]{0:T(512)S(1)}, f32[512]{0:T(512)S(1)}, u32[]{:S(2)}, u32[]{:S(2)}) collective-permute-start(f32[512]{0:T(512)S(1)} %add.174), channel_id=1, source_target_pairs={{0,4},{4,0},{8,12},{12,8},{16,20},{20,16},{24,28},{28,24},{1,5},{5... | collective-permute-start | bytes 6152 | tf_op jit(solution)/shard_map/ppermute | solution.py:118
  19.7 2.1 collective-permute-done.3
  21.8 3.0 collective-permute-start.4
  26.9 2.1 fusion
  29.0 1.9 copy-done.2
  35.8 2.0 gather_fusion.1
  37.8 3.3 %select_select_fusion = bf16[8,4,16,2048]{3,2,1,0:T(8,128)(2,1)} fusion(bf16[8,4,16,2048]{3,2,1,0:T(8,128)(2,1)} %bitcast.65, pred[8,4]{1,0:T(8,128)(4,1)S(1)} %copy.39, pred[8,4]{1,0:T(8,128)(4,1)S(1)} %copy.38), kind=kLoop, calls=%fused_computation.8 | loop fusion | flops 2097152 | bytes 4194368 | tf_op jit(solution)/shard_map/jit(_where)/select_n | solution.py:175
  41.1 4.8 %all-to-all-start.1 = ((bf16[8,4,16,2048]{3,2,1,0:T(8,128)(2,1)}), bf16[8,4,16,2048]{3,2,1,0:T(8,128)(2,1)}, u32[]{:S(2)}, u32[]{:S(2)}) async-start(bf16[8,4,16,2048]{3,2,1,0:T(8,128)(2,1)} %select_select_fusion), calls=%async_computation.1 | async-start | bytes 4194304 | tf_op jit(solution)/shard_map/all_to_all | solution.py:180
  45.9 29.2 %collective-permute-done.5 = f32[256,2048]{1,0:T(8,128)} collective-permute-done((f32[256,2048]{1,0:T(8,128)}, f32[256,2048]{1,0:T(8,128)}, u32[]{:S(2)}, u32[]{:S(2)}) %collective-permute-start.5) | collective-permute-done | bytes 2097184 | tf_op jit(solution)/shard_map/ppermute | solution.py:132
  75.1 2.5 bitcast_add_fusion
  79.0 2.0 collective-permute-start.6
  81.0 40.6 %collective-permute-done.6 = f32[128,2048]{1,0:T(8,128)} collective-permute-done((f32[128,2048]{1,0:T(8,128)S(1)}, f32[128,2048]{1,0:T(8,128)}, u32[]{:S(2)}, u32[]{:S(2)}) %collective-permute-start.6) | collective-permute-done | bytes 1048608 | tf_op jit(solution)/shard_map/ppermute | solution.py:132
  121.6 1.7 bitcast_add_fusion.1
  124.6 2.3 copy.37
  126.9 8.6 %all-to-all-start = ((f32[8,128,2,128]{3,2,1,0:T(2,128)}), f32[8,128,2,128]{3,2,1,0:T(2,128)}, u32[]{:S(2)}, u32[]{:S(2)}) async-start(f32[8,128,2,128]{3,2,1,0:T(2,128)} %copy.37), calls=%async_computation | async-start | bytes 2097152 | tf_op jit(solution)/shard_map/all_to_all | solution.py:194
  135.6 2.2 gather_fusion.2
  138.3 3.4 %gather_fusion.3 = bf16[32,16,16,2,128]{4,2,3,1,0:T(8,128)(2,1)} fusion(bf16[16,16,2,8,128]{4,1,3,2,0:T(8,128)(2,1)S(1)} %copy_select_fusion, s32[1024]{0:T(1024)S(1)} %pad_clamp_fusion), kind=kCustom, calls=%fused_computation.3 | custom fusion | bytes 8388736 | tf_op jit(solution)/shard_map/jit(_take)/gather | solution.py:33
  141.7 5.6 %copy_bitcast_fusion = bf16[32,16,16,256]{3,2,1,0:T(8,128)(2,1)} fusion(bf16[32,16,16,2,128]{4,2,3,1,0:T(8,128)(2,1)} %gather_fusion.3, pred[32]{0:T(512)(128)(4,1)S(1)} %compare_and_fusion.2), kind=kLoop, calls=%fused_computation.4 | loop fusion | flops 2097152 | bytes 8388640 | tf_op jit(solution)/shard_map/reshape | solution.py:35
  147.3 16.0 %all-to-all-done = f32[8,128,2,128]{3,2,1,0:T(2,128)} async-done(((f32[8,128,2,128]{3,2,1,0:T(2,128)}), f32[8,128,2,128]{3,2,1,0:T(2,128)}, u32[]{:S(2)}, u32[]{:S(2)}) %all-to-all-start) | async-done | bytes 1048608 | tf_op jit(solution)/shard_map/all_to_all | solution.py:194
  163.3 5.6 %all-to-all-start.2 = ((bf16[32,16,16,256]{3,2,1,0:T(8,128)(2,1)}), bf16[32,16,16,256]{3,2,1,0:T(8,128)(2,1)}, u32[]{:S(2)}, u32[]{:S(2)}) async-start(bf16[32,16,16,256]{3,2,1,0:T(8,128)(2,1)} %copy_bitcast_fusion), calls=%async_computation.2 | async-start | bytes 8388608 | tf_op jit(solution)/shard_map/all_to_all | solution.py:183
  168.9 1.6 reduce_sum.37
  170.5 2.7 collective-permute-start.7
  173.2 5.6 %copy.49 = bf16[128,8,16,128]{3,2,1,0:T(8,128)(2,1)} copy(bf16[128,8,16,128]{3,1,2,0:T(8,128)(2,1)} %bitcast.71) | data formatting | bytes 8388608
  178.8 84.1 %collective-permute-done.7 = bf16[128,256]{1,0:T(8,128)(2,1)S(1)} collective-permute-done((bf16[128,256]{1,0:T(8,128)(2,1)S(1)}, bf16[128,256]{1,0:T(8,128)(2,1)S(1)}, u32[]{:S(2)}, u32[]{:S(2)}) %collective-permute-start.7) | collective-permute-done | bytes 65568 | tf_op jit(solution)/shard_map/ppermute | solution.py:143
  263.3 5.9 %dynamic-slice_reduce_fusion = bf16[1024,2,128]{2,1,0:T(2,128)(2,1)S(1)} fusion(bf16[1024,2,8,128]{3,2,1,0:T(8,128)(2,1)} %bitcast.66, s32[]{:T(128)S(6)} %select_n.226), kind=kLoop, calls=%fused_computation.14 | loop fusion | bytes 1048580 | tf_op jit(solution)/shard_map/jit(dynamic_index_in_dim)/dynamic_slice | solution.py:27
  270.6 2.6 copy.43
  273.3 4.2 %convert_select_fusion = bf16[16,512,256]{2,1,0:T(8,128)(2,1)} fusion(bf16[16,512,256]{2,1,0:T(8,128)(2,1)S(1)} %bitcast.62, pred[16,512]{1,0:T(8,128)(4,1)S(1)} %fusion.2, bf16[16,32,256]{2,1,0:T(8,128)(2,1)S(1)} %bitcast.74, s32[16,32]{1,0:T(8,128)S(1)} %bitcast.81), kind=kOutput, calls=%fused_computation.6 | convolution fusion | flops 138674176 | bytes 8660992 | tf_op jit(solution)/shard_map/kib,kic->kbc/dot_general | solution.py:201
  277.5 43.5 %shard_map.91 = bf16[1024,256]{1,0:T(8,128)(2,1)} custom-call(bf16[1024,256]{1,0:T(8,128)(2,1)} %bitcast.76, bf16[8192,256]{1,0:T(8,128)(2,1)} %bitcast.60, bf16[8192,256]{1,0:T(8,128)(2,1)} %bitcast.61, bf16[1024,256]{1,0:T(8,128)(2,1)} %bitcast.67, bf16[1024,256]{1,0:T(8,128)(2,1)} %bitcast.68), custom_call_target="tpu_custom_call" | custom-call | tf_op jit(solution)/shard_map/pallas_call | solution.py:98
  (60 shorter events, 16.3 us)
Async XLA Ops:
  0.0 35.8 %copy-start = (bf16[32,16,2048]{2,1,0:T(8,128)(2,1)S(1)}, bf16[32,16,2048]{2,1,0:T(8,128)(2,1)}, u32[]{:S(2)}) copy-start(bf16[32,16,2048]{2,1,0:T(8,128)(2,1)} %param.10) | copy-start | bytes 6291460
  1.3 3.7 %collective-permute-start = (f32[512]{0:T(512)S(1)}, f32[512]{0:T(512)S(1)}, u32[]{:S(2)}, u32[]{:S(2)}) collective-permute-start(f32[512]{0:T(512)S(1)} %multiply_reduce_fusion), channel_id=1, source_target_pairs={{0,1},{1,0},{2,3},{3,2},{4,5},{5,4},{6,7},{7,6},{8,9},{9,8},{10,11... | collective-permute-start | bytes 6152 | tf_op jit(solution)/shard_map/ppermute | solution.py:118
  4.9 4.8 %collective-permute-start.1 = (f32[512]{0:T(512)S(1)}, f32[512]{0:T(512)S(1)}, u32[]{:S(2)}, u32[]{:S(2)}) collective-permute-start(f32[512]{0:T(512)S(1)} %add.173), channel_id=1, source_target_pairs={{0,2},{1,3},{2,0},{3,1},{4,6},{5,7},{6,4},{7,5},{8,10},{9,11},{10,... | collective-permute-start | bytes 6152 | tf_op jit(solution)/shard_map/ppermute | solution.py:118
  9.8 8.4 %collective-permute-start.2 = (f32[512]{0:T(512)S(1)}, f32[512]{0:T(512)S(1)}, u32[]{:S(2)}, u32[]{:S(2)}) collective-permute-start(f32[512]{0:T(512)S(1)} %add.174), channel_id=1, source_target_pairs={{0,4},{4,0},{8,12},{12,8},{16,20},{20,16},{24,28},{28,24},{1,5},{5... | collective-permute-start | bytes 6152 | tf_op jit(solution)/shard_map/ppermute | solution.py:118
  18.2 3.6 %collective-permute-start.3 = (f32[512]{0:T(512)S(1)}, f32[512]{0:T(512)S(1)}, u32[]{:S(2)}, u32[]{:S(2)}) collective-permute-start(f32[512]{0:T(512)S(1)} %add.175), channel_id=1, source_target_pairs={{0,8},{4,12},{8,0},{12,4},{16,24},{20,28},{24,16},{28,20},{1,9},{5... | collective-permute-start | bytes 6152 | tf_op jit(solution)/shard_map/ppermute | solution.py:118
  21.8 5.1 %collective-permute-start.4 = (f32[512]{0:T(512)S(1)}, f32[512]{0:T(512)S(1)}, u32[]{:S(2)}, u32[]{:S(2)}) collective-permute-start(f32[512]{0:T(512)S(1)} %add.176), channel_id=1, source_target_pairs={{0,16},{4,20},{8,24},{12,28},{16,0},{20,4},{24,8},{28,12},{1,17},{... | collective-permute-start | bytes 6152 | tf_op jit(solution)/shard_map/ppermute | solution.py:118
  26.9 6.5 %copy-start.1 = (s32[256]{0:T(256)S(1)}, s32[256]{0:T(256)}, u32[]{:S(2)}) copy-start(s32[256]{0:T(256)} %param.16) | copy-start | bytes 3076
  29.0 1.9 copy-start.2
  30.9 3.8 %copy-start.4 = (s32[8,16]{1,0:T(8,128)S(1)}, s32[8,16]{1,0:T(8,128)}, u32[]{:S(2)}) copy-start(s32[8,16]{1,0:T(8,128)} %param.15) | copy-start | bytes 1540
  32.4 42.8 %collective-permute-start.5 = (f32[256,2048]{1,0:T(8,128)}, f32[256,2048]{1,0:T(8,128)}, u32[]{:S(2)}, u32[]{:S(2)}) collective-permute-start(f32[256,2048]{1,0:T(8,128)} %dynamic-slice_bitcast_fusion), channel_id=1, source_target_pairs={{0,1},{1,0},{2,3},{3,2},{4,5},{5,4},{6,7},{7,6},{8,9},{9,8},{10,11... | collective-permute-start | bytes 6291464 | tf_op jit(solution)/shard_map/ppermute | solution.py:132
  41.1 85.8 %all-to-all-start.1 = ((bf16[8,4,16,2048]{3,2,1,0:T(8,128)(2,1)}), bf16[8,4,16,2048]{3,2,1,0:T(8,128)(2,1)}, u32[]{:S(2)}, u32[]{:S(2)}) async-start(bf16[8,4,16,2048]{3,2,1,0:T(8,128)(2,1)} %select_select_fusion), calls=%async_computation.1 | async-start | bytes 4194304 | tf_op jit(solution)/shard_map/all_to_all | solution.py:180
  77.6 1.3 copy-start.3
  79.0 42.6 %collective-permute-start.6 = (f32[128,2048]{1,0:T(8,128)S(1)}, f32[128,2048]{1,0:T(8,128)}, u32[]{:S(2)}, u32[]{:S(2)}) collective-permute-start(f32[128,2048]{1,0:T(8,128)S(1)} %dynamic-slice_bitcast_fusion.1), channel_id=1, source_target_pairs={{0,2},{1,3},{2,0},{3,1},{4,6},{5,7},{6,4},{7,5},{8,10},{9,11},{10,... | collective-permute-start | bytes 3145736 | tf_op jit(solution)/shard_map/ppermute | solution.py:132
  126.9 36.4 %all-to-all-start = ((f32[8,128,2,128]{3,2,1,0:T(2,128)}), f32[8,128,2,128]{3,2,1,0:T(2,128)}, u32[]{:S(2)}, u32[]{:S(2)}) async-start(f32[8,128,2,128]{3,2,1,0:T(2,128)} %copy.37), calls=%async_computation | async-start | bytes 2097152 | tf_op jit(solution)/shard_map/all_to_all | solution.py:194
  163.3 107.3 %all-to-all-start.2 = ((bf16[32,16,16,256]{3,2,1,0:T(8,128)(2,1)}), bf16[32,16,16,256]{3,2,1,0:T(8,128)(2,1)}, u32[]{:S(2)}, u32[]{:S(2)}) async-start(bf16[32,16,16,256]{3,2,1,0:T(8,128)(2,1)} %copy_bitcast_fusion), calls=%async_computation.2 | async-start | bytes 8388608 | tf_op jit(solution)/shard_map/all_to_all | solution.py:183
  170.5 92.3 %collective-permute-start.7 = (bf16[128,256]{1,0:T(8,128)(2,1)S(1)}, bf16[128,256]{1,0:T(8,128)(2,1)S(1)}, u32[]{:S(2)}, u32[]{:S(2)}) collective-permute-start(bf16[128,256]{1,0:T(8,128)(2,1)S(1)} %bitcast.78), channel_id=1, source_target_pairs={{0,2},{1,3},{2,0},{3,1},{4,6},{5,7},{6,4},{7,5},{8,10},{9,11},{10,... | collective-permute-start | bytes 196616 | tf_op jit(solution)/shard_map/ppermute | solution.py:143
  173.2 96.9 %copy-start.5 = (s32[1,16,32]{2,1,0:T(8,128)S(1)}, s32[1,16,32]{2,1,0:T(8,128)}, u32[]{:S(2)}) copy-start(s32[1,16,32]{2,1,0:T(8,128)} %param.17) | copy-start | bytes 6148
  262.9 7.6 %collective-permute-start.8 = (bf16[256,256]{1,0:T(8,128)(2,1)S(1)}, bf16[256,256]{1,0:T(8,128)(2,1)S(1)}, u32[]{:S(2)}, u32[]{:S(2)}) collective-permute-start(bf16[256,256]{1,0:T(8,128)(2,1)S(1)} %maximum_select_fusion.1), channel_id=1, source_target_pairs={{0,1},{1,0},{2,3},{3,2},{4,5},{5,4},{6,7},{7,6},{8,9},{9,8},{10,11... | collective-permute-start | bytes 393224 | tf_op jit(solution)/shard_map/ppermute | solution.py:143

commit v7 on v6

--- a/solution.py
+++ b/solution.py
@@ -35,9 +35,9 @@
     return moved.reshape(moved.shape[:-2] + (2 * head_size,))
 
 
-def attn_kernel(q_ref, kd_ref, vd_ref, ks_ref, vs_ref, o_ref, m_sc, l_sc, acc_sc, *, n_doc, n_self, blk_self, inv_root):
-    phase = pl.program_id(1)
-    j = pl.program_id(2)
+def attn_kernel(q_ref, kd_ref, vd_ref, ks_ref, vs_ref, o_ref, m_sc, l_sc, acc_sc, *, n_doc, n_self, blk_self, inv_root, heads):
+    phase = pl.program_id(0)
+    j = pl.program_id(1)
 
     @pl.when((phase == 0) & (j == 0))
     def _():
@@ -45,10 +45,9 @@
         l_sc[...] = jnp.zeros(l_sc.shape, jnp.float32)
         acc_sc[...] = jnp.zeros(acc_sc.shape, jnp.float32)
 
-    def raw(k_ref):
-        return lax.dot_general(q_ref[...], k_ref[...], (((1,), (1,)), ((), ())), preferred_element_type=jnp.float32)
-
-    def mask(s, first_key):
+    def scores(h, k_ref, first_key):
+        q = q_ref[:, h * HD:(h + 1) * HD]
+        s = lax.dot_general(q, k_ref[...], (((1,), (1,)), ((), ())), preferred_element_type=jnp.float32) * inv_root
         if first_key is None:
             return s
         t = lax.broadcasted_iota(jnp.int32, s.shape, 0)
@@ -58,16 +57,17 @@
     def step(k_ref, v_ref, first_key):
         @pl.when(phase == 0)
         def _():
-            s = mask(raw(k_ref) * inv_root, first_key)
-            m_sc[...] = jnp.maximum(m_sc[...], jnp.max(s, axis=1, keepdims=True))
+            for h in range(heads):
+                s = scores(h, k_ref, first_key)
+                m_sc[h] = jnp.maximum(m_sc[h], jnp.max(s, axis=1, keepdims=True))
 
         @pl.when(phase == 1)
         def _():
-            s = mask(raw(k_ref) * inv_root, first_key)
-            e = jnp.exp(s - m_sc[:, :1])
-            eb = e.astype(jnp.bfloat16)
-            l_sc[...] = l_sc[...] + jnp.sum(e, axis=1, keepdims=True)
-            acc_sc[...] = acc_sc[...] + jnp.dot(eb, v_ref[...], preferred_element_type=jnp.float32)
+            for h in range(heads):
+                s = scores(h, k_ref, first_key)
+                e = jnp.exp(s - m_sc[h][:, :1])
+                l_sc[h] = l_sc[h] + jnp.sum(e, axis=1, keepdims=True)
+                acc_sc[h] = acc_sc[h] + jnp.dot(e.astype(jnp.bfloat16), v_ref[...], preferred_element_type=jnp.float32)
 
     @pl.when(j < n_doc)
     def _():
@@ -78,9 +78,10 @@
         def _(b=b):
             step(ks_ref, vs_ref, b * blk_self)
 
-    @pl.when((phase == 1) & (j == pl.num_programs(2) - 1))
+    @pl.when((phase == 1) & (j == pl.num_programs(1) - 1))
     def _():
-        o_ref[...] = (acc_sc[...] / l_sc[...][:, :1]).astype(o_ref.dtype)
+        for h in range(heads):
+            o_ref[:, h * HD:(h + 1) * HD] = (acc_sc[h] / l_sc[h][:, :1]).astype(o_ref.dtype)
 
 
 def attention(q2d, blocks, own_self, bk=2048):
@@ -90,24 +91,22 @@
     n_doc = flat.shape[0] // bk
     bs = min(bk, T)
     n_self = T // bs
-    kern = functools.partial(attn_kernel, n_doc=n_doc, n_self=n_self, blk_self=bs, inv_root=1.0 / math.sqrt(HD))
+    kern = functools.partial(attn_kernel, n_doc=n_doc, n_self=n_self, blk_self=bs, inv_root=1.0 / math.sqrt(HD), heads=heads)
     doc_at = lambda j: jnp.minimum(j, n_doc - 1)
     self_at = lambda j: jnp.maximum(j - n_doc, 0)
-    kd_spec = pl.BlockSpec((bk, HD), lambda h, p, j: (doc_at(j), 0))
-    ks_spec = pl.BlockSpec((bs, HD), lambda h, p, j: (self_at(j), 0))
     return pl.pallas_call(
         kern,
-        grid=(heads, 2, n_doc + n_self),
+        grid=(2, n_doc + n_self),
         in_specs=[
-            pl.BlockSpec((T, HD), lambda h, p, j: (0, h)),
-            kd_spec,
-            pl.BlockSpec((bk, HD), lambda h, p, j: (doc_at(j), 1)),
-            ks_spec,
-            pl.BlockSpec((bs, HD), lambda h, p, j: (self_at(j), 1)),
+            pl.BlockSpec((T, width), lambda p, j: (0, 0)),
+            pl.BlockSpec((bk, HD), lambda p, j: (doc_at(j), 0)),
+            pl.BlockSpec((bk, HD), lambda p, j: (doc_at(j), 1)),
+            pl.BlockSpec((bs, HD), lambda p, j: (self_at(j), 0)),
+            pl.BlockSpec((bs, HD), lambda p, j: (self_at(j), 1)),
         ],
-        out_specs=pl.BlockSpec((T, HD), lambda h, p, j: (0, h)),
+        out_specs=pl.BlockSpec((T, width), lambda p, j: (0, 0)),
         out_shape=jax.ShapeDtypeStruct((T, width), q2d.dtype),
-        scratch_shapes=[pltpu.VMEM((T, HD), jnp.float32)] * 3,
+        scratch_shapes=[pltpu.VMEM((heads, T, HD), jnp.float32)] * 3,
     )(q2d, flat, flat, own_self, own_self)
 
 
@@ -184,7 +183,8 @@
     states = rec_states[0].astype(jnp.float32)
     rows_rec = states.shape[0]
     partial_sq = jnp.sum(states * states, axis=1)
-    total_sq = pair_sum(pair_sum(partial_sq, "dq"), "dh")
+    sq_rows = jnp.broadcast_to(partial_sq[None, :], (members, rows_rec))
+    total_sq = jnp.sum(lax.all_to_all(sq_rows, ("dh", "dq"), split_axis=0, concat_axis=0, tiled=True), axis=0)
     inv_rms = lax.rsqrt(total_sq / D + eps_norm)
     normed = (states * norm_gain.astype(jnp.float32)[None, :] * inv_rms[:, None]).astype(jnp.bfloat16)
     partial_kv = jnp.dot(normed, w_kv, preferred_element_type=jnp.float32)

time: 322 us -> 318 us (0.988)
  starting transfers between devices: 41.8 us -> 31.1 us
  waiting for transfers between devices: 177 us -> 186 us
    ppermute x5 -> x0, starting transfers between devices: 16.6 us -> none  [pair_sum(): lax.ppermute(value, axis, [(i, i ^ step) for i in range(size)])]
    all_to_all x0 -> x1, starting transfers between devices: none -> 11.3 us  [shards(): lax.all_to_all(sq_rows, ('dh', 'dq'), split_axis=0, concat_axis=0, tiled=...]
    all_to_all x0 -> x1, waiting for transfers between devices: none -> 8.57 us  [shards(): lax.all_to_all(sq_rows, ('dh', 'dq'), split_axis=0, concat_axis=0, tiled=...]
    ppermute x2, waiting for transfers between devices: 69.8 us -> 77.7 us  [halve_sum(): lax.ppermute(send, axis, [(i, i ^ step) for i in range(size)])]
    ppermute x5 -> x0, waiting for transfers between devices: 7.53 us -> none  [pair_sum(): lax.ppermute(value, axis, [(i, i ^ step) for i in range(size)])]
    all_to_all x1, starting transfers between devices: 8.62 us -> 4.24 us  [shards(): lax.all_to_all(by_head, 'dh', split_axis=0, concat_axis=0, tiled=True)]
  transfers between devices with their start and end apart: 12 -> 8, of which waited for: 9 -> 5; matrix products, arithmetic and copies ran while one was open for 13% -> 14% of each run, Pallas kernels for 0% -> 0%
where the time goes in v7:
time: 318 us; the launch traced here: 317 us
  waiting for transfers between devices  186 us (58%)
  Pallas kernels  40.8 us (13%)
  local copies, waits for them, and re-layouts  33.8 us (11%)
  starting transfers between devices  31.1 us (10%)
  other arithmetic  18.7 us (6%)
  matrix products  6.3 us (2%)
    ppermute x2, waiting for transfers between devices, double_gather(): other = lax.ppermute(value, axis, [(i, i ^ step) for i in range(size)])  83.9 us
    ppermute x2, waiting for transfers between devices, halve_sum(): lax.ppermute(send, axis, [(i, i ^ step) for i in range(size)])  77.7 us
    pallas_call x1, Pallas kernels, attention(): pl.pallas_call(kern, grid=(2, n_doc + n_self), in_specs=[pl.BlockSpec((T,...  40.8 us
    all_to_all x1, waiting for transfers between devices, shards(): lax.all_to_all(by_head, 'dh', split_axis=0, concat_axis=0, tiled=True)  15.9 us
    all_to_all x1, starting transfers between devices, shards(): lax.all_to_all(sq_rows, ('dh', 'dq'), split_axis=0, concat_axis=0, tiled=...  11.3 us
    unnamed x16, local copies, waits for them, and re-layouts  10 us
    all_to_all x1, waiting for transfers between devices, shards(): lax.all_to_all(sq_rows, ('dh', 'dq'), split_axis=0, concat_axis=0, tiled=...  8.57 us
  transfers between devices with their start and end apart: 8, of which 5 were waited for; matrix products, arithmetic and copies ran while one was open for 14% of the time, Pallas kernels for 0%

profile of v7, /device:TPU:16, one launch (start us, length us, event | category | flops | bytes accessed | tf_op | source)
XLA Modules:
  0.0 317.1 jit_solution(10321978161394289116)
XLA Ops:
  0.0 1.2 multiply_reduce_fusion
  1.9 11.3 %all-to-all-start = ((f32[32,1,512]{2,1,0:T(1,128)}), f32[32,1,512]{2,1,0:T(1,128)S(1)}, u32[]{:S(2)}, u32[]{:S(2)}) async-start(f32[32,1,512]{2,1,0:T(1,128)} %broadcast_in_dim.94), calls=%async_computation | async-start | bytes 131072 | tf_op jit(solution)/shard_map/all_to_all | solution.py:187
  14.7 8.6 %all-to-all-done = f32[32,1,512]{2,1,0:T(1,128)S(1)} async-done(((f32[32,1,512]{2,1,0:T(1,128)}), f32[32,1,512]{2,1,0:T(1,128)S(1)}, u32[]{:S(2)}, u32[]{:S(2)}) %all-to-all-start) | async-done | bytes 65568 | tf_op jit(solution)/shard_map/all_to_all | solution.py:187
  23.4 2.1 fusion
  25.4 1.9 copy-done.2
  27.4 1.4 dynamic-slice_bitcast_fusion
  29.7 1.3 gather_fusion
  32.1 2.0 gather_fusion.1
  34.1 3.3 %select_select_fusion = bf16[8,4,16,2048]{3,2,1,0:T(8,128)(2,1)} fusion(bf16[8,4,16,2048]{3,2,1,0:T(8,128)(2,1)} %bitcast.65, pred[8,4]{1,0:T(8,128)(4,1)S(1)} %copy.49, pred[8,4]{1,0:T(8,128)(4,1)S(1)} %copy.48), kind=kLoop, calls=%fused_computation.8 | loop fusion | flops 2097152 | bytes 4194368 | tf_op jit(solution)/shard_map/jit(_where)/select_n | solution.py:174
  37.4 4.8 %all-to-all-start.2 = ((bf16[8,4,16,2048]{3,2,1,0:T(8,128)(2,1)}), bf16[8,4,16,2048]{3,2,1,0:T(8,128)(2,1)}, u32[]{:S(2)}, u32[]{:S(2)}) async-start(bf16[8,4,16,2048]{3,2,1,0:T(8,128)(2,1)} %select_select_fusion), calls=%async_computation.2 | async-start | bytes 4194304 | tf_op jit(solution)/shard_map/all_to_all | solution.py:179
  42.2 32.9 %collective-permute-done = f32[256,2048]{1,0:T(8,128)} collective-permute-done((f32[256,2048]{1,0:T(8,128)}, f32[256,2048]{1,0:T(8,128)}, u32[]{:S(2)}, u32[]{:S(2)}) %collective-permute-start) | collective-permute-done | bytes 2097184 | tf_op jit(solution)/shard_map/ppermute | solution.py:131
  75.1 2.5 bitcast_add_fusion
  77.5 1.3 copy-done.3
  79.0 1.2 collective-permute-start.1
  80.2 44.9 %collective-permute-done.1 = f32[128,2048]{1,0:T(8,128)} collective-permute-done((f32[128,2048]{1,0:T(8,128)S(1)}, f32[128,2048]{1,0:T(8,128)}, u32[]{:S(2)}, u32[]{:S(2)}) %collective-permute-start.1) | collective-permute-done | bytes 1048608 | tf_op jit(solution)/shard_map/ppermute | solution.py:131
  125.1 1.7 bitcast_add_fusion.1
  126.7 1.3 copy.46
  128.1 2.3 copy.47
  130.4 4.2 %all-to-all-start.1 = ((f32[8,128,2,128]{3,2,1,0:T(2,128)}), f32[8,128,2,128]{3,2,1,0:T(2,128)}, u32[]{:S(2)}, u32[]{:S(2)}) async-start(f32[8,128,2,128]{3,2,1,0:T(2,128)} %copy.47), calls=%async_computation.1 | async-start | bytes 2097152 | tf_op jit(solution)/shard_map/all_to_all | solution.py:194
  134.7 2.2 gather_fusion.2
  137.4 3.4 %gather_fusion.3 = bf16[32,16,16,2,128]{4,2,3,1,0:T(8,128)(2,1)} fusion(bf16[16,16,2,8,128]{4,1,3,2,0:T(8,128)(2,1)S(1)} %copy_select_fusion, s32[1024]{0:T(1024)S(1)} %pad_clamp_fusion), kind=kCustom, calls=%fused_computation.3 | custom fusion | bytes 8388736 | tf_op jit(solution)/shard_map/jit(_take)/gather | solution.py:33
  140.8 5.6 %copy_bitcast_fusion = bf16[32,16,16,256]{3,2,1,0:T(8,128)(2,1)} fusion(bf16[32,16,16,2,128]{4,2,3,1,0:T(8,128)(2,1)} %gather_fusion.3, pred[32]{0:T(512)(128)(4,1)S(1)} %compare_and_fusion.2), kind=kLoop, calls=%fused_computation.4 | loop fusion | flops 2097152 | bytes 8388640 | tf_op jit(solution)/shard_map/reshape | solution.py:35
  146.4 15.9 %all-to-all-done.1 = f32[8,128,2,128]{3,2,1,0:T(2,128)} async-done(((f32[8,128,2,128]{3,2,1,0:T(2,128)}), f32[8,128,2,128]{3,2,1,0:T(2,128)}, u32[]{:S(2)}, u32[]{:S(2)}) %all-to-all-start.1) | async-done | bytes 1048608 | tf_op jit(solution)/shard_map/all_to_all | solution.py:194
  162.2 5.6 %all-to-all-start.3 = ((bf16[32,16,16,256]{3,2,1,0:T(8,128)(2,1)}), bf16[32,16,16,256]{3,2,1,0:T(8,128)(2,1)}, u32[]{:S(2)}, u32[]{:S(2)}) async-start(bf16[32,16,16,256]{3,2,1,0:T(8,128)(2,1)} %copy_bitcast_fusion), calls=%async_computation.3 | async-start | bytes 8388608 | tf_op jit(solution)/shard_map/all_to_all | solution.py:182
  167.8 1.6 reduce_sum.47
  169.4 2.7 collective-permute-start.2
  172.1 5.6 %copy.60 = bf16[128,8,16,128]{3,2,1,0:T(8,128)(2,1)} copy(bf16[128,8,16,128]{3,1,2,0:T(8,128)(2,1)} %bitcast.71) | data formatting | bytes 8388608
  177.7 83.9 %collective-permute-done.2 = bf16[128,256]{1,0:T(8,128)(2,1)S(1)} collective-permute-done((bf16[128,256]{1,0:T(8,128)(2,1)S(1)}, bf16[128,256]{1,0:T(8,128)(2,1)S(1)}, u32[]{:S(2)}, u32[]{:S(2)}) %collective-permute-start.2) | collective-permute-done | bytes 65568 | tf_op jit(solution)/shard_map/ppermute | solution.py:142
  262.1 5.9 %dynamic-slice_reduce_fusion = bf16[1024,2,128]{2,1,0:T(2,128)(2,1)S(1)} fusion(bf16[1024,2,8,128]{3,2,1,0:T(8,128)(2,1)} %bitcast.66, s32[]{:T(128)S(6)} %select_n.226), kind=kLoop, calls=%fused_computation.14 | loop fusion | bytes 1048580 | tf_op jit(solution)/shard_map/jit(dynamic_index_in_dim)/dynamic_slice | solution.py:27
  269.4 2.6 copy.53
  272.1 4.2 %convert_select_fusion = bf16[16,512,256]{2,1,0:T(8,128)(2,1)} fusion(bf16[16,512,256]{2,1,0:T(8,128)(2,1)S(1)} %bitcast.62, pred[16,512]{1,0:T(8,128)(4,1)S(1)} %fusion.2, bf16[16,32,256]{2,1,0:T(8,128)(2,1)S(1)} %bitcast.74, s32[16,32]{1,0:T(8,128)S(1)} %bitcast.81), kind=kOutput, calls=%fused_computation.6 | convolution fusion | flops 138674176 | bytes 8660992 | tf_op jit(solution)/shard_map/kib,kic->kbc/dot_general | solution.py:201
  276.3 40.8 %shard_map.91 = bf16[1024,256]{1,0:T(8,128)(2,1)} custom-call(bf16[1024,256]{1,0:T(8,128)(2,1)} %bitcast.76, bf16[8192,256]{1,0:T(8,128)(2,1)} %bitcast.60, bf16[8192,256]{1,0:T(8,128)(2,1)} %bitcast.61, bf16[1024,256]{1,0:T(8,128)(2,1)} %bitcast.67, bf16[1024,256]{1,0:T(8,128)(2,1)} %bitcast.68), custom_call_target="tpu_custom_call" | custom-call | tf_op jit(solution)/shard_map/pallas_call | solution.py:97
  (50 shorter events, 6.6 us)
Async XLA Ops:
  0.0 32.1 %copy-start = (bf16[32,16,2048]{2,1,0:T(8,128)(2,1)S(1)}, bf16[32,16,2048]{2,1,0:T(8,128)(2,1)}, u32[]{:S(2)}) copy-start(bf16[32,16,2048]{2,1,0:T(8,128)(2,1)} %param.10) | copy-start | bytes 6291460
  1.9 21.3 %all-to-all-start = ((f32[32,1,512]{2,1,0:T(1,128)}), f32[32,1,512]{2,1,0:T(1,128)S(1)}, u32[]{:S(2)}, u32[]{:S(2)}) async-start(f32[32,1,512]{2,1,0:T(1,128)} %broadcast_in_dim.94), calls=%async_computation | async-start | bytes 131072 | tf_op jit(solution)/shard_map/all_to_all | solution.py:187
  23.4 6.3 %copy-start.1 = (s32[256]{0:T(256)S(1)}, s32[256]{0:T(256)}, u32[]{:S(2)}) copy-start(s32[256]{0:T(256)} %param.16) | copy-start | bytes 3076
  25.4 1.9 copy-start.2
  27.4 3.7 %copy-start.4 = (s32[8,16]{1,0:T(8,128)S(1)}, s32[8,16]{1,0:T(8,128)}, u32[]{:S(2)}) copy-start(s32[8,16]{1,0:T(8,128)} %param.15) | copy-start | bytes 1540
  28.8 46.3 %collective-permute-start = (f32[256,2048]{1,0:T(8,128)}, f32[256,2048]{1,0:T(8,128)}, u32[]{:S(2)}, u32[]{:S(2)}) collective-permute-start(f32[256,2048]{1,0:T(8,128)} %dynamic-slice_bitcast_fusion), channel_id=1, source_target_pairs={{0,1},{1,0},{2,3},{3,2},{4,5},{5,4},{6,7},{7,6},{8,9},{9,8},{10,11... | collective-permute-start | bytes 6291464 | tf_op jit(solution)/shard_map/ppermute | solution.py:131
  37.4 93.0 %all-to-all-start.2 = ((bf16[8,4,16,2048]{3,2,1,0:T(8,128)(2,1)}), bf16[8,4,16,2048]{3,2,1,0:T(8,128)(2,1)}, u32[]{:S(2)}, u32[]{:S(2)}) async-start(bf16[8,4,16,2048]{3,2,1,0:T(8,128)(2,1)} %select_select_fusion), calls=%async_computation.2 | async-start | bytes 4194304 | tf_op jit(solution)/shard_map/all_to_all | solution.py:179
  77.5 1.4 copy-start.3
  79.0 46.1 %collective-permute-start.1 = (f32[128,2048]{1,0:T(8,128)S(1)}, f32[128,2048]{1,0:T(8,128)}, u32[]{:S(2)}, u32[]{:S(2)}) collective-permute-start(f32[128,2048]{1,0:T(8,128)S(1)} %dynamic-slice_bitcast_fusion.1), channel_id=1, source_target_pairs={{0,2},{1,3},{2,0},{3,1},{4,6},{5,7},{6,4},{7,5},{8,10},{9,11},{10,... | collective-permute-start | bytes 3145736 | tf_op jit(solution)/shard_map/ppermute | solution.py:131
  130.4 31.9 %all-to-all-start.1 = ((f32[8,128,2,128]{3,2,1,0:T(2,128)}), f32[8,128,2,128]{3,2,1,0:T(2,128)}, u32[]{:S(2)}, u32[]{:S(2)}) async-start(f32[8,128,2,128]{3,2,1,0:T(2,128)} %copy.47), calls=%async_computation.1 | async-start | bytes 2097152 | tf_op jit(solution)/shard_map/all_to_all | solution.py:194
  162.2 107.2 %all-to-all-start.3 = ((bf16[32,16,16,256]{3,2,1,0:T(8,128)(2,1)}), bf16[32,16,16,256]{3,2,1,0:T(8,128)(2,1)}, u32[]{:S(2)}, u32[]{:S(2)}) async-start(bf16[32,16,16,256]{3,2,1,0:T(8,128)(2,1)} %copy_bitcast_fusion), calls=%async_computation.3 | async-start | bytes 8388608 | tf_op jit(solution)/shard_map/all_to_all | solution.py:182
  169.4 92.2 %collective-permute-start.2 = (bf16[128,256]{1,0:T(8,128)(2,1)S(1)}, bf16[128,256]{1,0:T(8,128)(2,1)S(1)}, u32[]{:S(2)}, u32[]{:S(2)}) collective-permute-start(bf16[128,256]{1,0:T(8,128)(2,1)S(1)} %bitcast.78), channel_id=1, source_target_pairs={{0,2},{1,3},{2,0},{3,1},{4,6},{5,7},{6,4},{7,5},{8,10},{9,11},{10,... | collective-permute-start | bytes 196616 | tf_op jit(solution)/shard_map/ppermute | solution.py:142
  172.1 96.8 %copy-start.5 = (s32[1,16,32]{2,1,0:T(8,128)S(1)}, s32[1,16,32]{2,1,0:T(8,128)}, u32[]{:S(2)}) copy-start(s32[1,16,32]{2,1,0:T(8,128)} %param.17) | copy-start | bytes 6148
  261.7 7.6 %collective-permute-start.3 = (bf16[256,256]{1,0:T(8,128)(2,1)S(1)}, bf16[256,256]{1,0:T(8,128)(2,1)S(1)}, u32[]{:S(2)}, u32[]{:S(2)}) collective-permute-start(bf16[256,256]{1,0:T(8,128)(2,1)S(1)} %maximum_select_fusion.1), channel_id=1, source_target_pairs={{0,1},{1,0},{2,3},{3,2},{4,5},{5,4},{6,7},{7,6},{8,9},{9,8},{10,11... | collective-permute-start | bytes 393224 | tf_op jit(solution)/shard_map/ppermute | solution.py:142

commit v8 on v7

--- a/solution.py
+++ b/solution.py
@@ -35,7 +35,7 @@
     return moved.reshape(moved.shape[:-2] + (2 * head_size,))
 
 
-def attn_kernel(q_ref, kd_ref, vd_ref, ks_ref, vs_ref, o_ref, m_sc, l_sc, acc_sc, *, n_doc, n_self, blk_self, inv_root, heads):
+def attn_kernel(q_ref, kd_ref, vd_ref, kp_ref, vp_ref, fl_ref, ks_ref, vs_ref, o_ref, m_sc, l_sc, acc_sc, *, n_doc, n_self, blk_self, inv_root, heads):
     phase = pl.program_id(0)
     j = pl.program_id(1)
 
@@ -45,38 +45,44 @@
         l_sc[...] = jnp.zeros(l_sc.shape, jnp.float32)
         acc_sc[...] = jnp.zeros(acc_sc.shape, jnp.float32)
 
-    def scores(h, k_ref, first_key):
+    def scores(h, keys, first_key):
         q = q_ref[:, h * HD:(h + 1) * HD]
-        s = lax.dot_general(q, k_ref[...], (((1,), (1,)), ((), ())), preferred_element_type=jnp.float32) * inv_root
+        s = lax.dot_general(q, keys, (((1,), (1,)), ((), ())), preferred_element_type=jnp.float32) * inv_root
         if first_key is None:
             return s
         t = lax.broadcasted_iota(jnp.int32, s.shape, 0)
         u = lax.broadcasted_iota(jnp.int32, s.shape, 1) + first_key
         return jnp.where(u <= t, s, -jnp.inf)
 
-    def step(k_ref, v_ref, first_key):
+    def step(get_keys, get_values, first_key):
         @pl.when(phase == 0)
         def _():
+            keys = get_keys()
             for h in range(heads):
-                s = scores(h, k_ref, first_key)
+                s = scores(h, keys, first_key)
                 m_sc[h] = jnp.maximum(m_sc[h], jnp.max(s, axis=1, keepdims=True))
 
         @pl.when(phase == 1)
         def _():
+            keys = get_keys()
+            values = get_values()
             for h in range(heads):
-                s = scores(h, k_ref, first_key)
+                s = scores(h, keys, first_key)
                 e = jnp.exp(s - m_sc[h][:, :1])
                 l_sc[h] = l_sc[h] + jnp.sum(e, axis=1, keepdims=True)
-                acc_sc[h] = acc_sc[h] + jnp.dot(e.astype(jnp.bfloat16), v_ref[...], preferred_element_type=jnp.float32)
+                acc_sc[h] = acc_sc[h] + jnp.dot(e.astype(jnp.bfloat16), values, preferred_element_type=jnp.float32)
+
+    def merged(placed_ref, stored_ref):
+        return jnp.where(fl_ref[...] != 0, placed_ref[...], stored_ref[...])
 
     @pl.when(j < n_doc)
     def _():
-        step(kd_ref, vd_ref, None)
+        step(lambda: merged(kp_ref, kd_ref), lambda: merged(vp_ref, vd_ref), None)
 
     for b in range(n_self):
         @pl.when(j == n_doc + b)
         def _(b=b):
-            step(ks_ref, vs_ref, b * blk_self)
+            step(lambda: ks_ref[...], lambda: vs_ref[...], b * blk_self)
 
     @pl.when((phase == 1) & (j == pl.num_programs(1) - 1))
     def _():
@@ -84,10 +90,9 @@
             o_ref[:, h * HD:(h + 1) * HD] = (acc_sc[h] / l_sc[h][:, :1]).astype(o_ref.dtype)
 
 
-def attention(q2d, blocks, own_self, bk=2048):
+def attention(q2d, flat, placed, flags, own_self, bk=2048):
     T, width = q2d.shape
     heads = width // HD
-    flat = blocks.reshape(-1, blocks.shape[-1])
     n_doc = flat.shape[0] // bk
     bs = min(bk, T)
     n_self = T // bs
@@ -101,13 +106,16 @@
             pl.BlockSpec((T, width), lambda p, j: (0, 0)),
             pl.BlockSpec((bk, HD), lambda p, j: (doc_at(j), 0)),
             pl.BlockSpec((bk, HD), lambda p, j: (doc_at(j), 1)),
+            pl.BlockSpec((bk, HD), lambda p, j: (doc_at(j), 0)),
+            pl.BlockSpec((bk, HD), lambda p, j: (doc_at(j), 1)),
+            pl.BlockSpec((bk, 1), lambda p, j: (doc_at(j), 0)),
             pl.BlockSpec((bs, HD), lambda p, j: (self_at(j), 0)),
             pl.BlockSpec((bs, HD), lambda p, j: (self_at(j), 1)),
         ],
         out_specs=pl.BlockSpec((T, width), lambda p, j: (0, 0)),
         out_shape=jax.ShapeDtypeStruct((T, width), q2d.dtype),
         scratch_shapes=[pltpu.VMEM((heads, T, HD), jnp.float32)] * 3,
-    )(q2d, flat, flat, own_self, own_self)
+    )(q2d, flat, flat, placed, placed, flags, own_self, own_self)
 
 
 def pair_sum(value, axis):
@@ -179,7 +187,7 @@
     arrived = lax.all_to_all(outgoing, "cache", split_axis=0, concat_axis=0, tiled=True)
     compact = jnp.take(arrived.reshape(groups * CAP, shard_rows, kv_width), slot_place, axis=0)
     spread = pick_heads(compact, KVH, HD, dest_heads)
-    fetched = lax.all_to_all(spread, ("dh", "dq"), split_axis=0, concat_axis=2, tiled=True)[0]
+    fetched = lax.all_to_all(spread, ("dh", "dq"), split_axis=0, concat_axis=0, tiled=True)
     states = rec_states[0].astype(jnp.float32)
     rows_rec = states.shape[0]
     partial_sq = jnp.sum(states * states, axis=1)
@@ -195,16 +203,19 @@
     head_rows = jnp.sum(head_parts, axis=0).reshape(part_rows, 2 * HD).astype(jnp.bfloat16)
     redone = double_gather(head_rows, "dq")
     own_rows = redone.reshape(RET, REC, 2 * HD)
-    full_block = fetched.shape[1]
     positions = rec_index[0]
-    onehot = positions[:, :, None] == jnp.arange(full_block, dtype=jnp.int32)[None, None, :]
+    shard_tokens = fetched.shape[2]
+    spots = jnp.arange(members, dtype=jnp.int32)[:, None] * shard_tokens + jnp.arange(
+        shard_tokens, dtype=jnp.int32
+    )[None, :]
+    onehot = positions[None, :, None, :] == spots[:, None, :, None]
     placed = jnp.einsum(
-        "kib,kic->kbc", onehot.astype(jnp.bfloat16), own_rows, preferred_element_type=jnp.float32
+        "mkti,kic->mktc", onehot.astype(jnp.bfloat16), own_rows, preferred_element_type=jnp.float32
     ).astype(jnp.bfloat16)
-    replaced_at = jnp.any(onehot, axis=1)
-    blocks = jnp.where(replaced_at[:, :, None], placed, fetched)
+    flags = jnp.any(onehot, axis=3).astype(jnp.int32).reshape(-1, 1)
     own_self = own_head(self_kv[0], KVH, HD, my_head)
-    return attention(queries[0], blocks, own_self)[None]
+    width = fetched.shape[-1]
+    return attention(queries[0], fetched.reshape(-1, width), placed.reshape(-1, width), flags, own_self)[None]
 
 
 def solution(mesh):

time: 318 us -> 320 us (level)
  waiting for transfers between devices: 186 us -> 179 us
  local copies, waits for them, and re-layouts: 33.8 us -> 39.3 us
  other arithmetic: 18.7 us -> 22.9 us
    convert_element_type x0 -> x3, local copies, waits for them, and re-layouts: none -> 8.2 us  [the longest x1 4.39 us: shards(): placed = jnp.einsum('mkti,kic->mktc', onehot.astype(jnp.bfloat16), own_ro...]
    ppermute x2, waiting for transfers between devices: 83.9 us -> 76.9 us  [double_gather(): other = lax.ppermute(value, axis, [(i, i ^ step) for i in range(size)])]
    reduce_or x1, other arithmetic: 0.34 us -> 4.5 us  [shards(): flags = jnp.any(onehot, axis=3).astype(jnp.int32).reshape(-1, 1)]
  transfers between devices with their start and end apart: 8 -> 8, of which waited for: 5 -> 5; matrix products, arithmetic and copies ran while one was open for 14% -> 18% of each run, Pallas kernels for 0% -> 0%
where the time goes in v8:
time: 320 us; the launch traced here: 319 us
  waiting for transfers between devices  179 us (56%)
  Pallas kernels  43.4 us (14%)
  local copies, waits for them, and re-layouts  39.3 us (12%)
  starting transfers between devices  31.1 us (10%)
  other arithmetic  22.9 us (7%)
  matrix products  3.37 us (1%)
    ppermute x2, waiting for transfers between devices, halve_sum(): lax.ppermute(send, axis, [(i, i ^ step) for i in range(size)])  77.7 us
    ppermute x2, waiting for transfers between devices, double_gather(): other = lax.ppermute(value, axis, [(i, i ^ step) for i in range(size)])  76.9 us
    pallas_call x1, Pallas kernels, attention(): pl.pallas_call(kern, grid=(2, n_doc + n_self), in_specs=[pl.BlockSpec((T,...  43.4 us
    all_to_all x1, waiting for transfers between devices, shards(): lax.all_to_all(by_head, 'dh', split_axis=0, concat_axis=0, tiled=True)  15.9 us
    all_to_all x1, starting transfers between devices, shards(): lax.all_to_all(sq_rows, ('dh', 'dq'), split_axis=0, concat_axis=0, tiled=...  11.3 us
    unnamed x16, local copies, waits for them, and re-layouts  9.98 us
    all_to_all x1, waiting for transfers between devices, shards(): lax.all_to_all(sq_rows, ('dh', 'dq'), split_axis=0, concat_axis=0, tiled=...  8.57 us
  transfers between devices with their start and end apart: 8, of which 5 were waited for; matrix products, arithmetic and copies ran while one was open for 18% of the time, Pallas kernels for 0%

profile of v8, /device:TPU:16, one launch (start us, length us, event | category | flops | bytes accessed | tf_op | source)
XLA Modules:
  0.0 319.5 jit_solution(2839048901560362253)
XLA Ops:
  1.9 11.3 %all-to-all-start.2 = ((f32[32,1,512]{2,1,0:T(1,128)}), f32[32,1,512]{2,1,0:T(1,128)S(1)}, u32[]{:S(2)}, u32[]{:S(2)}) async-start(f32[32,1,512]{2,1,0:T(1,128)} %broadcast_in_dim.98), calls=%async_computation.2 | async-start | bytes 131072 | tf_op jit(solution)/shard_map/all_to_all | solution.py:195
  14.7 8.6 %all-to-all-done.2 = f32[32,1,512]{2,1,0:T(1,128)S(1)} async-done(((f32[32,1,512]{2,1,0:T(1,128)}), f32[32,1,512]{2,1,0:T(1,128)S(1)}, u32[]{:S(2)}, u32[]{:S(2)}) %all-to-all-start.2) | async-done | bytes 65568 | tf_op jit(solution)/shard_map/all_to_all | solution.py:195
  23.4 2.1 fusion.6
  25.4 1.9 copy-done.2
  27.4 1.4 dynamic-slice_bitcast_fusion
  29.7 1.3 gather_fusion
  32.1 2.0 gather_fusion.1
  34.1 3.3 %select_select_fusion = bf16[8,4,16,2048]{3,2,1,0:T(8,128)(2,1)} fusion(bf16[8,4,16,2048]{3,2,1,0:T(8,128)(2,1)} %bitcast.67, pred[8,4]{1,0:T(8,128)(4,1)S(1)} %copy.60, pred[8,4]{1,0:T(8,128)(4,1)S(1)} %copy.59), kind=kLoop, calls=%fused_computation.14 | loop fusion | flops 2097152 | bytes 4194368 | tf_op jit(solution)/shard_map/jit(_where)/select_n | solution.py:182
  37.4 4.8 %all-to-all-start = ((bf16[8,4,16,2048]{3,2,1,0:T(8,128)(2,1)}), bf16[8,4,16,2048]{3,2,1,0:T(8,128)(2,1)}, u32[]{:S(2)}, u32[]{:S(2)}) async-start(bf16[8,4,16,2048]{3,2,1,0:T(8,128)(2,1)} %select_select_fusion), calls=%async_computation | async-start | bytes 4194304 | tf_op jit(solution)/shard_map/all_to_all | solution.py:187
  42.2 32.9 %collective-permute-done = f32[256,2048]{1,0:T(8,128)} collective-permute-done((f32[256,2048]{1,0:T(8,128)}, f32[256,2048]{1,0:T(8,128)}, u32[]{:S(2)}, u32[]{:S(2)}) %collective-permute-start) | collective-permute-done | bytes 2097184 | tf_op jit(solution)/shard_map/ppermute | solution.py:139
  75.1 2.5 bitcast_add_fusion
  77.5 1.3 copy-done.3
  80.2 44.9 %collective-permute-done.1 = f32[128,2048]{1,0:T(8,128)} collective-permute-done((f32[128,2048]{1,0:T(8,128)S(1)}, f32[128,2048]{1,0:T(8,128)}, u32[]{:S(2)}, u32[]{:S(2)}) %collective-permute-start.1) | collective-permute-done | bytes 1048608 | tf_op jit(solution)/shard_map/ppermute | solution.py:139
  125.1 1.7 bitcast_add_fusion.1
  126.7 1.3 copy.65
  128.1 2.3 copy.66
  130.4 4.2 %all-to-all-start.3 = ((f32[8,128,2,128]{3,2,1,0:T(2,128)}), f32[8,128,2,128]{3,2,1,0:T(2,128)}, u32[]{:S(2)}, u32[]{:S(2)}) async-start(f32[8,128,2,128]{3,2,1,0:T(2,128)} %copy.66), calls=%async_computation.3 | async-start | bytes 2097152 | tf_op jit(solution)/shard_map/all_to_all | solution.py:202
  134.7 2.2 gather_fusion.2
  137.4 3.4 %gather_fusion.3 = bf16[32,16,16,2,128]{4,2,3,1,0:T(8,128)(2,1)} fusion(bf16[16,16,2,8,128]{4,1,3,2,0:T(8,128)(2,1)S(1)} %copy_select_fusion, s32[1024]{0:T(1024)S(1)} %pad_clamp_fusion), kind=kCustom, calls=%fused_computation.3 | custom fusion | bytes 8388736 | tf_op jit(solution)/shard_map/jit(_take)/gather | solution.py:33
  140.8 5.6 %copy_bitcast_fusion = bf16[32,16,16,256]{3,2,1,0:T(8,128)(2,1)} fusion(bf16[32,16,16,2,128]{4,2,3,1,0:T(8,128)(2,1)} %gather_fusion.3, pred[32]{0:T(512)(128)(4,1)S(1)} %compare_and_fusion.2), kind=kLoop, calls=%fused_computation.7 | loop fusion | flops 2097152 | bytes 8388640 | tf_op jit(solution)/shard_map/reshape | solution.py:35
  146.4 15.9 %all-to-all-done.3 = f32[8,128,2,128]{3,2,1,0:T(2,128)} async-done(((f32[8,128,2,128]{3,2,1,0:T(2,128)}), f32[8,128,2,128]{3,2,1,0:T(2,128)}, u32[]{:S(2)}, u32[]{:S(2)}) %all-to-all-start.3) | async-done | bytes 1048608 | tf_op jit(solution)/shard_map/all_to_all | solution.py:202
  162.3 5.6 %all-to-all-start.1 = ((bf16[32,16,16,256]{3,2,1,0:T(8,128)(2,1)}), bf16[32,16,16,256]{3,2,1,0:T(8,128)(2,1)}, u32[]{:S(2)}, u32[]{:S(2)}) async-start(bf16[32,16,16,256]{3,2,1,0:T(8,128)(2,1)} %copy_bitcast_fusion), calls=%async_computation.1 | async-start | bytes 8388608 | tf_op jit(solution)/shard_map/all_to_all | solution.py:190
  167.9 5.6 %copy.77 = bf16[128,8,16,128]{3,2,1,0:T(8,128)(2,1)} copy(bf16[128,8,16,128]{3,1,2,0:T(8,128)(2,1)} %bitcast.73) | data formatting | bytes 8388608
  173.5 1.6 reduce_sum.49
  175.1 2.9 collective-permute-start.2
  178.0 5.9 %dynamic-slice_reduce_fusion = bf16[1024,2,128]{2,1,0:T(2,128)(2,1)S(1)} fusion(bf16[1024,2,8,128]{3,2,1,0:T(8,128)(2,1)} %bitcast.68, s32[]{:T(128)S(6)} %select_n.221), kind=kLoop, calls=%fused_computation.19 | loop fusion | bytes 1048580 | tf_op jit(solution)/shard_map/jit(dynamic_index_in_dim)/dynamic_slice | solution.py:27
  184.8 76.9 %collective-permute-done.2 = bf16[128,256]{1,0:T(8,128)(2,1)S(1)} collective-permute-done((bf16[128,256]{1,0:T(8,128)(2,1)S(1)}, bf16[128,256]{1,0:T(8,128)(2,1)S(1)}, u32[]{:S(2)}, u32[]{:S(2)}) %collective-permute-start.2) | collective-permute-done | bytes 65568 | tf_op jit(solution)/shard_map/ppermute | solution.py:150
  261.9 4.5 %compare_reduce_fusion = pred[32,16,16]{0,2,1:T(8,128)(4,1)S(1)} fusion(s32[32,16]{0,1:T(8,128)S(1)} %iota_add_fusion, s32[16,32]{1,0:T(8,128)S(1)} %bitcast.82), kind=kLoop, calls=%fused_computation.4 | loop fusion | flops 516096 | bytes 12288 | tf_op jit(solution)/shard_map/reduce_or | solution.py:215
  266.6 3.6 %reshape.378.fl_ref = s32[8192,1]{1,0:T(8,128)} reshape(s32[32,16,16]{2,1,0:T(8,128)S(1)} %copy.68) | data formatting | bytes 65536 | tf_op jit(solution)/shard_map/convert_element_type | solution.py:215
  270.4 1.3 convert_bitcast_fusion
  271.7 4.4 %copy.67 = bf16[32,16,16,256]{3,2,1,0:T(8,128)(2,1)} copy(bf16[32,16,16,256]{3,0,2,1:T(8,128)(2,1)S(1)} %convert_bitcast_fusion) | data formatting | bytes 8388608 | tf_op jit(solution)/shard_map/convert_element_type | solution.py:214
  276.1 43.4 %shard_map.91 = bf16[1024,256]{1,0:T(8,128)(2,1)} custom-call(bf16[1024,256]{1,0:T(8,128)(2,1)} %bitcast.78, bf16[8192,256]{1,0:T(8,128)(2,1)} %bitcast.8.kd_ref.vd_ref, bf16[8192,256]{1,0:T(8,128)(2,1)} %bitcast.8.kd_ref.vd_ref, bf16[8192,256]{1,0:T(8,128)(2,1)} %bitcast.63, bf16[8192,256]{1,0:T(8,128)(2,1)} %bitcast.64, s32[8192,1]{1,0:T(8,128)} %reshape.378.fl_ref, ...), custom_call_target="tpu_custom_call" | custom-call | tf_op jit(solution)/shard_map/pallas_call | solution.py:102
  (55 shorter events, 8.7 us)
Async XLA Ops:
  0.0 32.1 %copy-start = (bf16[32,16,2048]{2,1,0:T(8,128)(2,1)S(1)}, bf16[32,16,2048]{2,1,0:T(8,128)(2,1)}, u32[]{:S(2)}) copy-start(bf16[32,16,2048]{2,1,0:T(8,128)(2,1)} %param.10) | copy-start | bytes 6291460
  1.9 21.3 %all-to-all-start.2 = ((f32[32,1,512]{2,1,0:T(1,128)}), f32[32,1,512]{2,1,0:T(1,128)S(1)}, u32[]{:S(2)}, u32[]{:S(2)}) async-start(f32[32,1,512]{2,1,0:T(1,128)} %broadcast_in_dim.98), calls=%async_computation.2 | async-start | bytes 131072 | tf_op jit(solution)/shard_map/all_to_all | solution.py:195
  23.4 6.3 %copy-start.1 = (s32[256]{0:T(256)S(1)}, s32[256]{0:T(256)}, u32[]{:S(2)}) copy-start(s32[256]{0:T(256)} %param.16) | copy-start | bytes 3076
  25.4 1.9 copy-start.2
  27.4 3.7 %copy-start.4 = (s32[8,16]{1,0:T(8,128)S(1)}, s32[8,16]{1,0:T(8,128)}, u32[]{:S(2)}) copy-start(s32[8,16]{1,0:T(8,128)} %param.15) | copy-start | bytes 1540
  28.8 46.3 %collective-permute-start = (f32[256,2048]{1,0:T(8,128)}, f32[256,2048]{1,0:T(8,128)}, u32[]{:S(2)}, u32[]{:S(2)}) collective-permute-start(f32[256,2048]{1,0:T(8,128)} %dynamic-slice_bitcast_fusion), channel_id=1, source_target_pairs={{0,1},{1,0},{2,3},{3,2},{4,5},{5,4},{6,7},{7,6},{8,9},{9,8},{10,11... | collective-permute-start | bytes 6291464 | tf_op jit(solution)/shard_map/ppermute | solution.py:139
  37.4 93.0 %all-to-all-start = ((bf16[8,4,16,2048]{3,2,1,0:T(8,128)(2,1)}), bf16[8,4,16,2048]{3,2,1,0:T(8,128)(2,1)}, u32[]{:S(2)}, u32[]{:S(2)}) async-start(bf16[8,4,16,2048]{3,2,1,0:T(8,128)(2,1)} %select_select_fusion), calls=%async_computation | async-start | bytes 4194304 | tf_op jit(solution)/shard_map/all_to_all | solution.py:187
  77.5 1.4 copy-start.3
  79.0 46.1 %collective-permute-start.1 = (f32[128,2048]{1,0:T(8,128)S(1)}, f32[128,2048]{1,0:T(8,128)}, u32[]{:S(2)}, u32[]{:S(2)}) collective-permute-start(f32[128,2048]{1,0:T(8,128)S(1)} %dynamic-slice_bitcast_fusion.1), channel_id=1, source_target_pairs={{0,2},{1,3},{2,0},{3,1},{4,6},{5,7},{6,4},{7,5},{8,10},{9,11},{10,... | collective-permute-start | bytes 3145736 | tf_op jit(solution)/shard_map/ppermute | solution.py:139
  130.4 31.9 %all-to-all-start.3 = ((f32[8,128,2,128]{3,2,1,0:T(2,128)}), f32[8,128,2,128]{3,2,1,0:T(2,128)}, u32[]{:S(2)}, u32[]{:S(2)}) async-start(f32[8,128,2,128]{3,2,1,0:T(2,128)} %copy.66), calls=%async_computation.3 | async-start | bytes 2097152 | tf_op jit(solution)/shard_map/all_to_all | solution.py:202
  162.3 113.8 %all-to-all-start.1 = ((bf16[32,16,16,256]{3,2,1,0:T(8,128)(2,1)}), bf16[32,16,16,256]{3,2,1,0:T(8,128)(2,1)}, u32[]{:S(2)}, u32[]{:S(2)}) async-start(bf16[32,16,16,256]{3,2,1,0:T(8,128)(2,1)} %copy_bitcast_fusion), calls=%async_computation.1 | async-start | bytes 8388608 | tf_op jit(solution)/shard_map/all_to_all | solution.py:190
  167.8 94.1 %copy-start.5 = (s32[1,16,32]{2,1,0:T(8,128)S(1)}, s32[1,16,32]{2,1,0:T(8,128)}, u32[]{:S(2)}) copy-start(s32[1,16,32]{2,1,0:T(8,128)} %param.17) | copy-start | bytes 6148
  175.1 86.6 %collective-permute-start.2 = (bf16[128,256]{1,0:T(8,128)(2,1)S(1)}, bf16[128,256]{1,0:T(8,128)(2,1)S(1)}, u32[]{:S(2)}, u32[]{:S(2)}) collective-permute-start(bf16[128,256]{1,0:T(8,128)(2,1)S(1)} %bitcast.80), channel_id=1, source_target_pairs={{0,2},{1,3},{2,0},{3,1},{4,6},{5,7},{6,4},{7,5},{8,10},{9,11},{10,... | collective-permute-start | bytes 196616 | tf_op jit(solution)/shard_map/ppermute | solution.py:150
  261.7 8.6 %collective-permute-start.3 = (bf16[256,256]{1,0:T(8,128)(2,1)S(1)}, bf16[256,256]{1,0:T(8,128)(2,1)S(1)}, u32[]{:S(2)}, u32[]{:S(2)}) collective-permute-start(bf16[256,256]{1,0:T(8,128)(2,1)S(1)} %maximum_select_fusion.1), channel_id=1, source_target_pairs={{0,1},{1,0},{2,3},{3,2},{4,5},{5,4},{6,7},{7,6},{8,9},{9,8},{10,11... | collective-permute-start | bytes 393224 | tf_op jit(solution)/shard_map/ppermute | solution.py:150

commit v9 on v7

--- a/solution.py
+++ b/solution.py
@@ -119,15 +119,16 @@
     return value
 
 
-def halve_sum(value, axis):
+def halve_sum(value, axis, dim=0):
     size = lax.axis_size(axis)
     me = lax.axis_index(axis)
     step = 1
     while step < size:
         bit = (me // step) % 2
-        halves = value.reshape((2, value.shape[0] // 2) + value.shape[1:])
-        keep = lax.dynamic_index_in_dim(halves, bit, 0, keepdims=False)
-        send = lax.dynamic_index_in_dim(halves, 1 - bit, 0, keepdims=False)
+        shape = value.shape
+        halves = value.reshape(shape[:dim] + (2, shape[dim] // 2) + shape[dim + 1 :])
+        keep = lax.dynamic_index_in_dim(halves, bit, dim, keepdims=False)
+        send = lax.dynamic_index_in_dim(halves, 1 - bit, dim, keepdims=False)
         value = keep + lax.ppermute(send, axis, [(i, i ^ step) for i in range(size)])
         step *= 2
     return value
@@ -188,11 +189,11 @@
     inv_rms = lax.rsqrt(total_sq / D + eps_norm)
     normed = (states * norm_gain.astype(jnp.float32)[None, :] * inv_rms[:, None]).astype(jnp.bfloat16)
     partial_kv = jnp.dot(normed, w_kv, preferred_element_type=jnp.float32)
-    row_part = halve_sum(partial_kv, "dq")
-    part_rows = row_part.shape[0]
-    by_head = jnp.transpose(row_part.reshape(part_rows, 2, KVH, HD), (2, 0, 1, 3))
+    kv_heads = jnp.transpose(partial_kv.reshape(rows_rec, 2, KVH, HD), (2, 0, 1, 3))
+    by_head = halve_sum(kv_heads.reshape(KVH, rows_rec, 2 * HD), "dq", 1)
+    part_rows = by_head.shape[1]
     head_parts = lax.all_to_all(by_head, "dh", split_axis=0, concat_axis=0, tiled=True)
-    head_rows = jnp.sum(head_parts, axis=0).reshape(part_rows, 2 * HD).astype(jnp.bfloat16)
+    head_rows = jnp.sum(head_parts, axis=0).astype(jnp.bfloat16)
     redone = double_gather(head_rows, "dq")
     own_rows = redone.reshape(RET, REC, 2 * HD)
     full_block = fetched.shape[1]

time: 318 us -> 324 us (1.019)
  local copies, waits for them, and re-layouts: 33.8 us -> 41.6 us
    another operation x0 -> x1, local copies, waits for them, and re-layouts: none -> 6.42 us  [halve_sum(): halves = value.reshape(shape[:dim] + (2, shape[dim] // 2) + shape[dim + 1:])]
    unnamed x16 -> x13, local copies, waits for them, and re-layouts: 10 us -> 6.77 us
  transfers between devices with their start and end apart: 8 -> 8, of which waited for: 5 -> 5; matrix products, arithmetic and copies ran while one was open for 14% -> 12% of each run, Pallas kernels for 0% -> 0%
where the time goes in v9:
time: 324 us; the launch traced here: 323 us
  waiting for transfers between devices  186 us (57%)
  local copies, waits for them, and re-layouts  41.6 us (13%)
  Pallas kernels  40.9 us (13%)
  starting transfers between devices  30.4 us (9%)
  other arithmetic  17.9 us (6%)
  matrix products  5.94 us (2%)
    ppermute x2, waiting for transfers between devices, double_gather(): other = lax.ppermute(value, axis, [(i, i ^ step) for i in range(size)])  85.5 us
    ppermute x2, waiting for transfers between devices, halve_sum(): lax.ppermute(send, axis, [(i, i ^ step) for i in range(size)])  77.7 us
    pallas_call x1, Pallas kernels, attention(): pl.pallas_call(kern, grid=(2, n_doc + n_self), in_specs=[pl.BlockSpec((T,...  40.9 us
    all_to_all x1, waiting for transfers between devices, shards(): lax.all_to_all(by_head, 'dh', split_axis=0, concat_axis=0, tiled=True)  15.6 us
    all_to_all x1, starting transfers between devices, shards(): lax.all_to_all(sq_rows, ('dh', 'dq'), split_axis=0, concat_axis=0, tiled=...  11.3 us
    all_to_all x1, waiting for transfers between devices, shards(): lax.all_to_all(sq_rows, ('dh', 'dq'), split_axis=0, concat_axis=0, tiled=...  7.08 us
    unnamed x13, local copies, waits for them, and re-layouts  6.77 us
  transfers between devices with their start and end apart: 8, of which 5 were waited for; matrix products, arithmetic and copies ran while one was open for 12% of the time, Pallas kernels for 0%

profile of v9, /device:TPU:16, one launch (start us, length us, event | category | flops | bytes accessed | tf_op | source)
XLA Modules:
  0.0 323.0 jit_solution(3448778737857572270)
XLA Ops:
  0.0 1.2 fusion.3
  1.9 11.3 %all-to-all-start = ((f32[32,1,512]{2,1,0:T(1,128)}), f32[32,1,512]{2,1,0:T(1,128)S(1)}, u32[]{:S(2)}, u32[]{:S(2)}) async-start(f32[32,1,512]{2,1,0:T(1,128)} %broadcast_in_dim.94), calls=%async_computation | async-start | bytes 131072 | tf_op jit(solution)/shard_map/all_to_all | solution.py:188
  13.3 1.5 copy.41
  16.2 7.1 %all-to-all-done = f32[32,1,512]{2,1,0:T(1,128)S(1)} async-done(((f32[32,1,512]{2,1,0:T(1,128)}), f32[32,1,512]{2,1,0:T(1,128)S(1)}, u32[]{:S(2)}, u32[]{:S(2)}) %all-to-all-start) | async-done | bytes 65568 | tf_op jit(solution)/shard_map/all_to_all | solution.py:188
  23.3 1.7 convolution_bitcast_fusion
  25.1 5.2 %copy.32 = f32[8,512,2,128]{3,2,1,0:T(2,128)} copy(f32[8,512,2,128]{3,1,0,2:T(8,128)S(1)} %convolution_bitcast_fusion) | data formatting | bytes 8388608 | tf_op jit(solution)/shard_map/transpose | solution.py:192
  30.3 6.4 %reshape_reshape.3 = f32[8,2,256,256]{3,2,1,0:T(8,128)} reshape(f32[8,512,2,128]{3,2,1,0:T(2,128)} %copy.32) | data formatting | bytes 8388608 | tf_op jit(solution)/shard_map/reshape;reshape | solution.py:129
  36.7 3.0 dynamic-slice_bitcast_fusion
  39.7 0.9 collective-permute-start
  40.6 1.3 gather_fusion
  43.0 2.0 gather_fusion.1
  45.1 3.3 %select_select_fusion = bf16[8,4,16,2048]{3,2,1,0:T(8,128)(2,1)} fusion(bf16[8,4,16,2048]{3,2,1,0:T(8,128)(2,1)} %bitcast.65, pred[8,4]{1,0:T(8,128)(4,1)S(1)} %copy.34, pred[8,4]{1,0:T(8,128)(4,1)S(1)} %copy.33), kind=kLoop, calls=%fused_computation.9 | loop fusion | flops 2097152 | bytes 4194368 | tf_op jit(solution)/shard_map/jit(_where)/select_n | solution.py:175
  48.3 4.8 %all-to-all-start.2 = ((bf16[8,4,16,2048]{3,2,1,0:T(8,128)(2,1)}), bf16[8,4,16,2048]{3,2,1,0:T(8,128)(2,1)}, u32[]{:S(2)}, u32[]{:S(2)}) async-start(bf16[8,4,16,2048]{3,2,1,0:T(8,128)(2,1)} %select_select_fusion), calls=%async_computation.2 | async-start | bytes 4194304 | tf_op jit(solution)/shard_map/all_to_all | solution.py:180
  53.1 32.9 %collective-permute-done = f32[8,256,256]{2,1,0:T(8,128)} collective-permute-done((f32[8,256,256]{2,1,0:T(8,128)}, f32[8,256,256]{2,1,0:T(8,128)}, u32[]{:S(2)}, u32[]{:S(2)}) %collective-permute-start) | collective-permute-done | bytes 2097184 | tf_op jit(solution)/shard_map/ppermute | solution.py:132
  86.0 2.5 bitcast_add_fusion
  88.6 1.2 collective-permute-start.1
  89.8 44.9 %collective-permute-done.1 = f32[8,128,256]{2,1,0:T(8,128)} collective-permute-done((f32[8,128,256]{2,1,0:T(8,128)S(1)}, f32[8,128,256]{2,1,0:T(8,128)}, u32[]{:S(2)}, u32[]{:S(2)}) %collective-permute-start.1) | collective-permute-done | bytes 1048608 | tf_op jit(solution)/shard_map/ppermute | solution.py:132
  134.7 2.4 bitcast_add_fusion.1
  137.1 3.7 %all-to-all-start.1 = ((f32[8,128,256]{2,1,0:T(8,128)}), f32[8,128,256]{2,1,0:T(8,128)S(1)}, u32[]{:S(2)}, u32[]{:S(2)}) async-start(f32[8,128,256]{2,1,0:T(8,128)} %bitcast_add_fusion.1), calls=%async_computation.1 | async-start | bytes 2097152 | tf_op jit(solution)/shard_map/all_to_all | solution.py:195
  141.0 2.2 gather_fusion.2
  143.7 3.4 %gather_fusion.3 = bf16[32,16,16,2,128]{4,2,3,1,0:T(8,128)(2,1)} fusion(bf16[16,16,2,8,128]{4,1,3,2,0:T(8,128)(2,1)S(1)} %copy_select_fusion, s32[1024]{0:T(1024)S(1)} %pad_clamp_fusion), kind=kCustom, calls=%fused_computation.3 | custom fusion | bytes 8388736 | tf_op jit(solution)/shard_map/jit(_take)/gather | solution.py:33
  147.0 5.6 %copy_bitcast_fusion = bf16[32,16,16,256]{3,2,1,0:T(8,128)(2,1)} fusion(bf16[32,16,16,2,128]{4,2,3,1,0:T(8,128)(2,1)} %gather_fusion.3, pred[32]{0:T(512)(128)(4,1)S(1)} %compare_and_fusion.2), kind=kLoop, calls=%fused_computation.4 | loop fusion | flops 2097152 | bytes 8388640 | tf_op jit(solution)/shard_map/reshape | solution.py:35
  152.6 15.6 %all-to-all-done.1 = f32[8,128,256]{2,1,0:T(8,128)S(1)} async-done(((f32[8,128,256]{2,1,0:T(8,128)}), f32[8,128,256]{2,1,0:T(8,128)S(1)}, u32[]{:S(2)}, u32[]{:S(2)}) %all-to-all-start.1) | async-done | bytes 1048608 | tf_op jit(solution)/shard_map/all_to_all | solution.py:195
  168.2 5.6 %all-to-all-start.3 = ((bf16[32,16,16,256]{3,2,1,0:T(8,128)(2,1)}), bf16[32,16,16,256]{3,2,1,0:T(8,128)(2,1)}, u32[]{:S(2)}, u32[]{:S(2)}) async-start(bf16[32,16,16,256]{3,2,1,0:T(8,128)(2,1)} %copy_bitcast_fusion), calls=%async_computation.3 | async-start | bytes 8388608 | tf_op jit(solution)/shard_map/all_to_all | solution.py:183
  173.8 2.7 collective-permute-start.2
  176.5 5.6 %copy.46 = bf16[128,8,16,128]{3,2,1,0:T(8,128)(2,1)} copy(bf16[128,8,16,128]{3,1,2,0:T(8,128)(2,1)} %bitcast.71) | data formatting | bytes 8388608
  182.1 85.5 %collective-permute-done.2 = bf16[128,256]{1,0:T(8,128)(2,1)S(1)} collective-permute-done((bf16[128,256]{1,0:T(8,128)(2,1)S(1)}, bf16[128,256]{1,0:T(8,128)(2,1)S(1)}, u32[]{:S(2)}, u32[]{:S(2)}) %collective-permute-start.2) | collective-permute-done | bytes 65568 | tf_op jit(solution)/shard_map/ppermute | solution.py:143
  267.9 5.9 %dynamic-slice_reduce_fusion = bf16[1024,2,128]{2,1,0:T(2,128)(2,1)S(1)} fusion(bf16[1024,2,8,128]{3,2,1,0:T(8,128)(2,1)} %bitcast.66, s32[]{:T(128)S(6)} %select_n.226), kind=kLoop, calls=%fused_computation.13 | loop fusion | bytes 1048580 | tf_op jit(solution)/shard_map/jit(dynamic_index_in_dim)/dynamic_slice | solution.py:27
  273.8 0.9 copy.51
  275.2 2.6 copy.38
  277.8 4.2 %convert_select_fusion = bf16[16,512,256]{2,1,0:T(8,128)(2,1)} fusion(bf16[16,512,256]{2,1,0:T(8,128)(2,1)S(1)} %bitcast.62, pred[16,512]{1,0:T(8,128)(4,1)S(1)} %fusion, bf16[16,32,256]{2,1,0:T(8,128)(2,1)S(1)} %bitcast.74, s32[16,32]{1,0:T(8,128)S(1)} %bitcast.78), kind=kOutput, calls=%fused_computation.6 | convolution fusion | flops 138674176 | bytes 8660992 | tf_op jit(solution)/shard_map/kib,kic->kbc/dot_general | solution.py:202
  282.1 40.9 %shard_map.91 = bf16[1024,256]{1,0:T(8,128)(2,1)} custom-call(bf16[1024,256]{1,0:T(8,128)(2,1)} %bitcast.76, bf16[8192,256]{1,0:T(8,128)(2,1)} %bitcast.60, bf16[8192,256]{1,0:T(8,128)(2,1)} %bitcast.61, bf16[1024,256]{1,0:T(8,128)(2,1)} %bitcast.67, bf16[1024,256]{1,0:T(8,128)(2,1)} %bitcast.68), custom_call_target="tpu_custom_call" | custom-call | tf_op jit(solution)/shard_map/pallas_call | solution.py:97
  (47 shorter events, 4.7 us)
Async XLA Ops:
  0.0 43.0 %copy-start = (bf16[32,16,2048]{2,1,0:T(8,128)(2,1)S(1)}, bf16[32,16,2048]{2,1,0:T(8,128)(2,1)}, u32[]{:S(2)}) copy-start(bf16[32,16,2048]{2,1,0:T(8,128)(2,1)} %param.10) | copy-start | bytes 6291460
  1.9 21.3 %all-to-all-start = ((f32[32,1,512]{2,1,0:T(1,128)}), f32[32,1,512]{2,1,0:T(1,128)S(1)}, u32[]{:S(2)}, u32[]{:S(2)}) async-start(f32[32,1,512]{2,1,0:T(1,128)} %broadcast_in_dim.94), calls=%async_computation | async-start | bytes 131072 | tf_op jit(solution)/shard_map/all_to_all | solution.py:188
  36.7 3.9 %copy-start.2 = (s32[256]{0:T(256)S(1)}, s32[256]{0:T(256)}, u32[]{:S(2)}) copy-start(s32[256]{0:T(256)} %param.16) | copy-start | bytes 3076
  36.7 5.3 %copy-start.3 = (s32[8,16]{1,0:T(8,128)S(1)}, s32[8,16]{1,0:T(8,128)}, u32[]{:S(2)}) copy-start(s32[8,16]{1,0:T(8,128)} %param.15) | copy-start | bytes 1540
  39.7 46.2 %collective-permute-start = (f32[8,256,256]{2,1,0:T(8,128)}, f32[8,256,256]{2,1,0:T(8,128)}, u32[]{:S(2)}, u32[]{:S(2)}) collective-permute-start(f32[8,256,256]{2,1,0:T(8,128)} %dynamic-slice_bitcast_fusion), channel_id=1, source_target_pairs={{0,1},{1,0},{2,3},{3,2},{4,5},{5,4},{6,7},{7,6},{8,9},{9,8},{10,11... | collective-permute-start | bytes 6291464 | tf_op jit(solution)/shard_map/ppermute | solution.py:132
  48.3 88.8 %all-to-all-start.2 = ((bf16[8,4,16,2048]{3,2,1,0:T(8,128)(2,1)}), bf16[8,4,16,2048]{3,2,1,0:T(8,128)(2,1)}, u32[]{:S(2)}, u32[]{:S(2)}) async-start(bf16[8,4,16,2048]{3,2,1,0:T(8,128)(2,1)} %select_select_fusion), calls=%async_computation.2 | async-start | bytes 4194304 | tf_op jit(solution)/shard_map/all_to_all | solution.py:180
  88.6 46.1 %collective-permute-start.1 = (f32[8,128,256]{2,1,0:T(8,128)S(1)}, f32[8,128,256]{2,1,0:T(8,128)}, u32[]{:S(2)}, u32[]{:S(2)}) collective-permute-start(f32[8,128,256]{2,1,0:T(8,128)S(1)} %dynamic-slice_bitcast_fusion.1), channel_id=1, source_target_pairs={{0,2},{1,3},{2,0},{3,1},{4,6},{5,7},{6,4},{7,5},{8,10},{9,11},{10,... | collective-permute-start | bytes 3145736 | tf_op jit(solution)/shard_map/ppermute | solution.py:132
  137.1 31.1 %all-to-all-start.1 = ((f32[8,128,256]{2,1,0:T(8,128)}), f32[8,128,256]{2,1,0:T(8,128)S(1)}, u32[]{:S(2)}, u32[]{:S(2)}) async-start(f32[8,128,256]{2,1,0:T(8,128)} %bitcast_add_fusion.1), calls=%async_computation.1 | async-start | bytes 2097152 | tf_op jit(solution)/shard_map/all_to_all | solution.py:195
  168.2 107.0 %all-to-all-start.3 = ((bf16[32,16,16,256]{3,2,1,0:T(8,128)(2,1)}), bf16[32,16,16,256]{3,2,1,0:T(8,128)(2,1)}, u32[]{:S(2)}, u32[]{:S(2)}) async-start(bf16[32,16,16,256]{3,2,1,0:T(8,128)(2,1)} %copy_bitcast_fusion), calls=%async_computation.3 | async-start | bytes 8388608 | tf_op jit(solution)/shard_map/all_to_all | solution.py:183
  173.8 93.8 %collective-permute-start.2 = (bf16[128,256]{1,0:T(8,128)(2,1)S(1)}, bf16[128,256]{1,0:T(8,128)(2,1)S(1)}, u32[]{:S(2)}, u32[]{:S(2)}) collective-permute-start(bf16[128,256]{1,0:T(8,128)(2,1)S(1)} %reduce_sum.47), channel_id=1, source_target_pairs={{0,2},{1,3},{2,0},{3,1},{4,6},{5,7},{6,4},{7,5},{8,10},{9,11},{10,... | collective-permute-start | bytes 196616 | tf_op jit(solution)/shard_map/ppermute | solution.py:143
  176.5 98.2 %copy-start.4 = (s32[1,16,32]{2,1,0:T(8,128)S(1)}, s32[1,16,32]{2,1,0:T(8,128)}, u32[]{:S(2)}) copy-start(s32[1,16,32]{2,1,0:T(8,128)} %param.17) | copy-start | bytes 6148
  267.6 7.4 %collective-permute-start.3 = (bf16[256,256]{1,0:T(8,128)(2,1)S(1)}, bf16[256,256]{1,0:T(8,128)(2,1)S(1)}, u32[]{:S(2)}, u32[]{:S(2)}) collective-permute-start(bf16[256,256]{1,0:T(8,128)(2,1)S(1)} %maximum_select_fusion.1), channel_id=1, source_target_pairs={{0,1},{1,0},{2,3},{3,2},{4,5},{5,4},{6,7},{7,6},{8,9},{9,8},{10,11... | collective-permute-start | bytes 393224 | tf_op jit(solution)/shard_map/ppermute | solution.py:143
  282.1 41.0 %copy-start.1 = (bf16[32,16,2048]{2,1,0:T(8,128)(2,1)S(1)}, bf16[32,16,2048]{2,1,0:T(8,128)(2,1)}, u32[]{:S(2)}) copy-start(bf16[32,16,2048]{2,1,0:T(8,128)(2,1)} %param.10) | copy-start | bytes 6291460

commit v10 on v9

--- a/solution.py
+++ b/solution.py
@@ -16,6 +16,7 @@
 CAP = 4
 REC = 32
 DOC_GRP = 32
+DEV = ("xh", "xl", "zh", "zq1", "zq0")
 
 
 eps_norm = 1e-05
@@ -150,9 +151,9 @@
 
 def shards(queries, store_kv, self_kv, rec_states, norm_gain, w_kv, retrieval, doc_home, rec_index):
     groups = lax.axis_size("cache")
-    members = lax.axis_size("dh") * lax.axis_size("dq")
+    members = lax.axis_size(DEV)
     my_group = lax.axis_index("cache")
-    my_member = lax.axis_index("dh") * lax.axis_size("dq") + lax.axis_index("dq")
+    my_member = lax.axis_index(DEV)
     per_device = QH // members
     ratio_heads = QH // KVH
     my_head = my_member * per_device // ratio_heads
@@ -180,21 +181,25 @@
     arrived = lax.all_to_all(outgoing, "cache", split_axis=0, concat_axis=0, tiled=True)
     compact = jnp.take(arrived.reshape(groups * CAP, shard_rows, kv_width), slot_place, axis=0)
     spread = pick_heads(compact, KVH, HD, dest_heads)
-    fetched = lax.all_to_all(spread, ("dh", "dq"), split_axis=0, concat_axis=2, tiled=True)[0]
+    fetched = lax.all_to_all(spread, DEV, split_axis=0, concat_axis=2, tiled=True)[0]
     states = rec_states[0].astype(jnp.float32)
     rows_rec = states.shape[0]
     partial_sq = jnp.sum(states * states, axis=1)
     sq_rows = jnp.broadcast_to(partial_sq[None, :], (members, rows_rec))
-    total_sq = jnp.sum(lax.all_to_all(sq_rows, ("dh", "dq"), split_axis=0, concat_axis=0, tiled=True), axis=0)
+    total_sq = jnp.sum(lax.all_to_all(sq_rows, DEV, split_axis=0, concat_axis=0, tiled=True), axis=0)
     inv_rms = lax.rsqrt(total_sq / D + eps_norm)
     normed = (states * norm_gain.astype(jnp.float32)[None, :] * inv_rms[:, None]).astype(jnp.bfloat16)
     partial_kv = jnp.dot(normed, w_kv, preferred_element_type=jnp.float32)
-    kv_heads = jnp.transpose(partial_kv.reshape(rows_rec, 2, KVH, HD), (2, 0, 1, 3))
-    by_head = halve_sum(kv_heads.reshape(KVH, rows_rec, 2 * HD), "dq", 1)
-    part_rows = by_head.shape[1]
-    head_parts = lax.all_to_all(by_head, "dh", split_axis=0, concat_axis=0, tiled=True)
-    head_rows = jnp.sum(head_parts, axis=0).astype(jnp.bfloat16)
-    redone = double_gather(head_rows, "dq")
+    row_part = halve_sum(partial_kv, "zq0")
+    half_rows = row_part.shape[0]
+    by_bits = row_part.reshape(half_rows, 2, 2, 2, 2, HD)
+    head_part = halve_sum(by_bits, "xl", 3)
+    part_rows = half_rows // 2
+    by_dest = jnp.transpose(head_part.reshape(2, part_rows, 2, 2, 2, HD), (3, 4, 0, 1, 2, 5))
+    by_dest = by_dest.reshape(KVH, part_rows, 2, HD)
+    head_parts = lax.all_to_all(by_dest, ("xh", "zh", "zq1"), split_axis=0, concat_axis=0, tiled=True)
+    head_rows = jnp.sum(head_parts, axis=0).reshape(part_rows, 2 * HD).astype(jnp.bfloat16)
+    redone = double_gather(head_rows, ("zq1", "zq0"))
     own_rows = redone.reshape(RET, REC, 2 * HD)
     full_block = fetched.shape[1]
     positions = rec_index[0]
@@ -209,10 +214,9 @@
 
 
 def solution(mesh):
-    dev = ("dh", "dq")
+    dev = DEV
     groups = mesh.shape["cache"]
-    members = mesh.shape["dev"]
-    view = Mesh(mesh.devices.reshape(groups, KVH, members // KVH), ("cache", "dh", "dq"))
+    view = Mesh(mesh.devices.reshape((groups,) + (2,) * len(DEV)), ("cache",) + DEV)
     placed = (
         P("cache", None, dev),
         P("cache", dev, None),

time: 324 us -> 300 us (0.926)
  waiting for transfers between devices: 186 us -> 158 us
  starting transfers between devices: 30.4 us -> 35 us
    ppermute x2, waiting for transfers between devices: 77.7 us -> 53.8 us  [halve_sum(): lax.ppermute(send, axis, [(i, i ^ step) for i in range(size)])]
    dynamic_slice x0 -> x3, local copies, waits for them, and re-layouts: none -> 6.63 us  [the longest x2 4.08 us: halve_sum(): keep = lax.dynamic_index_in_dim(halves, bit, dim, keepdims=False)]
    another operation x1 -> x0, local copies, waits for them, and re-layouts: 6.42 us -> none  [halve_sum(): halves = value.reshape(shape[:dim] + (2, shape[dim] // 2) + shape[dim + 1:])]
    all_to_all x3, starting transfers between devices: 20.6 us -> 25.6 us  [the longest x1 11.3 us: shards(): lax.all_to_all(sq_rows, DEV, split_axis=0, concat_axis=0, tiled=True)]
    all_to_all x3, waiting for transfers between devices: 22.7 us -> 18 us  [the longest x1 9.42 us: shards(): lax.all_to_all(by_dest, ('xh', 'zh', 'zq1'), split_axis=0, concat_axis=0,...]
    transpose x1, local copies, waits for them, and re-layouts: 5.21 us -> 1.05 us  [shards(): jnp.transpose(head_part.reshape(2, part_rows, 2, 2, 2, HD), (3, 4, 0, 1,...]
  transfers between devices with their start and end apart: 8 -> 8, of which waited for: 5 -> 5; matrix products, arithmetic and copies ran while one was open for 12% -> 17% of each run, Pallas kernels for 0% -> 0%
where the time goes in v10:
time: 300 us; the launch traced here: 299 us
  waiting for transfers between devices  158 us (53%)
  Pallas kernels  40.8 us (14%)
  local copies, waits for them, and re-layouts  39.6 us (13%)
  starting transfers between devices  35 us (12%)
  other arithmetic  19.8 us (7%)
  matrix products  6.3 us (2%)
    ppermute x2, waiting for transfers between devices, double_gather(): other = lax.ppermute(value, axis, [(i, i ^ step) for i in range(size)])  86 us
    ppermute x2, waiting for transfers between devices, halve_sum(): lax.ppermute(send, axis, [(i, i ^ step) for i in range(size)])  53.8 us
    pallas_call x1, Pallas kernels, attention(): pl.pallas_call(kern, grid=(2, n_doc + n_self), in_specs=[pl.BlockSpec((T,...  40.8 us
    all_to_all x1, starting transfers between devices, shards(): lax.all_to_all(sq_rows, DEV, split_axis=0, concat_axis=0, tiled=True)  11.3 us
    all_to_all x1, starting transfers between devices, shards(): lax.all_to_all(spread, DEV, split_axis=0, concat_axis=2, tiled=True)[0]  10 us
    all_to_all x1, waiting for transfers between devices, shards(): lax.all_to_all(by_dest, ('xh', 'zh', 'zq1'), split_axis=0, concat_axis=0,...  9.42 us
    unnamed x13, local copies, waits for them, and re-layouts  8.69 us
    all_to_all x1, waiting for transfers between devices, shards(): lax.all_to_all(sq_rows, DEV, split_axis=0, concat_axis=0, tiled=True)  8.57 us
  transfers between devices with their start and end apart: 8, of which 5 were waited for; matrix products, arithmetic and copies ran while one was open for 17% of the time, Pallas kernels for 0%

profile of v10, /device:TPU:16, one launch (start us, length us, event | category | flops | bytes accessed | tf_op | source)
XLA Modules:
  0.0 299.4 jit_solution(11182768430588803277)
XLA Ops:
  0.0 1.2 multiply_reduce_fusion
  1.9 11.3 %all-to-all-start = ((f32[32,1,512]{2,1,0:T(1,128)}), f32[32,1,512]{2,1,0:T(1,128)S(1)}, u32[]{:S(2)}, u32[]{:S(2)}) async-start(f32[32,1,512]{2,1,0:T(1,128)} %broadcast_in_dim.94), calls=%async_computation | async-start | bytes 131072 | tf_op jit(solution)/shard_map/all_to_all | solution.py:189
  14.7 8.6 %all-to-all-done = f32[32,1,512]{2,1,0:T(1,128)S(1)} async-done(((f32[32,1,512]{2,1,0:T(1,128)}), f32[32,1,512]{2,1,0:T(1,128)S(1)}, u32[]{:S(2)}, u32[]{:S(2)}) %all-to-all-start) | async-done | bytes 65568 | tf_op jit(solution)/shard_map/all_to_all | solution.py:189
  23.4 2.1 fusion
  25.4 1.9 copy-done.2
  27.4 1.4 dynamic-slice_bitcast_fusion
  29.7 1.3 gather_fusion
  32.1 2.0 gather_fusion.1
  34.1 3.3 %select_select_fusion = bf16[8,4,16,2048]{3,2,1,0:T(8,128)(2,1)} fusion(bf16[8,4,16,2048]{3,2,1,0:T(8,128)(2,1)} %bitcast.61, pred[8,4]{1,0:T(8,128)(4,1)S(1)} %copy.79, pred[8,4]{1,0:T(8,128)(4,1)S(1)} %copy.78), kind=kLoop, calls=%fused_computation.8 | loop fusion | flops 2097152 | bytes 4194368 | tf_op jit(solution)/shard_map/jit(_where)/select_n | solution.py:176
  37.4 4.8 %all-to-all-start.2 = ((bf16[8,4,16,2048]{3,2,1,0:T(8,128)(2,1)}), bf16[8,4,16,2048]{3,2,1,0:T(8,128)(2,1)}, u32[]{:S(2)}, u32[]{:S(2)}) async-start(bf16[8,4,16,2048]{3,2,1,0:T(8,128)(2,1)} %select_select_fusion), calls=%async_computation.2 | async-start | bytes 4194304 | tf_op jit(solution)/shard_map/all_to_all | solution.py:181
  42.2 32.9 %collective-permute-done = f32[256,2048]{1,0:T(8,128)} collective-permute-done((f32[256,2048]{1,0:T(8,128)}, f32[256,2048]{1,0:T(8,128)}, u32[]{:S(2)}, u32[]{:S(2)}) %collective-permute-start) | collective-permute-done | bytes 2097184 | tf_op jit(solution)/shard_map/ppermute | solution.py:133
  75.1 3.9 %bitcast_add_fusion = f32[256,2048]{1,0:T(8,128)} fusion(f32[256,2048]{1,0:T(8,128)} %collective-permute-done, f32[2,256,2048]{2,1,0:T(8,128)} %copy-done.2, s32[]{:T(128)S(6)} %select_n.203), kind=kLoop, calls=%fused_computation.7 | loop fusion | flops 524288 | bytes 6291460 | tf_op jit(solution)/shard_map/add | solution.py:133
  78.9 3.0 copy.72
  81.9 2.8 constant_dynamic-slice_fusion.3
  84.6 2.5 copy.74
  87.8 1.3 copy.73
  89.1 20.9 %collective-permute-done.1 = f32[256,2,2,1,2,128]{5,0,4,3,2,1:T(8,128)} collective-permute-done((f32[256,2,2,1,2,128]{5,0,4,3,2,1:T(8,128)}, f32[256,2,2,1,2,128]{5,0,4,3,2,1:T(8,128)}, u32[]{:S(2)}, u32[]{:S(2)}) %collective-permute-start.1) | collective-permute-done | bytes 1048608 | tf_op jit(solution)/shard_map/ppermute | solution.py:133
  110.0 1.6 bitcast_add_fusion.1
  112.7 4.2 %all-to-all-start.1 = ((f32[8,128,2,128]{3,1,2,0:T(8,128)}), f32[8,128,2,128]{3,1,2,0:T(8,128)}, u32[]{:S(2)}, u32[]{:S(2)}) async-start(f32[8,128,2,128]{3,1,2,0:T(8,128)} %bitcast.11), calls=%async_computation.1 | async-start | bytes 2097152 | tf_op jit(solution)/shard_map/all_to_all | solution.py:200
  117.1 2.2 gather_fusion.2
  119.8 3.4 %gather_fusion.3 = bf16[32,16,16,2,128]{4,2,3,1,0:T(8,128)(2,1)} fusion(bf16[16,16,2,8,128]{4,1,3,2,0:T(8,128)(2,1)S(1)} %copy_select_fusion, s32[1024]{0:T(1024)S(1)} %pad_clamp_fusion), kind=kCustom, calls=%fused_computation.3 | custom fusion | bytes 8388736 | tf_op jit(solution)/shard_map/jit(_take)/gather | solution.py:34
  123.2 5.6 %copy_bitcast_fusion = bf16[32,16,16,256]{3,2,1,0:T(8,128)(2,1)} fusion(bf16[32,16,16,2,128]{4,2,3,1,0:T(8,128)(2,1)} %gather_fusion.3, pred[32]{0:T(512)(128)(4,1)S(1)} %compare_and_fusion.2), kind=kLoop, calls=%fused_computation.4 | loop fusion | flops 2097152 | bytes 8388640 | tf_op jit(solution)/shard_map/reshape | solution.py:36
  128.7 9.4 %all-to-all-done.1 = f32[8,128,2,128]{3,1,2,0:T(8,128)} async-done(((f32[8,128,2,128]{3,1,2,0:T(8,128)}), f32[8,128,2,128]{3,1,2,0:T(8,128)}, u32[]{:S(2)}, u32[]{:S(2)}) %all-to-all-start.1) | async-done | bytes 1048608 | tf_op jit(solution)/shard_map/all_to_all | solution.py:200
  138.2 10.0 %all-to-all-start.3 = ((bf16[32,16,16,256]{3,2,1,0:T(8,128)(2,1)}), bf16[32,16,16,256]{3,2,1,0:T(8,128)(2,1)}, u32[]{:S(2)}, u32[]{:S(2)}) async-start(bf16[32,16,16,256]{3,2,1,0:T(8,128)(2,1)} %copy_bitcast_fusion), calls=%async_computation.3 | async-start | bytes 8388608 | tf_op jit(solution)/shard_map/all_to_all | solution.py:184
  148.2 1.3 reduce_sum.47
  149.6 2.7 collective-permute-start.2
  152.3 5.6 %copy.89 = bf16[128,8,16,128]{3,2,1,0:T(8,128)(2,1)} copy(bf16[128,8,16,128]{3,1,2,0:T(8,128)(2,1)} %bitcast.68) | data formatting | bytes 8388608
  157.9 86.0 %collective-permute-done.2 = bf16[128,256]{0,1:T(8,128)(2,1)S(1)} collective-permute-done((bf16[128,256]{0,1:T(8,128)(2,1)S(1)}, bf16[128,256]{0,1:T(8,128)(2,1)S(1)}, u32[]{:S(2)}, u32[]{:S(2)}) %collective-permute-start.2) | collective-permute-done | bytes 65568 | tf_op jit(solution)/shard_map/ppermute | solution.py:144
  244.3 5.9 %dynamic-slice_reduce_fusion = bf16[1024,2,128]{2,1,0:T(2,128)(2,1)S(1)} fusion(bf16[1024,2,8,128]{3,2,1,0:T(8,128)(2,1)} %bitcast.62, s32[]{:T(128)S(6)} %select_n.232), kind=kLoop, calls=%fused_computation.14 | loop fusion | bytes 1048580 | tf_op jit(solution)/shard_map/jit(dynamic_index_in_dim)/dynamic_slice | solution.py:28
  251.8 2.6 copy.83
  254.4 4.2 %convert_select_fusion = bf16[16,512,256]{2,1,0:T(8,128)(2,1)} fusion(bf16[16,512,256]{2,1,0:T(8,128)(2,1)S(1)} %bitcast.59, pred[16,512]{1,0:T(8,128)(4,1)S(1)} %fusion.2, bf16[16,32,256]{2,1,0:T(8,128)(2,1)S(1)} %bitcast.71, s32[16,32]{1,0:T(8,128)S(1)} %bitcast.77), kind=kOutput, calls=%fused_computation.6 | convolution fusion | flops 138674176 | bytes 8660992 | tf_op jit(solution)/shard_map/kib,kic->kbc/dot_general | solution.py:207
  258.6 40.8 %shard_map.91 = bf16[1024,256]{1,0:T(8,128)(2,1)} custom-call(bf16[1024,256]{1,0:T(8,128)(2,1)} %bitcast.73, bf16[8192,256]{1,0:T(8,128)(2,1)} %bitcast.57, bf16[8192,256]{1,0:T(8,128)(2,1)} %bitcast.58, bf16[1024,256]{1,0:T(8,128)(2,1)} %bitcast.63, bf16[1024,256]{1,0:T(8,128)(2,1)} %bitcast.64), custom_call_target="tpu_custom_call" | custom-call | tf_op jit(solution)/shard_map/pallas_call | solution.py:98
  (51 shorter events, 8.4 us)
Async XLA Ops:
  0.0 32.1 %copy-start = (bf16[32,16,2048]{2,1,0:T(8,128)(2,1)S(1)}, bf16[32,16,2048]{2,1,0:T(8,128)(2,1)}, u32[]{:S(2)}) copy-start(bf16[32,16,2048]{2,1,0:T(8,128)(2,1)} %param.10) | copy-start | bytes 6291460
  1.9 21.3 %all-to-all-start = ((f32[32,1,512]{2,1,0:T(1,128)}), f32[32,1,512]{2,1,0:T(1,128)S(1)}, u32[]{:S(2)}, u32[]{:S(2)}) async-start(f32[32,1,512]{2,1,0:T(1,128)} %broadcast_in_dim.94), calls=%async_computation | async-start | bytes 131072 | tf_op jit(solution)/shard_map/all_to_all | solution.py:189
  23.4 6.3 %copy-start.1 = (s32[256]{0:T(256)S(1)}, s32[256]{0:T(256)}, u32[]{:S(2)}) copy-start(s32[256]{0:T(256)} %param.16) | copy-start | bytes 3076
  25.4 1.9 copy-start.2
  27.4 3.7 %copy-start.3 = (s32[8,16]{1,0:T(8,128)S(1)}, s32[8,16]{1,0:T(8,128)}, u32[]{:S(2)}) copy-start(s32[8,16]{1,0:T(8,128)} %param.15) | copy-start | bytes 1540
  28.8 46.3 %collective-permute-start = (f32[256,2048]{1,0:T(8,128)}, f32[256,2048]{1,0:T(8,128)}, u32[]{:S(2)}, u32[]{:S(2)}) collective-permute-start(f32[256,2048]{1,0:T(8,128)} %dynamic-slice_bitcast_fusion), channel_id=1, source_target_pairs={{0,1},{1,0},{2,3},{3,2},{4,5},{5,4},{6,7},{7,6},{8,9},{9,8},{10,11... | collective-permute-start | bytes 6291464 | tf_op jit(solution)/shard_map/ppermute | solution.py:133
  37.4 75.3 %all-to-all-start.2 = ((bf16[8,4,16,2048]{3,2,1,0:T(8,128)(2,1)}), bf16[8,4,16,2048]{3,2,1,0:T(8,128)(2,1)}, u32[]{:S(2)}, u32[]{:S(2)}) async-start(bf16[8,4,16,2048]{3,2,1,0:T(8,128)(2,1)} %select_select_fusion), calls=%async_computation.2 | async-start | bytes 4194304 | tf_op jit(solution)/shard_map/all_to_all | solution.py:181
  87.2 22.9 %collective-permute-start.1 = (f32[256,2,2,1,2,128]{5,0,4,3,2,1:T(8,128)}, f32[256,2,2,1,2,128]{5,0,4,3,2,1:T(8,128)}, u32[]{:S(2)}, u32[]{:S(2)}) collective-permute-start(f32[256,2,2,1,2,128]{5,0,4,3,2,1:T(8,128)} %bitcast.72), channel_id=1, source_target_pairs={{0,8},{8,0},{1,9},{9,1},{2,10},{10,2},{3,11},{11,3},{4,12},{12,4},... | collective-permute-start | bytes 3145736 | tf_op jit(solution)/shard_map/ppermute | solution.py:133
  112.7 25.4 %all-to-all-start.1 = ((f32[8,128,2,128]{3,1,2,0:T(8,128)}), f32[8,128,2,128]{3,1,2,0:T(8,128)}, u32[]{:S(2)}, u32[]{:S(2)}) async-start(f32[8,128,2,128]{3,1,2,0:T(8,128)} %bitcast.11), calls=%async_computation.1 | async-start | bytes 2097152 | tf_op jit(solution)/shard_map/all_to_all | solution.py:200
  138.2 113.6 %all-to-all-start.3 = ((bf16[32,16,16,256]{3,2,1,0:T(8,128)(2,1)}), bf16[32,16,16,256]{3,2,1,0:T(8,128)(2,1)}, u32[]{:S(2)}, u32[]{:S(2)}) async-start(bf16[32,16,16,256]{3,2,1,0:T(8,128)(2,1)} %copy_bitcast_fusion), calls=%async_computation.3 | async-start | bytes 8388608 | tf_op jit(solution)/shard_map/all_to_all | solution.py:184
  149.6 94.3 %collective-permute-start.2 = (bf16[128,256]{0,1:T(8,128)(2,1)S(1)}, bf16[128,256]{0,1:T(8,128)(2,1)S(1)}, u32[]{:S(2)}, u32[]{:S(2)}) collective-permute-start(bf16[128,256]{0,1:T(8,128)(2,1)S(1)} %bitcast.74), channel_id=1, source_target_pairs={{0,2},{1,3},{2,0},{3,1},{4,6},{5,7},{6,4},{7,5},{8,10},{9,11},{10,... | collective-permute-start | bytes 196616 | tf_op jit(solution)/shard_map/ppermute | solution.py:144
  152.3 98.9 %copy-start.4 = (s32[1,16,32]{2,1,0:T(8,128)S(1)}, s32[1,16,32]{2,1,0:T(8,128)}, u32[]{:S(2)}) copy-start(s32[1,16,32]{2,1,0:T(8,128)} %param.17) | copy-start | bytes 6148
  243.9 7.6 %collective-permute-start.3 = (bf16[256,256]{0,1:T(8,128)(2,1)S(1)}, bf16[256,256]{0,1:T(8,128)(2,1)S(1)}, u32[]{:S(2)}, u32[]{:S(2)}) collective-permute-start(bf16[256,256]{0,1:T(8,128)(2,1)S(1)} %maximum_select_fusion.1), channel_id=1, source_target_pairs={{0,1},{1,0},{2,3},{3,2},{4,5},{5,4},{6,7},{7,6},{8,9},{9,8},{10,11... | collective-permute-start | bytes 393224 | tf_op jit(solution)/shard_map/ppermute | solution.py:144

commit v11 on v10

--- a/solution.py
+++ b/solution.py
@@ -189,11 +189,12 @@
     total_sq = jnp.sum(lax.all_to_all(sq_rows, DEV, split_axis=0, concat_axis=0, tiled=True), axis=0)
     inv_rms = lax.rsqrt(total_sq / D + eps_norm)
     normed = (states * norm_gain.astype(jnp.float32)[None, :] * inv_rms[:, None]).astype(jnp.bfloat16)
-    partial_kv = jnp.dot(normed, w_kv, preferred_element_type=jnp.float32)
+    w_rows = w_kv.shape[0]
+    w_order = jnp.transpose(w_kv.reshape(w_rows, 2, 2, 2, 2, HD), (0, 3, 1, 2, 4, 5)).reshape(w_rows, -1)
+    partial_kv = jnp.dot(normed, w_order, preferred_element_type=jnp.float32)
     row_part = halve_sum(partial_kv, "zq0")
     half_rows = row_part.shape[0]
-    by_bits = row_part.reshape(half_rows, 2, 2, 2, 2, HD)
-    head_part = halve_sum(by_bits, "xl", 3)
+    head_part = halve_sum(row_part.reshape(half_rows, 2, -1), "xl", 1)
     part_rows = half_rows // 2
     by_dest = jnp.transpose(head_part.reshape(2, part_rows, 2, 2, 2, HD), (3, 4, 0, 1, 2, 5))
     by_dest = by_dest.reshape(KVH, part_rows, 2, HD)

time: 300 us -> 300 us (level)
  other arithmetic: 19.8 us -> 14.5 us
  waiting for transfers between devices: 158 us -> 162 us
    all_to_all x1, waiting for transfers between devices: 9.42 us -> 17 us  [shards(): lax.all_to_all(by_dest, ('xh', 'zh', 'zq1'), split_axis=0, concat_axis=0,...]
    reshape x0 -> x3, local copies, waits for them, and re-layouts: none -> 5.1 us  [the longest x1 2.58 us: shards(): w_kv.reshape(w_rows, 2, 2, 2, 2, HD)]
    all_to_all x1, starting transfers between devices: 10 us -> 5.05 us  [shards(): lax.all_to_all(spread, DEV, split_axis=0, concat_axis=2, tiled=True)[0]]
    all_to_all x1, waiting for transfers between devices: 8.57 us -> 3.74 us  [shards(): lax.all_to_all(sq_rows, DEV, split_axis=0, concat_axis=0, tiled=True)]
    all_to_all x1, starting transfers between devices: 4.25 us -> 7.41 us  [shards(): lax.all_to_all(by_dest, ('xh', 'zh', 'zq1'), split_axis=0, concat_axis=0,...]
    unnamed x13 -> x19, local copies, waits for them, and re-layouts: 8.69 us -> 8.7 us
  transfers between devices with their start and end apart: 8 -> 8, of which waited for: 5 -> 5; matrix products, arithmetic and copies ran while one was open for 17% -> 16% of each run, Pallas kernels for 0% -> 0%
where the time goes in v11:
time: 300 us; the launch traced here: 299 us
  waiting for transfers between devices  162 us (54%)
  local copies, waits for them, and re-layouts  42.5 us (14%)
  Pallas kernels  40.9 us (14%)
  starting transfers between devices  32.6 us (11%)
  other arithmetic  14.5 us (5%)
  matrix products  6.17 us (2%)
    ppermute x2, waiting for transfers between devices, double_gather(): other = lax.ppermute(value, axis, [(i, i ^ step) for i in range(size)])  86.5 us
    ppermute x2, waiting for transfers between devices, halve_sum(): lax.ppermute(send, axis, [(i, i ^ step) for i in range(size)])  54.7 us
    pallas_call x1, Pallas kernels, attention(): pl.pallas_call(kern, grid=(2, n_doc + n_self), in_specs=[pl.BlockSpec((T,...  40.9 us
    all_to_all x1, waiting for transfers between devices, shards(): lax.all_to_all(by_dest, ('xh', 'zh', 'zq1'), split_axis=0, concat_axis=0,...  17 us
    all_to_all x1, starting transfers between devices, shards(): lax.all_to_all(sq_rows, DEV, split_axis=0, concat_axis=0, tiled=True)  11.3 us
    unnamed x19, local copies, waits for them, and re-layouts  8.7 us
    all_to_all x1, starting transfers between devices, shards(): lax.all_to_all(by_dest, ('xh', 'zh', 'zq1'), split_axis=0, concat_axis=0,...  7.41 us
  transfers between devices with their start and end apart: 8, of which 5 were waited for; matrix products, arithmetic and copies ran while one was open for 16% of the time, Pallas kernels for 0%

profile of v11, /device:TPU:16, one launch (start us, length us, event | category | flops | bytes accessed | tf_op | source)
XLA Modules:
  0.0 299.0 jit_solution(17892119602148872606)
XLA Ops:
  1.9 11.3 %all-to-all-start = ((f32[32,1,512]{2,1,0:T(1,128)}), f32[32,1,512]{2,1,0:T(1,128)S(1)}, u32[]{:S(2)}, u32[]{:S(2)}) async-start(f32[32,1,512]{2,1,0:T(1,128)} %broadcast_in_dim.94), calls=%async_computation | async-start | bytes 131072 | tf_op jit(solution)/shard_map/all_to_all | solution.py:189
  13.3 2.6 reshape.304
  15.9 1.9 copy.81
  17.8 1.6 reshape.347
  19.5 3.7 %all-to-all-done = f32[32,1,512]{2,1,0:T(1,128)S(1)} async-done(((f32[32,1,512]{2,1,0:T(1,128)}), f32[32,1,512]{2,1,0:T(1,128)S(1)}, u32[]{:S(2)}, u32[]{:S(2)}) %all-to-all-start) | async-done | bytes 65568 | tf_op jit(solution)/shard_map/all_to_all | solution.py:189
  23.5 1.9 fusion.15
  25.5 1.9 copy-done.3
  27.4 1.5 dynamic-slice_bitcast_fusion
  29.7 1.3 gather_fusion
  32.1 2.0 gather_fusion.1
  34.2 3.3 %select_select_fusion = bf16[8,4,16,2048]{3,2,1,0:T(8,128)(2,1)} fusion(bf16[8,4,16,2048]{3,2,1,0:T(8,128)(2,1)} %bitcast.60, pred[8,4]{1,0:T(8,128)(4,1)S(1)} %copy.89, pred[8,4]{1,0:T(8,128)(4,1)S(1)} %copy.88), kind=kLoop, calls=%fused_computation.8 | loop fusion | flops 2097152 | bytes 4194368 | tf_op jit(solution)/shard_map/jit(_where)/select_n | solution.py:176
  37.4 4.8 %all-to-all-start.2 = ((bf16[8,4,16,2048]{3,2,1,0:T(8,128)(2,1)}), bf16[8,4,16,2048]{3,2,1,0:T(8,128)(2,1)}, u32[]{:S(2)}, u32[]{:S(2)}) async-start(bf16[8,4,16,2048]{3,2,1,0:T(8,128)(2,1)} %select_select_fusion), calls=%async_computation.2 | async-start | bytes 4194304 | tf_op jit(solution)/shard_map/all_to_all | solution.py:181
  42.2 32.9 %collective-permute-done = f32[256,2048]{1,0:T(8,128)} collective-permute-done((f32[256,2048]{1,0:T(8,128)}, f32[256,2048]{1,0:T(8,128)}, u32[]{:S(2)}, u32[]{:S(2)}) %collective-permute-start) | collective-permute-done | bytes 2097184 | tf_op jit(solution)/shard_map/ppermute | solution.py:133
  75.1 2.6 bitcast_add_fusion
  77.7 1.9 copy.82
  79.5 1.7 constant_dynamic-slice_fusion.3
  81.2 1.3 copy.84
  83.5 21.8 %collective-permute-done.1 = f32[256,1,1024]{2,0,1:T(8,128)S(1)} collective-permute-done((f32[256,1,1024]{2,0,1:T(8,128)}, f32[256,1,1024]{2,0,1:T(8,128)S(1)}, u32[]{:S(2)}, u32[]{:S(2)}) %collective-permute-start.1) | collective-permute-done | bytes 1048608 | tf_op jit(solution)/shard_map/ppermute | solution.py:133
  106.3 1.3 copy.85
  107.6 7.4 %all-to-all-start.1 = ((f32[8,128,2,128]{3,1,2,0:T(8,128)}), f32[8,128,2,128]{3,1,2,0:T(8,128)S(1)}, u32[]{:S(2)}, u32[]{:S(2)}) async-start(f32[8,128,2,128]{3,1,2,0:T(8,128)} %bitcast.10), calls=%async_computation.1 | async-start | bytes 2097152 | tf_op jit(solution)/shard_map/all_to_all | solution.py:201
  115.1 2.2 gather_fusion.2
  117.8 3.4 %gather_fusion.3 = bf16[32,16,16,2,128]{4,2,3,1,0:T(8,128)(2,1)} fusion(bf16[16,16,2,8,128]{4,1,3,2,0:T(8,128)(2,1)S(1)} %copy_select_fusion, s32[1024]{0:T(1024)S(1)} %pad_clamp_fusion), kind=kCustom, calls=%fused_computation.3 | custom fusion | bytes 8388736 | tf_op jit(solution)/shard_map/jit(_take)/gather | solution.py:34
  121.2 5.6 %copy_bitcast_fusion = bf16[32,16,16,256]{3,2,1,0:T(8,128)(2,1)} fusion(bf16[32,16,16,2,128]{4,2,3,1,0:T(8,128)(2,1)} %gather_fusion.3, pred[32]{0:T(512)(128)(4,1)S(1)} %compare_and_fusion.2), kind=kLoop, calls=%fused_computation.4 | loop fusion | flops 2097152 | bytes 8388640 | tf_op jit(solution)/shard_map/reshape | solution.py:36
  126.8 17.0 %all-to-all-done.1 = f32[8,128,2,128]{3,1,2,0:T(8,128)S(1)} async-done(((f32[8,128,2,128]{3,1,2,0:T(8,128)}), f32[8,128,2,128]{3,1,2,0:T(8,128)S(1)}, u32[]{:S(2)}, u32[]{:S(2)}) %all-to-all-start.1) | async-done | bytes 1048608 | tf_op jit(solution)/shard_map/all_to_all | solution.py:201
  143.8 5.0 %all-to-all-start.3 = ((bf16[32,16,16,256]{3,2,1,0:T(8,128)(2,1)}), bf16[32,16,16,256]{3,2,1,0:T(8,128)(2,1)}, u32[]{:S(2)}, u32[]{:S(2)}) async-start(bf16[32,16,16,256]{3,2,1,0:T(8,128)(2,1)} %copy_bitcast_fusion), calls=%async_computation.3 | async-start | bytes 8388608 | tf_op jit(solution)/shard_map/all_to_all | solution.py:184
  149.0 2.4 collective-permute-start.2
  151.4 5.6 %copy.99 = bf16[128,8,16,128]{3,2,1,0:T(8,128)(2,1)} copy(bf16[128,8,16,128]{3,1,2,0:T(8,128)(2,1)} %bitcast.66) | data formatting | bytes 8388608
  157.0 86.5 %collective-permute-done.2 = bf16[128,256]{0,1:T(8,128)(2,1)S(1)} collective-permute-done((bf16[128,256]{0,1:T(8,128)(2,1)S(1)}, bf16[128,256]{0,1:T(8,128)(2,1)S(1)}, u32[]{:S(2)}, u32[]{:S(2)}) %collective-permute-start.2) | collective-permute-done | bytes 65568 | tf_op jit(solution)/shard_map/ppermute | solution.py:144
  243.6 5.9 %dynamic-slice_reduce_fusion = bf16[1024,2,128]{2,1,0:T(2,128)(2,1)S(1)} fusion(bf16[1024,2,8,128]{3,2,1,0:T(8,128)(2,1)} %bitcast.61, s32[]{:T(128)S(6)} %select_n.232), kind=kLoop, calls=%fused_computation.12 | loop fusion | bytes 1048580 | tf_op jit(solution)/shard_map/jit(dynamic_index_in_dim)/dynamic_slice | solution.py:28
  251.1 2.6 copy.93
  253.8 4.2 %convert_select_fusion = bf16[16,512,256]{2,1,0:T(8,128)(2,1)} fusion(bf16[16,512,256]{2,1,0:T(8,128)(2,1)S(1)} %bitcast.58, pred[16,512]{1,0:T(8,128)(4,1)S(1)} %fusion, bf16[16,32,256]{2,1,0:T(8,128)(2,1)S(1)} %bitcast.70, s32[16,32]{1,0:T(8,128)S(1)} %bitcast.77), kind=kOutput, calls=%fused_computation.6 | convolution fusion | flops 138674176 | bytes 8660992 | tf_op jit(solution)/shard_map/kib,kic->kbc/dot_general | solution.py:208
  258.0 40.9 %shard_map.91 = bf16[1024,256]{1,0:T(8,128)(2,1)} custom-call(bf16[1024,256]{1,0:T(8,128)(2,1)} %bitcast.73, bf16[8192,256]{1,0:T(8,128)(2,1)} %bitcast.56, bf16[8192,256]{1,0:T(8,128)(2,1)} %bitcast.57, bf16[1024,256]{1,0:T(8,128)(2,1)} %bitcast.62, bf16[1024,256]{1,0:T(8,128)(2,1)} %bitcast.63), custom_call_target="tpu_custom_call" | custom-call | tf_op jit(solution)/shard_map/pallas_call | solution.py:98
  (61 shorter events, 8.5 us)
Async XLA Ops:
  0.0 32.1 %copy-start = (bf16[32,16,2048]{2,1,0:T(8,128)(2,1)S(1)}, bf16[32,16,2048]{2,1,0:T(8,128)(2,1)}, u32[]{:S(2)}) copy-start(bf16[32,16,2048]{2,1,0:T(8,128)(2,1)} %param.10) | copy-start | bytes 6291460
  0.0 23.4 %copy-start.4 = (bf16[1,512,256]{2,1,0:T(8,128)(2,1)S(1)}, bf16[1,512,256]{2,1,0:T(8,128)(2,1)}, u32[]{:S(2)}) copy-start(bf16[1,512,256]{2,1,0:T(8,128)(2,1)} %param.12) | copy-start | bytes 786436
  0.0 19.4 %copy-start.7 = (bf16[256]{0:T(256)(128)(2,1)S(1)}, bf16[256]{0:T(256)(128)(2,1)}, u32[]{:S(2)}) copy-start(bf16[256]{0:T(256)(128)(2,1)} %param.13) | copy-start | bytes 1540
  0.0 19.4 %copy-start.5 = (s32[8,16]{1,0:T(8,128)S(1)}, s32[8,16]{1,0:T(8,128)}, u32[]{:S(2)}) copy-start(s32[8,16]{1,0:T(8,128)} %param.15) | copy-start | bytes 1540
  1.9 21.3 %all-to-all-start = ((f32[32,1,512]{2,1,0:T(1,128)}), f32[32,1,512]{2,1,0:T(1,128)S(1)}, u32[]{:S(2)}, u32[]{:S(2)}) async-start(f32[32,1,512]{2,1,0:T(1,128)} %broadcast_in_dim.94), calls=%async_computation | async-start | bytes 131072 | tf_op jit(solution)/shard_map/all_to_all | solution.py:189
  23.5 6.2 %copy-start.2 = (s32[256]{0:T(256)S(1)}, s32[256]{0:T(256)}, u32[]{:S(2)}) copy-start(s32[256]{0:T(256)} %param.16) | copy-start | bytes 3076
  25.5 1.9 copy-start.3
  28.9 46.2 %collective-permute-start = (f32[256,2048]{1,0:T(8,128)}, f32[256,2048]{1,0:T(8,128)}, u32[]{:S(2)}, u32[]{:S(2)}) collective-permute-start(f32[256,2048]{1,0:T(8,128)} %dynamic-slice_bitcast_fusion), channel_id=1, source_target_pairs={{0,1},{1,0},{2,3},{3,2},{4,5},{5,4},{6,7},{7,6},{8,9},{9,8},{10,11... | collective-permute-start | bytes 6291464 | tf_op jit(solution)/shard_map/ppermute | solution.py:133
  37.4 70.2 %all-to-all-start.2 = ((bf16[8,4,16,2048]{3,2,1,0:T(8,128)(2,1)}), bf16[8,4,16,2048]{3,2,1,0:T(8,128)(2,1)}, u32[]{:S(2)}, u32[]{:S(2)}) async-start(bf16[8,4,16,2048]{3,2,1,0:T(8,128)(2,1)} %select_select_fusion), calls=%async_computation.2 | async-start | bytes 4194304 | tf_op jit(solution)/shard_map/all_to_all | solution.py:181
  82.5 22.8 %collective-permute-start.1 = (f32[256,1,1024]{2,0,1:T(8,128)}, f32[256,1,1024]{2,0,1:T(8,128)S(1)}, u32[]{:S(2)}, u32[]{:S(2)}) collective-permute-start(f32[256,1,1024]{2,0,1:T(8,128)} %bitcast.71), channel_id=1, source_target_pairs={{0,8},{8,0},{1,9},{9,1},{2,10},{10,2},{3,11},{11,3},{4,12},{12,4},... | collective-permute-start | bytes 3145736 | tf_op jit(solution)/shard_map/ppermute | solution.py:133
  107.6 36.2 %all-to-all-start.1 = ((f32[8,128,2,128]{3,1,2,0:T(8,128)}), f32[8,128,2,128]{3,1,2,0:T(8,128)S(1)}, u32[]{:S(2)}, u32[]{:S(2)}) async-start(f32[8,128,2,128]{3,1,2,0:T(8,128)} %bitcast.10), calls=%async_computation.1 | async-start | bytes 2097152 | tf_op jit(solution)/shard_map/all_to_all | solution.py:201
  143.8 107.4 %all-to-all-start.3 = ((bf16[32,16,16,256]{3,2,1,0:T(8,128)(2,1)}), bf16[32,16,16,256]{3,2,1,0:T(8,128)(2,1)}, u32[]{:S(2)}, u32[]{:S(2)}) async-start(bf16[32,16,16,256]{3,2,1,0:T(8,128)(2,1)} %copy_bitcast_fusion), calls=%async_computation.3 | async-start | bytes 8388608 | tf_op jit(solution)/shard_map/all_to_all | solution.py:184
  149.0 94.5 %collective-permute-start.2 = (bf16[128,256]{0,1:T(8,128)(2,1)S(1)}, bf16[128,256]{0,1:T(8,128)(2,1)S(1)}, u32[]{:S(2)}, u32[]{:S(2)}) collective-permute-start(bf16[128,256]{0,1:T(8,128)(2,1)S(1)} %bitcast.74), channel_id=1, source_target_pairs={{0,2},{1,3},{2,0},{3,1},{4,6},{5,7},{6,4},{7,5},{8,10},{9,11},{10,... | collective-permute-start | bytes 196616 | tf_op jit(solution)/shard_map/ppermute | solution.py:144
  151.4 99.1 %copy-start.6 = (s32[1,16,32]{2,1,0:T(8,128)S(1)}, s32[1,16,32]{2,1,0:T(8,128)}, u32[]{:S(2)}) copy-start(s32[1,16,32]{2,1,0:T(8,128)} %param.17) | copy-start | bytes 6148
  243.5 7.3 %collective-permute-start.3 = (bf16[256,256]{0,1:T(8,128)(2,1)S(1)}, bf16[256,256]{0,1:T(8,128)(2,1)S(1)}, u32[]{:S(2)}, u32[]{:S(2)}) collective-permute-start(bf16[256,256]{0,1:T(8,128)(2,1)S(1)} %maximum_select_fusion.1), channel_id=1, source_target_pairs={{0,1},{1,0},{2,3},{3,2},{4,5},{5,4},{6,7},{7,6},{8,9},{9,8},{10,11... | collective-permute-start | bytes 393224 | tf_op jit(solution)/shard_map/ppermute | solution.py:144
  258.0 41.0 %copy-start.1 = (bf16[32,16,2048]{2,1,0:T(8,128)(2,1)S(1)}, bf16[32,16,2048]{2,1,0:T(8,128)(2,1)}, u32[]{:S(2)}) copy-start(bf16[32,16,2048]{2,1,0:T(8,128)(2,1)} %param.10) | copy-start | bytes 6291460

commit v12 on v10

--- a/solution.py
+++ b/solution.py
@@ -190,11 +190,9 @@
     inv_rms = lax.rsqrt(total_sq / D + eps_norm)
     normed = (states * norm_gain.astype(jnp.float32)[None, :] * inv_rms[:, None]).astype(jnp.bfloat16)
     partial_kv = jnp.dot(normed, w_kv, preferred_element_type=jnp.float32)
-    row_part = halve_sum(partial_kv, "zq0")
-    half_rows = row_part.shape[0]
-    by_bits = row_part.reshape(half_rows, 2, 2, 2, 2, HD)
-    head_part = halve_sum(by_bits, "xl", 3)
-    part_rows = half_rows // 2
+    head_first = halve_sum(partial_kv.reshape(rows_rec, 2, 2, 2, 2, HD), "xl", 3)
+    head_part = halve_sum(head_first, "zq0")
+    part_rows = head_part.shape[0] // 2
     by_dest = jnp.transpose(head_part.reshape(2, part_rows, 2, 2, 2, HD), (3, 4, 0, 1, 2, 5))
     by_dest = by_dest.reshape(KVH, part_rows, 2, HD)
     head_parts = lax.all_to_all(by_dest, ("xh", "zh", "zq1"), split_axis=0, concat_axis=0, tiled=True)

time: 300 us -> 291 us (0.970)
  local copies, waits for them, and re-layouts: 39.6 us -> 32.9 us
    dynamic_slice x3 -> x0, local copies, waits for them, and re-layouts: 6.63 us -> none  [the longest x2 4.08 us: halve_sum(): keep = lax.dynamic_index_in_dim(halves, bit, dim, keepdims=False)]
    unnamed x13 -> x15, local copies, waits for them, and re-layouts: 8.69 us -> 10 us
  transfers between devices with their start and end apart: 8 -> 8, of which waited for: 5 -> 5; matrix products, arithmetic and copies ran while one was open for 17% -> 14% of each run, Pallas kernels for 0% -> 0%
where the time goes in v12:
time: 291 us
  waiting for transfers between devices  157 us (54%)
  Pallas kernels  40.8 us (14%)
  starting transfers between devices  35.3 us (12%)
  local copies, waits for them, and re-layouts  32.9 us (11%)
  other arithmetic  18.3 us (6%)
  matrix products  5.94 us (2%)
    ppermute x2, waiting for transfers between devices, double_gather(): other = lax.ppermute(value, axis, [(i, i ^ step) for i in range(size)])  86 us
    ppermute x2, waiting for transfers between devices, halve_sum(): lax.ppermute(send, axis, [(i, i ^ step) for i in range(size)])  54.6 us
    pallas_call x1, Pallas kernels, attention(): pl.pallas_call(kern, grid=(2, n_doc + n_self), in_specs=[pl.BlockSpec((T,...  40.8 us
    all_to_all x1, starting transfers between devices, shards(): lax.all_to_all(sq_rows, DEV, split_axis=0, concat_axis=0, tiled=True)  11.3 us
    unnamed x15, local copies, waits for them, and re-layouts  10 us
    all_to_all x1, starting transfers between devices, shards(): lax.all_to_all(spread, DEV, split_axis=0, concat_axis=2, tiled=True)[0]  10 us
    all_to_all x1, waiting for transfers between devices, shards(): lax.all_to_all(by_dest, ('xh', 'zh', 'zq1'), split_axis=0, concat_axis=0,...  9.43 us
    all_to_all x1, waiting for transfers between devices, shards(): lax.all_to_all(sq_rows, DEV, split_axis=0, concat_axis=0, tiled=True)  7.08 us
  transfers between devices with their start and end apart: 8, of which 5 were waited for; matrix products, arithmetic and copies ran while one was open for 14% of the time, Pallas kernels for 0%

profile of v12, /device:TPU:16, one launch (start us, length us, event | category | flops | bytes accessed | tf_op | source)
XLA Modules:
  0.0 290.7 jit_solution(18007914144277700601)
XLA Ops:
  0.0 1.2 fusion.3
  1.9 11.3 %all-to-all-start = ((f32[32,1,512]{2,1,0:T(1,128)}), f32[32,1,512]{2,1,0:T(1,128)S(1)}, u32[]{:S(2)}, u32[]{:S(2)}) async-start(f32[32,1,512]{2,1,0:T(1,128)} %broadcast_in_dim.94), calls=%async_computation | async-start | bytes 131072 | tf_op jit(solution)/shard_map/all_to_all | solution.py:189
  13.3 1.5 copy.69
  16.2 7.1 %all-to-all-done = f32[32,1,512]{2,1,0:T(1,128)S(1)} async-done(((f32[32,1,512]{2,1,0:T(1,128)}), f32[32,1,512]{2,1,0:T(1,128)S(1)}, u32[]{:S(2)}, u32[]{:S(2)}) %all-to-all-start) | async-done | bytes 65568 | tf_op jit(solution)/shard_map/all_to_all | solution.py:189
  23.3 1.7 fusion.6
  25.1 1.9 copy-done.2
  27.0 1.4 constant_dynamic-slice_fusion.2
  29.0 1.3 gather_fusion
  31.5 2.0 gather_fusion.1
  33.5 3.3 %select_select_fusion = bf16[8,4,16,2048]{3,2,1,0:T(8,128)(2,1)} fusion(bf16[8,4,16,2048]{3,2,1,0:T(8,128)(2,1)} %bitcast.65, pred[8,4]{1,0:T(8,128)(4,1)S(1)} %copy.62, pred[8,4]{1,0:T(8,128)(4,1)S(1)} %copy.61), kind=kLoop, calls=%fused_computation.7 | loop fusion | flops 2097152 | bytes 4194368 | tf_op jit(solution)/shard_map/jit(_where)/select_n | solution.py:176
  36.8 4.8 %all-to-all-start.2 = ((bf16[8,4,16,2048]{3,2,1,0:T(8,128)(2,1)}), bf16[8,4,16,2048]{3,2,1,0:T(8,128)(2,1)}, u32[]{:S(2)}, u32[]{:S(2)}) async-start(bf16[8,4,16,2048]{3,2,1,0:T(8,128)(2,1)} %select_select_fusion), calls=%async_computation.2 | async-start | bytes 4194304 | tf_op jit(solution)/shard_map/all_to_all | solution.py:181
  41.6 33.1 %collective-permute-done = f32[512,2,2,1,2,128]{5,0,4,3,2,1:T(8,128)} collective-permute-done((f32[512,2,2,1,2,128]{5,0,4,3,2,1:T(8,128)}, f32[512,2,2,1,2,128]{5,0,4,3,2,1:T(8,128)}, u32[]{:S(2)}, u32[]{:S(2)}) %collective-permute-start) | collective-permute-done | bytes 2097184 | tf_op jit(solution)/shard_map/ppermute | solution.py:133
  74.7 2.4 dynamic-slice_add_fusion
  77.1 1.3 copy-done.3
  78.5 1.2 collective-permute-start.1
  79.8 21.5 %collective-permute-done.1 = f32[256,2,2,1,2,128]{5,0,4,2,1,3:T(8,128)} collective-permute-done((f32[256,2,2,1,2,128]{5,0,4,2,1,3:T(8,128)S(1)}, f32[256,2,2,1,2,128]{5,0,4,2,1,3:T(8,128)}, u32[]{:S(2)}, u32[]{:S(2)}) %collective-permute-start.1) | collective-permute-done | bytes 1048608 | tf_op jit(solution)/shard_map/ppermute | solution.py:133
  101.3 1.7 bitcast_add_fusion
  102.9 1.0 copy.57
  104.0 4.2 %all-to-all-start.1 = ((f32[8,128,2,128]{3,1,2,0:T(8,128)}), f32[8,128,2,128]{3,1,2,0:T(8,128)}, u32[]{:S(2)}, u32[]{:S(2)}) async-start(f32[8,128,2,128]{3,1,2,0:T(8,128)} %copy.57), calls=%async_computation.1 | async-start | bytes 2097152 | tf_op jit(solution)/shard_map/all_to_all | solution.py:198
  108.3 2.2 gather_fusion.2
  111.0 3.4 %gather_fusion.3 = bf16[32,16,16,2,128]{4,2,3,1,0:T(8,128)(2,1)} fusion(bf16[16,16,2,8,128]{4,1,3,2,0:T(8,128)(2,1)S(1)} %copy_select_fusion, s32[1024]{0:T(1024)S(1)} %pad_clamp_fusion), kind=kCustom, calls=%fused_computation.3 | custom fusion | bytes 8388736 | tf_op jit(solution)/shard_map/jit(_take)/gather | solution.py:34
  114.4 5.6 %copy_bitcast_fusion = bf16[32,16,16,256]{3,2,1,0:T(8,128)(2,1)} fusion(bf16[32,16,16,2,128]{4,2,3,1,0:T(8,128)(2,1)} %gather_fusion.3, pred[32]{0:T(512)(128)(4,1)S(1)} %compare_and_fusion.2), kind=kLoop, calls=%fused_computation.4 | loop fusion | flops 2097152 | bytes 8388640 | tf_op jit(solution)/shard_map/reshape | solution.py:36
  120.0 9.4 %all-to-all-done.1 = f32[8,128,2,128]{3,1,2,0:T(8,128)} async-done(((f32[8,128,2,128]{3,1,2,0:T(8,128)}), f32[8,128,2,128]{3,1,2,0:T(8,128)}, u32[]{:S(2)}, u32[]{:S(2)}) %all-to-all-start.1) | async-done | bytes 1048608 | tf_op jit(solution)/shard_map/all_to_all | solution.py:198
  129.4 10.0 %all-to-all-start.3 = ((bf16[32,16,16,256]{3,2,1,0:T(8,128)(2,1)}), bf16[32,16,16,256]{3,2,1,0:T(8,128)(2,1)}, u32[]{:S(2)}, u32[]{:S(2)}) async-start(bf16[32,16,16,256]{3,2,1,0:T(8,128)(2,1)} %copy_bitcast_fusion), calls=%async_computation.3 | async-start | bytes 8388608 | tf_op jit(solution)/shard_map/all_to_all | solution.py:184
  139.4 1.3 reduce_sum.47
  140.8 2.7 collective-permute-start.2
  143.5 5.6 %copy.75 = bf16[128,8,16,128]{3,2,1,0:T(8,128)(2,1)} copy(bf16[128,8,16,128]{3,1,2,0:T(8,128)(2,1)} %bitcast.71) | data formatting | bytes 8388608
  149.1 86.0 %collective-permute-done.2 = bf16[128,256]{0,1:T(8,128)(2,1)S(1)} collective-permute-done((bf16[128,256]{0,1:T(8,128)(2,1)S(1)}, bf16[128,256]{0,1:T(8,128)(2,1)S(1)}, u32[]{:S(2)}, u32[]{:S(2)}) %collective-permute-start.2) | collective-permute-done | bytes 65568 | tf_op jit(solution)/shard_map/ppermute | solution.py:144
  235.5 5.9 %dynamic-slice_reduce_fusion = bf16[1024,2,128]{2,1,0:T(2,128)(2,1)S(1)} fusion(bf16[1024,2,8,128]{3,2,1,0:T(8,128)(2,1)} %bitcast.66, s32[]{:T(128)S(6)} %select_n.232), kind=kLoop, calls=%fused_computation.11 | loop fusion | bytes 1048580 | tf_op jit(solution)/shard_map/jit(dynamic_index_in_dim)/dynamic_slice | solution.py:28
  243.0 2.6 copy.66
  245.7 4.2 %convert_select_fusion = bf16[16,512,256]{2,1,0:T(8,128)(2,1)} fusion(bf16[16,512,256]{2,1,0:T(8,128)(2,1)S(1)} %bitcast.62, pred[16,512]{1,0:T(8,128)(4,1)S(1)} %fusion, bf16[16,32,256]{2,1,0:T(8,128)(2,1)S(1)} %bitcast.75, s32[16,32]{1,0:T(8,128)S(1)} %bitcast.81), kind=kOutput, calls=%fused_computation.6 | convolution fusion | flops 138674176 | bytes 8660992 | tf_op jit(solution)/shard_map/kib,kic->kbc/dot_general | solution.py:205
  249.9 40.8 %shard_map.91 = bf16[1024,256]{1,0:T(8,128)(2,1)} custom-call(bf16[1024,256]{1,0:T(8,128)(2,1)} %bitcast.77, bf16[8192,256]{1,0:T(8,128)(2,1)} %bitcast.60, bf16[8192,256]{1,0:T(8,128)(2,1)} %bitcast.61, bf16[1024,256]{1,0:T(8,128)(2,1)} %bitcast.67, bf16[1024,256]{1,0:T(8,128)(2,1)} %bitcast.68), custom_call_target="tpu_custom_call" | custom-call | tf_op jit(solution)/shard_map/pallas_call | solution.py:98
  (50 shorter events, 6.6 us)
Async XLA Ops:
  0.0 31.5 %copy-start = (bf16[32,16,2048]{2,1,0:T(8,128)(2,1)S(1)}, bf16[32,16,2048]{2,1,0:T(8,128)(2,1)}, u32[]{:S(2)}) copy-start(bf16[32,16,2048]{2,1,0:T(8,128)(2,1)} %param.10) | copy-start | bytes 6291460
  1.9 21.3 %all-to-all-start = ((f32[32,1,512]{2,1,0:T(1,128)}), f32[32,1,512]{2,1,0:T(1,128)S(1)}, u32[]{:S(2)}, u32[]{:S(2)}) async-start(f32[32,1,512]{2,1,0:T(1,128)} %broadcast_in_dim.94), calls=%async_computation | async-start | bytes 131072 | tf_op jit(solution)/shard_map/all_to_all | solution.py:189
  23.3 5.7 %copy-start.1 = (s32[256]{0:T(256)S(1)}, s32[256]{0:T(256)}, u32[]{:S(2)}) copy-start(s32[256]{0:T(256)} %param.16) | copy-start | bytes 3076
  25.1 1.9 copy-start.2
  27.0 3.4 %copy-start.4 = (s32[8,16]{1,0:T(8,128)S(1)}, s32[8,16]{1,0:T(8,128)}, u32[]{:S(2)}) copy-start(s32[8,16]{1,0:T(8,128)} %param.15) | copy-start | bytes 1540
  28.4 46.3 %collective-permute-start = (f32[512,2,2,1,2,128]{5,0,4,3,2,1:T(8,128)}, f32[512,2,2,1,2,128]{5,0,4,3,2,1:T(8,128)}, u32[]{:S(2)}, u32[]{:S(2)}) collective-permute-start(f32[512,2,2,1,2,128]{5,0,4,3,2,1:T(8,128)} %constant_dynamic-slice_fusion.2), channel_id=1, source_target_pairs={{0,8},{8,0},{1,9},{9,1},{2,10},{10,2},{3,11},{11,3},{4,12},{12,4},... | collective-permute-start | bytes 6291464 | tf_op jit(solution)/shard_map/ppermute | solution.py:133
  36.8 67.2 %all-to-all-start.2 = ((bf16[8,4,16,2048]{3,2,1,0:T(8,128)(2,1)}), bf16[8,4,16,2048]{3,2,1,0:T(8,128)(2,1)}, u32[]{:S(2)}, u32[]{:S(2)}) async-start(bf16[8,4,16,2048]{3,2,1,0:T(8,128)(2,1)} %select_select_fusion), calls=%async_computation.2 | async-start | bytes 4194304 | tf_op jit(solution)/shard_map/all_to_all | solution.py:181
  77.1 1.4 copy-start.3
  78.5 22.7 %collective-permute-start.1 = (f32[256,2,2,1,2,128]{5,0,4,2,1,3:T(8,128)S(1)}, f32[256,2,2,1,2,128]{5,0,4,2,1,3:T(8,128)}, u32[]{:S(2)}, u32[]{:S(2)}) collective-permute-start(f32[256,2,2,1,2,128]{5,0,4,2,1,3:T(8,128)S(1)} %dynamic-slice_bitcast_fusion), channel_id=1, source_target_pairs={{0,1},{1,0},{2,3},{3,2},{4,5},{5,4},{6,7},{7,6},{8,9},{9,8},{10,11... | collective-permute-start | bytes 3145736 | tf_op jit(solution)/shard_map/ppermute | solution.py:133
  104.0 25.4 %all-to-all-start.1 = ((f32[8,128,2,128]{3,1,2,0:T(8,128)}), f32[8,128,2,128]{3,1,2,0:T(8,128)}, u32[]{:S(2)}, u32[]{:S(2)}) async-start(f32[8,128,2,128]{3,1,2,0:T(8,128)} %copy.57), calls=%async_computation.1 | async-start | bytes 2097152 | tf_op jit(solution)/shard_map/all_to_all | solution.py:198
  129.4 113.6 %all-to-all-start.3 = ((bf16[32,16,16,256]{3,2,1,0:T(8,128)(2,1)}), bf16[32,16,16,256]{3,2,1,0:T(8,128)(2,1)}, u32[]{:S(2)}, u32[]{:S(2)}) async-start(bf16[32,16,16,256]{3,2,1,0:T(8,128)(2,1)} %copy_bitcast_fusion), calls=%async_computation.3 | async-start | bytes 8388608 | tf_op jit(solution)/shard_map/all_to_all | solution.py:184
  140.8 94.3 %collective-permute-start.2 = (bf16[128,256]{0,1:T(8,128)(2,1)S(1)}, bf16[128,256]{0,1:T(8,128)(2,1)S(1)}, u32[]{:S(2)}, u32[]{:S(2)}) collective-permute-start(bf16[128,256]{0,1:T(8,128)(2,1)S(1)} %bitcast.78), channel_id=1, source_target_pairs={{0,2},{1,3},{2,0},{3,1},{4,6},{5,7},{6,4},{7,5},{8,10},{9,11},{10,... | collective-permute-start | bytes 196616 | tf_op jit(solution)/shard_map/ppermute | solution.py:144
  143.5 98.9 %copy-start.5 = (s32[1,16,32]{2,1,0:T(8,128)S(1)}, s32[1,16,32]{2,1,0:T(8,128)}, u32[]{:S(2)}) copy-start(s32[1,16,32]{2,1,0:T(8,128)} %param.17) | copy-start | bytes 6148
  235.1 7.6 %collective-permute-start.3 = (bf16[256,256]{0,1:T(8,128)(2,1)S(1)}, bf16[256,256]{0,1:T(8,128)(2,1)S(1)}, u32[]{:S(2)}, u32[]{:S(2)}) collective-permute-start(bf16[256,256]{0,1:T(8,128)(2,1)S(1)} %maximum_select_fusion.1), channel_id=1, source_target_pairs={{0,1},{1,0},{2,3},{3,2},{4,5},{5,4},{6,7},{7,6},{8,9},{9,8},{10,11... | collective-permute-start | bytes 393224 | tf_op jit(solution)/shard_map/ppermute | solution.py:144

commit v13 on v12

--- a/solution.py
+++ b/solution.py
@@ -191,11 +191,11 @@
     normed = (states * norm_gain.astype(jnp.float32)[None, :] * inv_rms[:, None]).astype(jnp.bfloat16)
     partial_kv = jnp.dot(normed, w_kv, preferred_element_type=jnp.float32)
     head_first = halve_sum(partial_kv.reshape(rows_rec, 2, 2, 2, 2, HD), "xl", 3)
-    head_part = halve_sum(head_first, "zq0")
-    part_rows = head_part.shape[0] // 2
-    by_dest = jnp.transpose(head_part.reshape(2, part_rows, 2, 2, 2, HD), (3, 4, 0, 1, 2, 5))
-    by_dest = by_dest.reshape(KVH, part_rows, 2, HD)
-    head_parts = lax.all_to_all(by_dest, ("xh", "zh", "zq1"), split_axis=0, concat_axis=0, tiled=True)
+    quarter = halve_sum(halve_sum(head_first, "zq0"), "zq1")
+    part_rows = quarter.shape[0]
+    by_dest = jnp.transpose(quarter.reshape(part_rows, 2, 2, 2, HD), (2, 3, 0, 1, 4))
+    by_dest = by_dest.reshape(-1, part_rows, 2, HD)
+    head_parts = lax.all_to_all(by_dest, ("xh", "zh"), split_axis=0, concat_axis=0, tiled=True)
     head_rows = jnp.sum(head_parts, axis=0).reshape(part_rows, 2 * HD).astype(jnp.bfloat16)
     redone = double_gather(head_rows, ("zq1", "zq0"))
     own_rows = redone.reshape(RET, REC, 2 * HD)

time: 291 us -> 303 us (1.041)
  waiting for transfers between devices: 157 us -> 173 us
    ppermute x2 -> x3, waiting for transfers between devices: 54.6 us -> 77.3 us  [halve_sum(): lax.ppermute(send, axis, [(i, i ^ step) for i in range(size)])]
    all_to_all x1, waiting for transfers between devices: 9.43 us -> 3.38 us  [shards(): lax.all_to_all(by_dest, ('xh', 'zh'), split_axis=0, concat_axis=0, tiled=...]
    all_to_all x1, starting transfers between devices: 10 us -> 6.71 us  [shards(): lax.all_to_all(spread, DEV, split_axis=0, concat_axis=2, tiled=True)[0]]
    unnamed x15 -> x17, local copies, waits for them, and re-layouts: 10 us -> 9.98 us
  transfers between devices with their start and end apart: 8 -> 9, of which waited for: 5 -> 6; matrix products, arithmetic and copies ran while one was open for 14% -> 12% of each run, Pallas kernels for 0% -> 0%
where the time goes in v13:
time: 303 us; the launch traced here: 302 us
  waiting for transfers between devices  173 us (57%)
  Pallas kernels  40.8 us (13%)
  starting transfers between devices  33.3 us (11%)
  local copies, waits for them, and re-layouts  32.8 us (11%)
  other arithmetic  15.9 us (5%)
  matrix products  5.94 us (2%)
    ppermute x2, waiting for transfers between devices, double_gather(): other = lax.ppermute(value, axis, [(i, i ^ step) for i in range(size)])  84.8 us
    ppermute x3, waiting for transfers between devices, halve_sum(): lax.ppermute(send, axis, [(i, i ^ step) for i in range(size)])  77.3 us
    pallas_call x1, Pallas kernels, attention(): pl.pallas_call(kern, grid=(2, n_doc + n_self), in_specs=[pl.BlockSpec((T,...  40.8 us
    all_to_all x1, starting transfers between devices, shards(): lax.all_to_all(sq_rows, DEV, split_axis=0, concat_axis=0, tiled=True)  11.3 us
    unnamed x17, local copies, waits for them, and re-layouts  9.98 us
    all_to_all x1, waiting for transfers between devices, shards(): lax.all_to_all(sq_rows, DEV, split_axis=0, concat_axis=0, tiled=True)  7.85 us
    all_to_all x1, starting transfers between devices, shards(): lax.all_to_all(spread, DEV, split_axis=0, concat_axis=2, tiled=True)[0]  6.71 us
  transfers between devices with their start and end apart: 9, of which 6 were waited for; matrix products, arithmetic and copies ran while one was open for 12% of the time, Pallas kernels for 0%

profile of v13, /device:TPU:16, one launch (start us, length us, event | category | flops | bytes accessed | tf_op | source)
XLA Modules:
  0.0 302.4 jit_solution(4223211562230546268)
XLA Ops:
  0.0 1.2 fusion.3
  1.9 11.3 %all-to-all-start = ((f32[32,1,512]{2,1,0:T(1,128)}), f32[32,1,512]{2,1,0:T(1,128)S(1)}, u32[]{:S(2)}, u32[]{:S(2)}) async-start(f32[32,1,512]{2,1,0:T(1,128)} %broadcast_in_dim.94), calls=%async_computation | async-start | bytes 131072 | tf_op jit(solution)/shard_map/all_to_all | solution.py:189
  13.3 1.5 copy.68
  15.4 7.8 %all-to-all-done = f32[32,1,512]{2,1,0:T(1,128)S(1)} async-done(((f32[32,1,512]{2,1,0:T(1,128)}), f32[32,1,512]{2,1,0:T(1,128)S(1)}, u32[]{:S(2)}, u32[]{:S(2)}) %all-to-all-start) | async-done | bytes 65568 | tf_op jit(solution)/shard_map/all_to_all | solution.py:189
  23.4 1.7 fusion.6
  25.1 1.9 copy-done.2
  27.0 1.5 constant_dynamic-slice_fusion.2
  29.2 1.3 gather_fusion
  31.7 2.0 gather_fusion.1
  33.7 41.1 %collective-permute-done = f32[512,2,2,1,2,128]{5,0,4,3,2,1:T(8,128)} collective-permute-done((f32[512,2,2,1,2,128]{5,0,4,3,2,1:T(8,128)}, f32[512,2,2,1,2,128]{5,0,4,3,2,1:T(8,128)}, u32[]{:S(2)}, u32[]{:S(2)}) %collective-permute-start) | collective-permute-done | bytes 2097184 | tf_op jit(solution)/shard_map/ppermute | solution.py:133
  74.8 2.4 dynamic-slice_add_fusion
  77.2 1.3 copy-done.3
  78.6 1.2 collective-permute-start.1
  79.8 1.7 select_select_fusion
  81.5 4.8 %all-to-all-start.2 = ((bf16[8,4,16,2048]{3,2,1,0:T(8,128)(2,1)}), bf16[8,4,16,2048]{3,2,1,0:T(8,128)(2,1)}, u32[]{:S(2)}, u32[]{:S(2)}) async-start(bf16[8,4,16,2048]{3,2,1,0:T(8,128)(2,1)} %select_select_fusion), calls=%async_computation.2 | async-start | bytes 4194304 | tf_op jit(solution)/shard_map/all_to_all | solution.py:181
  86.3 15.0 %collective-permute-done.1 = f32[256,2,2,1,2,128]{5,0,4,2,1,3:T(8,128)} collective-permute-done((f32[256,2,2,1,2,128]{5,0,4,2,1,3:T(8,128)S(1)}, f32[256,2,2,1,2,128]{5,0,4,2,1,3:T(8,128)}, u32[]{:S(2)}, u32[]{:S(2)}) %collective-permute-start.1) | collective-permute-done | bytes 1048608 | tf_op jit(solution)/shard_map/ppermute | solution.py:133
  101.3 1.7 bitcast_add_fusion
  103.1 1.4 collective-permute-start.2
  104.5 21.2 %collective-permute-done.2 = f32[128,2,2,1,2,128]{5,0,4,3,2,1:T(8,128)S(1)} collective-permute-done((f32[128,2,2,1,2,128]{5,0,4,3,2,1:T(8,128)S(1)}, f32[128,2,2,1,2,128]{5,0,4,3,2,1:T(8,128)S(1)}, u32[]{:S(2)}, u32[]{:S(2)}) %collective-permute-start.2) | collective-permute-done | bytes 524320 | tf_op jit(solution)/shard_map/ppermute | solution.py:133
  126.6 4.1 %all-to-all-start.1 = ((f32[4,128,2,128]{3,1,2,0:T(8,128)}), f32[4,128,2,128]{3,1,2,0:T(8,128)}, u32[]{:S(2)}, u32[]{:S(2)}) async-start(f32[4,128,2,128]{3,1,2,0:T(8,128)} %copy.56), calls=%async_computation.1 | async-start | bytes 1048576 | tf_op jit(solution)/shard_map/all_to_all | solution.py:198
  130.8 2.2 gather_fusion.2
  133.5 3.4 %gather_fusion.3 = bf16[32,16,16,2,128]{4,2,3,1,0:T(8,128)(2,1)} fusion(bf16[16,16,2,8,128]{4,1,3,2,0:T(8,128)(2,1)S(1)} %copy_select_fusion, s32[1024]{0:T(1024)S(1)} %pad_clamp_fusion), kind=kCustom, calls=%fused_computation.3 | custom fusion | bytes 8388736 | tf_op jit(solution)/shard_map/jit(_take)/gather | solution.py:34
  136.8 5.6 %copy_bitcast_fusion = bf16[32,16,16,256]{3,2,1,0:T(8,128)(2,1)} fusion(bf16[32,16,16,2,128]{4,2,3,1,0:T(8,128)(2,1)} %gather_fusion.3, pred[32]{0:T(512)(128)(4,1)S(1)} %compare_and_fusion.2), kind=kLoop, calls=%fused_computation.4 | loop fusion | flops 2097152 | bytes 8388640 | tf_op jit(solution)/shard_map/reshape | solution.py:36
  142.4 3.4 %all-to-all-done.1 = f32[4,128,2,128]{3,1,2,0:T(8,128)} async-done(((f32[4,128,2,128]{3,1,2,0:T(8,128)}), f32[4,128,2,128]{3,1,2,0:T(8,128)}, u32[]{:S(2)}, u32[]{:S(2)}) %all-to-all-start.1) | async-done | bytes 524320 | tf_op jit(solution)/shard_map/all_to_all | solution.py:198
  145.8 6.7 %all-to-all-start.3 = ((bf16[32,16,16,256]{3,2,1,0:T(8,128)(2,1)}), bf16[32,16,16,256]{3,2,1,0:T(8,128)(2,1)}, u32[]{:S(2)}, u32[]{:S(2)}) async-start(bf16[32,16,16,256]{3,2,1,0:T(8,128)(2,1)} %copy_bitcast_fusion), calls=%async_computation.3 | async-start | bytes 8388608 | tf_op jit(solution)/shard_map/all_to_all | solution.py:184
  153.7 2.7 collective-permute-start.3
  156.4 5.6 %copy.74 = bf16[128,8,16,128]{3,2,1,0:T(8,128)(2,1)} copy(bf16[128,8,16,128]{3,1,2,0:T(8,128)(2,1)} %bitcast.76) | data formatting | bytes 8388608
  162.0 84.8 %collective-permute-done.3 = bf16[128,256]{0,1:T(8,128)(2,1)S(1)} collective-permute-done((bf16[128,256]{0,1:T(8,128)(2,1)S(1)}, bf16[128,256]{0,1:T(8,128)(2,1)S(1)}, u32[]{:S(2)}, u32[]{:S(2)}) %collective-permute-start.3) | collective-permute-done | bytes 65568 | tf_op jit(solution)/shard_map/ppermute | solution.py:144
  247.2 5.9 %dynamic-slice_reduce_fusion = bf16[1024,2,128]{2,1,0:T(2,128)(2,1)S(1)} fusion(bf16[1024,2,8,128]{3,2,1,0:T(8,128)(2,1)} %bitcast.71, s32[]{:T(128)S(6)} %select_n.247), kind=kLoop, calls=%fused_computation.11 | loop fusion | bytes 1048580 | tf_op jit(solution)/shard_map/jit(dynamic_index_in_dim)/dynamic_slice | solution.py:28
  254.7 2.6 copy.65
  257.4 4.2 %convert_select_fusion = bf16[16,512,256]{2,1,0:T(8,128)(2,1)} fusion(bf16[16,512,256]{2,1,0:T(8,128)(2,1)S(1)} %bitcast.67, pred[16,512]{1,0:T(8,128)(4,1)S(1)} %fusion, bf16[16,32,256]{2,1,0:T(8,128)(2,1)S(1)} %bitcast.82, s32[16,32]{1,0:T(8,128)S(1)} %bitcast.88), kind=kOutput, calls=%fused_computation.6 | convolution fusion | flops 138674176 | bytes 8660992 | tf_op jit(solution)/shard_map/kib,kic->kbc/dot_general | solution.py:205
  261.6 40.8 %shard_map.91 = bf16[1024,256]{1,0:T(8,128)(2,1)} custom-call(bf16[1024,256]{1,0:T(8,128)(2,1)} %bitcast.84, bf16[8192,256]{1,0:T(8,128)(2,1)} %bitcast.65, bf16[8192,256]{1,0:T(8,128)(2,1)} %bitcast.66, bf16[1024,256]{1,0:T(8,128)(2,1)} %bitcast.72, bf16[1024,256]{1,0:T(8,128)(2,1)} %bitcast.73), custom_call_target="tpu_custom_call" | custom-call | tf_op jit(solution)/shard_map/pallas_call | solution.py:98
  (56 shorter events, 7.9 us)
Async XLA Ops:
  0.0 31.6 %copy-start = (bf16[32,16,2048]{2,1,0:T(8,128)(2,1)S(1)}, bf16[32,16,2048]{2,1,0:T(8,128)(2,1)}, u32[]{:S(2)}) copy-start(bf16[32,16,2048]{2,1,0:T(8,128)(2,1)} %param.10) | copy-start | bytes 6291460
  1.9 21.3 %all-to-all-start = ((f32[32,1,512]{2,1,0:T(1,128)}), f32[32,1,512]{2,1,0:T(1,128)S(1)}, u32[]{:S(2)}, u32[]{:S(2)}) async-start(f32[32,1,512]{2,1,0:T(1,128)} %broadcast_in_dim.94), calls=%async_computation | async-start | bytes 131072 | tf_op jit(solution)/shard_map/all_to_all | solution.py:189
  23.3 5.8 %copy-start.5 = (s32[8,16]{1,0:T(8,128)S(1)}, s32[8,16]{1,0:T(8,128)}, u32[]{:S(2)}) copy-start(s32[8,16]{1,0:T(8,128)} %param.15) | copy-start | bytes 1540
  23.3 5.9 %copy-start.1 = (s32[256]{0:T(256)S(1)}, s32[256]{0:T(256)}, u32[]{:S(2)}) copy-start(s32[256]{0:T(256)} %param.16) | copy-start | bytes 3076
  25.1 1.9 copy-start.2
  28.5 46.3 %collective-permute-start = (f32[512,2,2,1,2,128]{5,0,4,3,2,1:T(8,128)}, f32[512,2,2,1,2,128]{5,0,4,3,2,1:T(8,128)}, u32[]{:S(2)}, u32[]{:S(2)}) collective-permute-start(f32[512,2,2,1,2,128]{5,0,4,3,2,1:T(8,128)} %constant_dynamic-slice_fusion.2), channel_id=1, source_target_pairs={{0,8},{8,0},{1,9},{9,1},{2,10},{10,2},{3,11},{11,3},{4,12},{12,4},... | collective-permute-start | bytes 6291464 | tf_op jit(solution)/shard_map/ppermute | solution.py:133
  33.7 46.2 %copy-start.4 = (bf16[32,16,2048]{2,1,0:T(8,128)(2,1)S(1)}, bf16[32,16,2048]{2,1,0:T(8,128)(2,1)}, u32[]{:S(2)}) copy-start(bf16[32,16,2048]{2,1,0:T(8,128)(2,1)} %gather_fusion.1) | copy-start | bytes 6291460
  77.2 1.3 copy-start.3
  78.6 22.7 %collective-permute-start.1 = (f32[256,2,2,1,2,128]{5,0,4,2,1,3:T(8,128)S(1)}, f32[256,2,2,1,2,128]{5,0,4,2,1,3:T(8,128)}, u32[]{:S(2)}, u32[]{:S(2)}) collective-permute-start(f32[256,2,2,1,2,128]{5,0,4,2,1,3:T(8,128)S(1)} %dynamic-slice_bitcast_fusion), channel_id=1, source_target_pairs={{0,1},{1,0},{2,3},{3,2},{4,5},{5,4},{6,7},{7,6},{8,9},{9,8},{10,11... | collective-permute-start | bytes 3145736 | tf_op jit(solution)/shard_map/ppermute | solution.py:133
  81.5 45.1 %all-to-all-start.2 = ((bf16[8,4,16,2048]{3,2,1,0:T(8,128)(2,1)}), bf16[8,4,16,2048]{3,2,1,0:T(8,128)(2,1)}, u32[]{:S(2)}, u32[]{:S(2)}) async-start(bf16[8,4,16,2048]{3,2,1,0:T(8,128)(2,1)} %select_select_fusion), calls=%async_computation.2 | async-start | bytes 4194304 | tf_op jit(solution)/shard_map/all_to_all | solution.py:181
  103.1 22.6 %collective-permute-start.2 = (f32[128,2,2,1,2,128]{5,0,4,3,2,1:T(8,128)S(1)}, f32[128,2,2,1,2,128]{5,0,4,3,2,1:T(8,128)S(1)}, u32[]{:S(2)}, u32[]{:S(2)}) collective-permute-start(f32[128,2,2,1,2,128]{5,0,4,3,2,1:T(8,128)S(1)} %dynamic-slice_bitcast_fusion.1), channel_id=1, source_target_pairs={{0,2},{2,0},{1,3},{3,1},{4,6},{6,4},{5,7},{7,5},{8,10},{10,8},{9,1... | collective-permute-start | bytes 1572872 | tf_op jit(solution)/shard_map/ppermute | solution.py:133
  126.6 19.2 %all-to-all-start.1 = ((f32[4,128,2,128]{3,1,2,0:T(8,128)}), f32[4,128,2,128]{3,1,2,0:T(8,128)}, u32[]{:S(2)}, u32[]{:S(2)}) async-start(f32[4,128,2,128]{3,1,2,0:T(8,128)} %copy.56), calls=%async_computation.1 | async-start | bytes 1048576 | tf_op jit(solution)/shard_map/all_to_all | solution.py:198
  145.8 108.9 %all-to-all-start.3 = ((bf16[32,16,16,256]{3,2,1,0:T(8,128)(2,1)}), bf16[32,16,16,256]{3,2,1,0:T(8,128)(2,1)}, u32[]{:S(2)}, u32[]{:S(2)}) async-start(bf16[32,16,16,256]{3,2,1,0:T(8,128)(2,1)} %copy_bitcast_fusion), calls=%async_computation.3 | async-start | bytes 8388608 | tf_op jit(solution)/shard_map/all_to_all | solution.py:184
  153.7 93.1 %collective-permute-start.3 = (bf16[128,256]{0,1:T(8,128)(2,1)S(1)}, bf16[128,256]{0,1:T(8,128)(2,1)S(1)}, u32[]{:S(2)}, u32[]{:S(2)}) collective-permute-start(bf16[128,256]{0,1:T(8,128)(2,1)S(1)} %bitcast.85), channel_id=1, source_target_pairs={{0,2},{1,3},{2,0},{3,1},{4,6},{5,7},{6,4},{7,5},{8,10},{9,11},{10,... | collective-permute-start | bytes 196616 | tf_op jit(solution)/shard_map/ppermute | solution.py:144
  156.4 97.7 %copy-start.6 = (s32[1,16,32]{2,1,0:T(8,128)S(1)}, s32[1,16,32]{2,1,0:T(8,128)}, u32[]{:S(2)}) copy-start(s32[1,16,32]{2,1,0:T(8,128)} %param.17) | copy-start | bytes 6148
  246.8 7.6 %collective-permute-start.4 = (bf16[256,256]{0,1:T(8,128)(2,1)S(1)}, bf16[256,256]{0,1:T(8,128)(2,1)S(1)}, u32[]{:S(2)}, u32[]{:S(2)}) collective-permute-start(bf16[256,256]{0,1:T(8,128)(2,1)S(1)} %maximum_select_fusion.1), channel_id=1, source_target_pairs={{0,1},{1,0},{2,3},{3,2},{4,5},{5,4},{6,7},{7,6},{8,9},{9,8},{10,11... | collective-permute-start | bytes 393224 | tf_op jit(solution)/shard_map/ppermute | solution.py:144
